TPU v7x, 32 devices: a whole 2x2x4 slice. The times are simulated.
32 devices in a mesh: groups: 2 (over y), expert: 4 (over z), dp: 4 (over x, core).
Axes of the slice: x: 2, y: 2, z: 4, core: 2. Of those that a mesh axis runs over, the one named last changes fastest.
Arguments:
- out_grad: bfloat16 [4096, 2048], P(('groups', 'expert', 'dp')), parts along dimension 0, may hold values from -0.5 to 0.5
- gate_weights: bfloat16 [4096, 8], P(('groups', 'expert', 'dp')), parts along dimension 0, may hold values from 0.049804688 to 0.5
- expert_ids: int32 [4096, 8], P(('groups', 'expert', 'dp')), parts along dimension 0, may hold values from 0 to 31, all different within a row; in each aligned block of 128 rows (0 to 127, 128 to 255, ...) at most 36 rows name the same one
- hidden: bfloat16 [32, 8, 4, 36, 768], P('expert', ('groups', 'dp')), parts along dimension 1, may hold values from -6 to 6
- down_weight: bfloat16 [32, 768, 2048], P('expert', None, 'dp'), may hold values from -0.21875 to 0.21875
Outputs:
- weight_grad: float32 [64, 768, 2048], P(('groups', 'expert'), None, 'dp'), parts along dimension 0
- gate_grad: float32 [4096, 8], P(('groups', 'expert', 'dp')), parts along dimension 0
There are 2 independent parts, one for each index of `groups`. A program takes and returns all parts, laid end to end along the dimension named above; an argument that names none is the same for every part. Nothing has to cross between parts.
Inputs may be any that keep to these rules, and one draw needn't show every extreme that they name: `expert_ids`: each token names 8 different experts; within each block of 128 tokens (one device's tokens) no expert is named by more than 36 tokens, a bound that some block reaches.
All inputs are finite; a program needn't handle non-finite values.
Results may differ from a plain program's by a relative error of at most 0.0095.
Values may be sent and summed in bfloat16 or wider, within the bound.
No kernel may reach another device: no remote copies, remote signals or barrier semaphores. Data moves between devices by JAX's collectives and lax.ppermute only.
A program may use at most 128 MiB of HBM per device.

v0:
```python
import jax
import jax.numpy as jnp
from jax import lax
from jax.experimental import pallas as pl
from jax.sharding import PartitionSpec as P


def expert_body(h_ref, s_ref, g_ref, w_ref, wg_ref, slot_ref):
    chunk = pl.program_id(1)
    blocks, slots, hidden_width = h_ref.shape[1:]
    col_width = s_ref.shape[3]
    rows = blocks * slots
    h = h_ref[0].reshape(rows, hidden_width)
    part = lax.dot_general(
        h, s_ref[:, 0].reshape(rows, col_width), (((0,), (0,)), ((), ())),
        preferred_element_type=jnp.float32,
    )

    @pl.when(chunk == 0)
    def _():
        wg_ref[0] = part

    @pl.when(chunk != 0)
    def _():
        wg_ref[0] = wg_ref[0] + part

    out = jnp.dot(h, w_ref[0], preferred_element_type=jnp.float32)
    g = g_ref[:, 0].reshape(rows, col_width).astype(jnp.float32)
    slot_ref[0] = jnp.sum(g * out, axis=1, keepdims=True)


def expert_kernel(hidden_rows, scaled_rows, grad_rows, weight):
    local_count, block_count, slots, hidden_width = hidden_rows.shape
    col_width = scaled_rows.shape[3]
    chunk = block_count
    for size in (16, 8, 4, 2, 1):
        if block_count % size == 0:
            chunk = size
            break
    steps = block_count // chunk
    rows = chunk * slots
    return pl.pallas_call(
        expert_body,
        grid=(local_count, steps),
        in_specs=[
            pl.BlockSpec((1, chunk, slots, hidden_width), lambda l, r: (l, r, 0, 0)),
            pl.BlockSpec((chunk, 1, slots, col_width), lambda l, r: (r, l, 0, 0)),
            pl.BlockSpec((chunk, 1, slots, col_width), lambda l, r: (r, l, 0, 0)),
            pl.BlockSpec((1, hidden_width, col_width), lambda l, r: (l, 0, 0)),
        ],
        out_specs=[
            pl.BlockSpec((1, hidden_width, col_width), lambda l, r: (l, 0, 0)),
            pl.BlockSpec((1, rows, 1), lambda l, r: (l, r, 0)),
        ],
        out_shape=[
            jax.ShapeDtypeStruct((local_count, hidden_width, col_width), jnp.float32),
            jax.ShapeDtypeStruct((local_count, block_count * slots, 1), jnp.float32),
        ],
    )(hidden_rows, scaled_rows, grad_rows, weight)


def per_device(out_grad, gate_weights, expert_ids, hidden, down_weight):
    tok_rows, top_count = expert_ids.shape
    row_width = out_grad.shape[1]
    local_count = hidden.shape[0]
    capacity = hidden.shape[3]
    hidden_width = hidden.shape[4]
    peer_count = lax.axis_size("expert")
    shards = lax.axis_size("dp")
    expert_count = local_count * peer_count
    col_width = row_width // shards
    block_count = peer_count * shards
    f32 = jnp.float32
    bf16 = jnp.bfloat16
    my_dp = lax.axis_index("dp")

    meta = jnp.concatenate([expert_ids.astype(bf16), gate_weights], axis=1).reshape(-1)
    meta_len = meta.shape[0]
    meta_rows = -(-meta_len // col_width)
    meta = jnp.pad(meta, (0, meta_rows * col_width - meta_len)).reshape(meta_rows, 1, col_width)
    cols = out_grad.reshape(tok_rows, shards, col_width)
    cols = jnp.concatenate([cols, jnp.broadcast_to(meta, (meta_rows, shards, col_width))], axis=0)
    cols = lax.all_to_all(cols, "dp", split_axis=1, concat_axis=0, tiled=True)
    cols = cols.reshape(shards, tok_rows + meta_rows, col_width)
    piece_xor = jnp.array([0, 2, 1, 3], jnp.int32)
    cols = jnp.take(cols, piece_xor ^ my_dp, axis=0)

    hidden_sent, cols = lax.optimization_barrier((hidden, cols))
    near = lax.ppermute(hidden_sent, "dp", [(j, j ^ 1) for j in range(shards)])
    far = lax.ppermute(hidden_sent, "dp", [(j, j ^ 2) for j in range(shards)])
    near_far = lax.ppermute(far, "dp", [(j, j ^ 1) for j in range(shards)])
    got = lax.all_gather(cols, "expert", axis=0, tiled=False)
    got = got.reshape(block_count, tok_rows + meta_rows, col_width)
    grad_all = got[:, :tok_rows]
    meta_all = got[:, tok_rows:].reshape(block_count, meta_rows * col_width)[:, :meta_len]
    meta_all = meta_all.reshape(block_count, tok_rows, 2 * top_count)
    ids_all = meta_all[:, :, :top_count].astype(jnp.int32)
    gate_all = meta_all[:, :, top_count:]

    my_experts = lax.axis_index("expert") * local_count + jnp.arange(local_count, dtype=jnp.int32)
    hit = ids_all[:, :, :, None] == my_experts[None, None, None, :]
    chose = jnp.any(hit, axis=2)
    gate_hit = jnp.sum(jnp.where(hit, gate_all.astype(f32)[:, :, :, None], 0.0), axis=2)
    before = (jnp.arange(tok_rows)[:, None] < jnp.arange(tok_rows)[None, :]).astype(bf16)
    rank = jnp.einsum(
        "bul,ut->btl", chose.astype(bf16), before, preferred_element_type=f32
    ).astype(jnp.int32)
    padded = -(-capacity // 8) * 8
    slot_ids = jnp.arange(padded, dtype=jnp.int32)
    chose_t = chose.transpose(0, 2, 1)
    rank_t = rank.transpose(0, 2, 1)
    gate_t = gate_hit.transpose(0, 2, 1)
    select = chose_t[:, :, None, :] & (rank_t[:, :, None, :] == slot_ids[None, None, :, None])
    select_gate = jnp.where(select, gate_t[:, :, None, :], 0.0).astype(bf16)
    grad_rows = jnp.einsum(
        "blct,btd->blcd", select.astype(bf16), grad_all, preferred_element_type=f32
    ).astype(bf16)
    scaled = jnp.einsum(
        "blct,btd->blcd", select_gate, grad_all, preferred_element_type=f32
    ).astype(bf16)

    hidden_all = jnp.stack([p[:, 0] for p in (hidden, far, near, near_far)], axis=2)
    hidden_all = jnp.pad(hidden_all, ((0, 0), (0, 0), (0, 0), (0, padded - capacity), (0, 0)))
    hidden_all = hidden_all.reshape(local_count, block_count, padded, hidden_width)
    weight_grad, slot_part = expert_kernel(hidden_all, scaled, grad_rows, down_weight)
    slot_part = slot_part.reshape(local_count, block_count, padded)[:, :, :capacity]
    slot_part = slot_part.transpose(1, 0, 2).reshape(peer_count, shards, local_count, capacity)
    piece_of = jnp.array([0, 2, 1, 3], jnp.int32)[jnp.arange(shards, dtype=jnp.int32) ^ my_dp]
    slot_part = jnp.take(slot_part, piece_of, axis=1)
    send_back = slot_part.reshape(block_count, local_count, capacity)
    returned = lax.all_to_all(
        send_back, ("expert", "dp"), split_axis=0, concat_axis=0, tiled=True
    )
    returned = returned.reshape(peer_count, shards, local_count, capacity)
    slot_grad = jnp.sum(returned, axis=1).reshape(expert_count, capacity)

    own_hit = expert_ids[:, :, None] == jnp.arange(expert_count, dtype=jnp.int32)[None, None, :]
    own_chose = jnp.any(own_hit, axis=1)
    own_rank = jnp.einsum(
        "ue,ut->te", own_chose.astype(bf16), before, preferred_element_type=f32
    ).astype(jnp.int32)
    own_slot = jnp.sum(jnp.where(own_hit, own_rank[:, None, :], 0), axis=2)
    by_slot = jnp.sum(jnp.where(own_hit[:, :, :, None], slot_grad[None, None], 0.0), axis=2)
    gate_grad = jnp.sum(
        jnp.where(own_slot[:, :, None] == slot_ids[None, None, :capacity], by_slot, 0.0), axis=2
    )
    return (weight_grad, gate_grad)


def solution(mesh):
    return jax.shard_map(
        per_device,
        mesh=mesh,
        in_specs=(
            P(("groups", "expert", "dp"), None),
            P(("groups", "expert", "dp"), None),
            P(("groups", "expert", "dp"), None),
            P("expert", ("groups", "dp"), None, None, None),
            P("expert", None, "dp"),
        ),
        out_specs=(P(("groups", "expert"), None, "dp"), P(("groups", "expert", "dp"), None)),
        check_vma=False,
    )
```

profile of v0, /device:TPU:0, one launch (start us, length us, event | category | flops | bytes accessed | tf_op | source)
XLA Modules:
  0.0 146.9 jit_solution(1054775163686925633)
XLA Ops:
  7.2 0.0 copy-start
  7.2 1.3 copy.58
  8.5 0.2 copy.60
  8.7 0.7 convert_element_type.31
  9.4 0.7 pad_maximum_fusion.2
  10.1 0.1 copy.59
  10.2 0.1 broadcast_in_dim.112
  10.4 0.0 copy-start.2
  10.4 0.9 pad_maximum_fusion.1
  11.2 4.2 %all-to-all-start = ((bf16[132,4,512]{2,0,1:T(8,128)(2,1)}), bf16[132,4,512]{2,0,1:T(8,128)(2,1)S(1)}, u32[]{:S(2)}, u32[]{:S(2)}) async-start(bf16[132,4,512]{2,0,1:T(8,128)(2,1)} %pad_maximum_fusion.1), calls=%async_computation | async-start | bytes 1114112 | tf_op jit(solution)/shard_map/all_to_all | solution.py:83
  15.5 9.2 %all-to-all-done = bf16[132,4,512]{2,0,1:T(8,128)(2,1)S(1)} async-done(((bf16[132,4,512]{2,0,1:T(8,128)(2,1)}), bf16[132,4,512]{2,0,1:T(8,128)(2,1)S(1)}, u32[]{:S(2)}, u32[]{:S(2)}) %all-to-all-start) | async-done | bytes 540704 | tf_op jit(solution)/shard_map/all_to_all | solution.py:83
  24.6 0.6 gather_fusion
  25.2 0.9 broadcast_select_fusion
  26.2 0.0 all-gather.3.cloned.1.call-update
  26.2 0.4 collective-permute-start
  26.6 0.6 gather_fusion.1
  27.3 0.1 broadcast_in_dim.124
  27.4 0.1 collective-permute-start.1
  27.5 39.0 %collective-permute-done = bf16[8,1,4,36,768]{4,2,3,0,1:T(4,128)(2,1)} collective-permute-done((bf16[8,1,4,36,768]{4,2,3,0,1:T(4,128)(2,1)}, bf16[8,1,4,36,768]{4,2,3,0,1:T(4,128)(2,1)}, u32[]{:S(2)}, u32[]{:S(2)}) %collective-permute-start) | collective-permute-done | bytes 1769504 | tf_op jit(solution)/shard_map/ppermute | solution.py:90
  66.5 0.1 convolution_convert_fusion.3
  66.7 9.0 %all-gather.3.cloned.1.call-done = bf16[16,132,512]{2,1,0:T(8,128)(2,1)} async-done(((bf16[4,132,512]{2,1,0:T(8,128)(2,1)}), bf16[16,132,512]{2,1,0:T(8,128)(2,1)}) %all-gather.3.cloned.1.call-update) | async-done | bytes 2162704 | tf_op jit(solution)/shard_map/all_gather | solution.py:92
  75.7 1.1 slice.30
  76.7 0.4 reshape_reshape.3
  77.1 1.0 fusion.15
  78.1 1.2 copy.71
  79.3 0.2 copy.72
  79.5 0.1 compare_reduce_fusion
  79.7 0.1 fusion.8
  79.8 0.1 convolution_convert_fusion.2
  80.0 3.8 %convolution_convert_fusion.1.g_ref = bf16[16,8,40,512]{3,2,1,0:T(8,128)(2,1)} fusion(bf16[16,132,512]{2,1,0:T(8,128)(2,1)S(1)} %copy-done.1, s32[16,8,128]{2,1,0:T(8,128)S(1)} %convolution_convert_fusion.2, pred[16,8,128]{2,1,0:T(8,128)(4,1)S(1)} %bitcast.44), kind=kOutput, calls=%fused_computation.6 | convolution fusion | flops 675020800 | bytes 7421952 | tf_op jit(solution)/shard_map/blct,btd->blcd/dot_general | solution.py:115
  83.8 3.8 %convolution_convert_fusion.s_ref = bf16[16,8,40,512]{3,2,1,0:T(8,128)(2,1)} fusion(bf16[16,132,512]{2,1,0:T(8,128)(2,1)S(1)} %copy-done.1, bf16[16,8,128]{2,1,0:T(8,128)(2,1)S(1)} %bitcast.48, s32[16,8,128]{2,1,0:T(8,128)S(1)} %convolution_convert_fusion.2, pred[16,8,128]{2,1,0:T(8,128)(4,1)S(1)} %bitcast.45), kind=kOutput, calls=%fused_computation.5 | convolution fusion | flops 675676160 | bytes 7454720 | tf_op jit(solution)/shard_map/blct,btd->blcd/dot_general | solution.py:118
  87.6 8.8 %pad_maximum_fusion = bf16[8,4,4,36,768]{4,1,3,0,2:T(4,128)(2,1)} fusion(bf16[8,4,1,36,768]{4,1,3,0,2:T(4,128)(2,1)} %bitcast.8, bf16[8,4,1,36,768]{4,1,3,0,2:T(4,128)(2,1)} %bitcast.7, bf16[8,4,1,36,768]{4,1,3,0,2:T(4,128)(2,1)} %bitcast.6, bf16[8,4,1,36,768]{4,1,3,0,2:T(4,128)(2,1)} %bitcast), kind=kLoop, calls=%fused_computation.3 | loop fusion | flops 10616832 | bytes 14155776 | tf_op jit(solution)/shard_map/stack | solution.py:122
  96.4 4.4 %copy.73 = bf16[8,4,4,36,768]{4,3,2,1,0:T(8,128)(2,1)S(1)} copy(bf16[8,4,4,36,768]{4,1,3,0,2:T(4,128)(2,1)} %pad_maximum_fusion) | data formatting | bytes 14155776
  100.9 4.0 %pad.4.clone = bf16[8,4,4,40,768]{4,3,2,1,0:T(8,128)(2,1)} pad(bf16[8,4,4,36,768]{4,3,2,1,0:T(8,128)(2,1)S(1)} %copy.73, bf16[]{:T(256)} %constant.43.clone.1), padding=0_0x0_0x0_0x0_4x0_0 | pad | bytes 14942210 | tf_op jit(solution)/shard_map/jit(_pad)/pad | solution.py:123
  104.9 18.1 %shard_map.86 = (f32[8,768,512]{2,1,0:T(8,128)}, f32[8,640,1]{2,1,0:T(8,128)}) custom-call(bf16[8,16,40,768]{3,2,1,0:T(8,128)(2,1)} %bitcast.41, bf16[16,8,40,512]{3,2,1,0:T(8,128)(2,1)} %convolution_convert_fusion.s_ref, bf16[16,8,40,512]{3,2,1,0:T(8,128)(2,1)} %convolution_convert_fusion.1.g_ref, bf16[8,768,512]{2,1,0:T(8,128)(2,1)} %w_ref.1), custom_call_target="tpu_custom_call" | custom-call | tf_op jit(solution)/shard_map/pallas_call | solution.py:42
  122.9 2.5 %reduce = f32[8,640]{1,0:T(8,128)S(1)} reduce(f32[8,640,1]{2,1,0:T(8,128)} %get-tuple-element.9, f32[]{:T(128)} %constant.53), dimensions={2}, to_apply=%get-tuple-element.9.reduce_sub_computation | reduce | bytes 40964 | tf_op jit(solution)/shard_map/pallas_call | solution.py:42
  125.4 0.1 reshape.93
  125.6 0.6 gather_fusion.2
  126.2 0.1 bitcast_select_fusion
  126.3 0.7 reshape.126
  127.0 3.5 %all-to-all-start.1 = ((f32[16,1,288]{2,1,0:T(1,128)}), f32[16,1,288]{2,1,0:T(1,128)S(1)}, u32[]{:S(2)}, u32[]{:S(2)}) async-start(f32[16,1,288]{2,1,0:T(1,128)} %reshape.126), calls=%async_computation.1 | async-start | bytes 49152 | tf_op jit(solution)/shard_map/all_to_all | solution.py:131
  130.5 6.5 %all-to-all-done.1 = f32[16,1,288]{2,1,0:T(1,128)S(1)} async-done(((f32[16,1,288]{2,1,0:T(1,128)}), f32[16,1,288]{2,1,0:T(1,128)S(1)}, u32[]{:S(2)}, u32[]{:S(2)}) %all-to-all-start.1) | async-done | bytes 18464 | tf_op jit(solution)/shard_map/all_to_all | solution.py:131
  137.1 0.5 broadcast.102
  137.6 0.7 reduce.1
  138.3 0.1 reshape.127
  138.4 0.1 copy.67
  138.5 0.8 select_reduce_fusion
  139.3 0.7 select_reduce_fusion.1
  (27 shorter events, 0.2 us)
Async XLA Ops:
  7.2 8.3 %copy-start = (s32[4]{0:T(128)S(1)}, s32[4]{0:T(128)}, u32[]{:S(2)}) copy-start(s32[4]{0:T(128)} %constant.49.clone) | copy-start | bytes 52
  10.4 17.0 %copy-start.2 = (s32[128,8]{0,1:T(8,128)S(1)}, s32[128,8]{0,1:T(8,128)}, u32[]{:S(2)}) copy-start(s32[128,8]{0,1:T(8,128)} %param.9) | copy-start | bytes 12292
  11.2 13.4 %all-to-all-start = ((bf16[132,4,512]{2,0,1:T(8,128)(2,1)}), bf16[132,4,512]{2,0,1:T(8,128)(2,1)S(1)}, u32[]{:S(2)}, u32[]{:S(2)}) async-start(bf16[132,4,512]{2,0,1:T(8,128)(2,1)} %pad_maximum_fusion.1), calls=%async_computation | async-start | bytes 1114112 | tf_op jit(solution)/shard_map/all_to_all | solution.py:83
  15.4 60.2 %all-gather.3.cloned.1.call-start = ((), (), s32[]{:S(2)}) async-start(), calls=%async_computation.2 | async-start | bytes 2785280 | tf_op jit(solution)/shard_map/all_gather | solution.py:92
  26.2 40.3 %collective-permute-start = (bf16[8,1,4,36,768]{4,2,3,0,1:T(4,128)(2,1)}, bf16[8,1,4,36,768]{4,2,3,0,1:T(4,128)(2,1)}, u32[]{:S(2)}, u32[]{:S(2)}) collective-permute-start(bf16[8,1,4,36,768]{4,2,3,0,1:T(4,128)(2,1)} %bitcast.5), channel_id=1, source_target_pairs={{0,2},{1,3},{2,0},{3,1},{4,6},{5,7},{6,4},{7,5},{8,10},{9,11},{10,... | collective-permute-start | bytes 5308424 | tf_op jit(solution)/shard_map/ppermute | solution.py:90
  27.4 60.2 %collective-permute-start.1 = (bf16[8,1,4,36,768]{4,2,3,1,0:T(4,128)(2,1)}, bf16[8,1,4,36,768]{4,2,3,1,0:T(4,128)(2,1)}, u32[]{:S(2)}, u32[]{:S(2)}) collective-permute-start(bf16[8,1,4,36,768]{4,2,3,1,0:T(4,128)(2,1)} %param.10), channel_id=1, source_target_pairs={{0,1},{1,0},{2,3},{3,2},{4,5},{5,4},{6,7},{7,6},{8,9},{9,8},{10,11... | collective-permute-start | bytes 5308424 | tf_op jit(solution)/shard_map/ppermute | solution.py:89
  66.5 21.1 %collective-permute-start.2 = (bf16[8,1,4,36,768]{4,2,3,0,1:T(4,128)(2,1)}, bf16[8,1,4,36,768]{4,2,3,0,1:T(4,128)(2,1)}, u32[]{:S(2)}, u32[]{:S(2)}) collective-permute-start(bf16[8,1,4,36,768]{4,2,3,0,1:T(4,128)(2,1)} %collective-permute-done), channel_id=1, source_target_pairs={{0,1},{1,0},{2,3},{3,2},{4,5},{5,4},{6,7},{7,6},{8,9},{9,8},{10,11... | collective-permute-start | bytes 5308424 | tf_op jit(solution)/shard_map/ppermute | solution.py:91
  75.7 4.3 %copy-start.1 = (bf16[16,132,512]{2,1,0:T(8,128)(2,1)S(1)}, bf16[16,132,512]{2,1,0:T(8,128)(2,1)}, u32[]{:S(2)}) copy-start(bf16[16,132,512]{2,1,0:T(8,128)(2,1)} %all-gather.3.cloned.1.call-done) | copy-start | bytes 6488068
  127.0 10.1 %all-to-all-start.1 = ((f32[16,1,288]{2,1,0:T(1,128)}), f32[16,1,288]{2,1,0:T(1,128)S(1)}, u32[]{:S(2)}, u32[]{:S(2)}) async-start(f32[16,1,288]{2,1,0:T(1,128)} %reshape.126), calls=%async_computation.1 | async-start | bytes 49152 | tf_op jit(solution)/shard_map/all_to_all | solution.py:131
Sparse Core Ops, SparseCore 0:
  26.3 49.3 all-gather.2
where the time goes:
time: 147 us
  waiting for transfers between devices  63.7 us (43%)
  Pallas kernels  18.1 us (12%)
  local copies, waits for them, and re-layouts  17.5 us (12%)
  other arithmetic  17.2 us (12%)
  between operations  14.3 us (10%)
  starting transfers between devices  8.24 us (6%)
  matrix products  7.88 us (5%)
    ppermute x1, waiting for transfers between devices, per_device(): far = lax.ppermute(hidden_sent, 'dp', [(j, j ^ 2) for j in range(shards)])  39 us
    pallas_call x1, Pallas kernels, expert_kernel(): pl.pallas_call(expert_body, grid=(local_count, steps), in_specs=[pl.Block...  18.1 us
    all_to_all x1, waiting for transfers between devices, per_device(): cols = lax.all_to_all(cols, 'dp', split_axis=1, concat_axis=0, tiled=True)  9.17 us
    all_gather x1, waiting for transfers between devices, per_device(): got = lax.all_gather(cols, 'expert', axis=0, tiled=False)  9.01 us
    another operation x1, other arithmetic, per_device(): jnp.stack([p[:, 0] for p in (hidden, far, near, near_far)], axis=2)  8.84 us
    unnamed x12, local copies, waits for them, and re-layouts  7.97 us
    all_to_all x1, waiting for transfers between devices, per_device(): lax.all_to_all(send_back, ('expert', 'dp'), split_axis=0, concat_axis=0,...  6.53 us
    all_to_all x1, starting transfers between devices, per_device(): cols = lax.all_to_all(cols, 'dp', split_axis=1, concat_axis=0, tiled=True)  4.21 us
  transfers between devices with their start and end apart: 6, of which 4 were waited for; matrix products, arithmetic and copies ran while one was open for 9% of the time, Pallas kernels for 0%

commit v1 on v0

--- a/solution.py
+++ b/solution.py
@@ -2,15 +2,29 @@
 import jax.numpy as jnp
 from jax import lax
 from jax.experimental import pallas as pl
+from jax.experimental.pallas import tpu as pltpu
 from jax.sharding import PartitionSpec as P
 
 
-def expert_body(h_ref, s_ref, g_ref, w_ref, wg_ref, slot_ref):
+def expert_body(own_ref, far_ref, near_ref, near_far_ref, s_ref, g_ref, w_ref, wg_ref, slot_ref, h_scr):
+    expert = pl.program_id(0)
     chunk = pl.program_id(1)
-    blocks, slots, hidden_width = h_ref.shape[1:]
+    sources, capacity, hidden_width = own_ref.shape[2:]
+    blocks, padded = s_ref.shape[0], s_ref.shape[2]
     col_width = s_ref.shape[3]
-    rows = blocks * slots
-    h = h_ref[0].reshape(rows, hidden_width)
+    rows = blocks * padded
+    pieces = (own_ref, far_ref, near_ref, near_far_ref)
+
+    @pl.when((expert == 0) & (chunk == 0))
+    def _():
+        h_scr[...] = jnp.zeros(h_scr.shape, h_scr.dtype)
+
+    for src in range(sources):
+        for j, ref in enumerate(pieces):
+            row = (src * len(pieces) + j) * padded
+            h_scr[row:row + capacity, :] = ref[0, 0, src]
+
+    h = h_scr[...]
     part = lax.dot_general(
         h, s_ref[:, 0].reshape(rows, col_width), (((0,), (0,)), ((), ())),
         preferred_element_type=jnp.float32,
@@ -29,23 +43,29 @@
     slot_ref[0] = jnp.sum(g * out, axis=1, keepdims=True)
 
 
-def expert_kernel(hidden_rows, scaled_rows, grad_rows, weight):
-    local_count, block_count, slots, hidden_width = hidden_rows.shape
-    col_width = scaled_rows.shape[3]
-    chunk = block_count
-    for size in (16, 8, 4, 2, 1):
-        if block_count % size == 0:
+def expert_kernel(pieces, scaled_rows, grad_rows, weight):
+    local_count, _, source_count, capacity, hidden_width = pieces[0].shape
+    block_count, _, padded, col_width = scaled_rows.shape
+    per_source = block_count // source_count
+    chunk = source_count
+    for size in (4, 2, 1):
+        if source_count % size == 0:
             chunk = size
             break
-    steps = block_count // chunk
-    rows = chunk * slots
+    steps = source_count // chunk
+    rows = chunk * per_source * padded
+    piece_spec = pl.BlockSpec(
+        (1, 1, chunk, capacity, hidden_width), lambda l, r: (l, 0, r, 0, 0)
+    )
+    row_spec = pl.BlockSpec(
+        (chunk * per_source, 1, padded, col_width), lambda l, r: (r, l, 0, 0)
+    )
     return pl.pallas_call(
         expert_body,
         grid=(local_count, steps),
-        in_specs=[
-            pl.BlockSpec((1, chunk, slots, hidden_width), lambda l, r: (l, r, 0, 0)),
-            pl.BlockSpec((chunk, 1, slots, col_width), lambda l, r: (r, l, 0, 0)),
-            pl.BlockSpec((chunk, 1, slots, col_width), lambda l, r: (r, l, 0, 0)),
+        in_specs=[piece_spec] * len(pieces) + [
+            row_spec,
+            row_spec,
             pl.BlockSpec((1, hidden_width, col_width), lambda l, r: (l, 0, 0)),
         ],
         out_specs=[
@@ -54,9 +74,10 @@
         ],
         out_shape=[
             jax.ShapeDtypeStruct((local_count, hidden_width, col_width), jnp.float32),
-            jax.ShapeDtypeStruct((local_count, block_count * slots, 1), jnp.float32),
+            jax.ShapeDtypeStruct((local_count, block_count * padded, 1), jnp.float32),
         ],
-    )(hidden_rows, scaled_rows, grad_rows, weight)
+        scratch_shapes=[pltpu.VMEM((rows, hidden_width), jnp.bfloat16)],
+    )(*pieces, scaled_rows, grad_rows, weight)
 
 
 def per_device(out_grad, gate_weights, expert_ids, hidden, down_weight):
@@ -105,7 +126,7 @@
     rank = jnp.einsum(
         "bul,ut->btl", chose.astype(bf16), before, preferred_element_type=f32
     ).astype(jnp.int32)
-    padded = -(-capacity // 8) * 8
+    padded = -(-capacity // 16) * 16
     slot_ids = jnp.arange(padded, dtype=jnp.int32)
     chose_t = chose.transpose(0, 2, 1)
     rank_t = rank.transpose(0, 2, 1)
@@ -119,10 +140,7 @@
         "blct,btd->blcd", select_gate, grad_all, preferred_element_type=f32
     ).astype(bf16)
 
-    hidden_all = jnp.stack([p[:, 0] for p in (hidden, far, near, near_far)], axis=2)
-    hidden_all = jnp.pad(hidden_all, ((0, 0), (0, 0), (0, 0), (0, padded - capacity), (0, 0)))
-    hidden_all = hidden_all.reshape(local_count, block_count, padded, hidden_width)
-    weight_grad, slot_part = expert_kernel(hidden_all, scaled, grad_rows, down_weight)
+    weight_grad, slot_part = expert_kernel((hidden, far, near, near_far), scaled, grad_rows, down_weight)
     slot_part = slot_part.reshape(local_count, block_count, padded)[:, :, :capacity]
     slot_part = slot_part.transpose(1, 0, 2).reshape(peer_count, shards, local_count, capacity)
     piece_of = jnp.array([0, 2, 1, 3], jnp.int32)[jnp.arange(shards, dtype=jnp.int32) ^ my_dp]

time: 147 us -> 138 us (0.939)
  waiting for transfers between devices: 63.7 us -> 54.1 us
  other arithmetic: 17.2 us -> 9.26 us
  local copies, waits for them, and re-layouts: 17.5 us -> 20.8 us
  starting transfers between devices: 8.24 us -> 10.2 us
  matrix products: 7.88 us -> 9.75 us
    another operation x1 -> x0, other arithmetic: 8.84 us -> none  [per_device(): jnp.stack([p[:, 0] for p in (hidden, far, near, near_far)], axis=2)]
    all_gather x1, waiting for transfers between devices: 9.01 us -> 0.51 us  [per_device(): got = lax.all_gather(cols, 'expert', axis=0, tiled=False)]
    ppermute x0 -> x3, local copies, waits for them, and re-layouts: none -> 7.87 us  [the longest x1 3.13 us: per_device(): near_far = lax.ppermute(far, 'dp', [(j, j ^ 1) for j in range(shards)])]
    pad x1 -> x0, local copies, waits for them, and re-layouts: 3.99 us -> none  [per_device(): jnp.pad(hidden_all, ((0, 0), (0, 0), (0, 0), (0, padded - capacity), (0,...]
    unnamed x12 -> x20, local copies, waits for them, and re-layouts: 7.97 us -> 5.13 us
    all_to_all x1, starting transfers between devices: 3.53 us -> 5.53 us  [per_device(): lax.all_to_all(send_back, ('expert', 'dp'), split_axis=0, concat_axis=0,...]
    optimization_barrier x0 -> x1, local copies, waits for them, and re-layouts: none -> 1.75 us  [per_device(): hidden_sent, cols = lax.optimization_barrier((hidden, cols))]
  transfers between devices with their start and end apart: 6 -> 6, of which waited for: 4 -> 4; matrix products, arithmetic and copies ran while one was open for 9% -> 17% of each run, Pallas kernels for 0% -> 0%
where the time goes in v1:
time: 138 us
  waiting for transfers between devices  54.1 us (39%)
  local copies, waits for them, and re-layouts  20.8 us (15%)
  Pallas kernels  19.1 us (14%)
  between operations  14.3 us (10%)
  starting transfers between devices  10.2 us (7%)
  matrix products  9.75 us (7%)
  other arithmetic  9.26 us (7%)
    ppermute x1, waiting for transfers between devices, per_device(): far = lax.ppermute(hidden_sent, 'dp', [(j, j ^ 2) for j in range(shards)])  37.9 us
    pallas_call x1, Pallas kernels, expert_kernel(): pl.pallas_call(expert_body, grid=(local_count, steps), in_specs=[piece_sp...  19.1 us
    all_to_all x1, waiting for transfers between devices, per_device(): cols = lax.all_to_all(cols, 'dp', split_axis=1, concat_axis=0, tiled=True)  9.17 us
    all_to_all x1, waiting for transfers between devices, per_device(): lax.all_to_all(send_back, ('expert', 'dp'), split_axis=0, concat_axis=0,...  6.52 us
    all_to_all x1, starting transfers between devices, per_device(): lax.all_to_all(send_back, ('expert', 'dp'), split_axis=0, concat_axis=0,...  5.53 us
    unnamed x20, local copies, waits for them, and re-layouts  5.13 us
    dot_general x1, matrix products, per_device(): jnp.einsum('blct,btd->blcd', select_gate, grad_all, preferred_element_typ...  4.48 us
    dot_general x1, matrix products, per_device(): jnp.einsum('blct,btd->blcd', select.astype(bf16), grad_all, preferred_ele...  4.39 us
  transfers between devices with their start and end apart: 6, of which 4 were waited for; matrix products, arithmetic and copies ran while one was open for 17% of the time, Pallas kernels for 0%

profile of v1, /device:TPU:0, one launch (start us, length us, event | category | flops | bytes accessed | tf_op | source)
XLA Modules:
  0.0 137.5 jit_solution(8903920102166639660)
XLA Ops:
  7.2 1.3 copy.73
  8.5 0.2 copy.75
  8.7 0.7 convert_element_type.29
  9.4 0.7 pad_maximum_fusion.1
  10.1 0.1 copy.74
  10.2 0.1 broadcast_in_dim.112
  10.4 0.9 pad_maximum_fusion
  11.2 4.3 %all-to-all-start = ((bf16[132,4,512]{2,0,1:T(8,128)(2,1)}), bf16[132,4,512]{2,0,1:T(8,128)(2,1)S(1)}, u32[]{:S(2)}, u32[]{:S(2)}) async-start(bf16[132,4,512]{2,0,1:T(8,128)(2,1)} %pad_maximum_fusion), calls=%async_computation | async-start | bytes 1114112 | tf_op jit(solution)/shard_map/all_to_all | solution.py:104
  15.6 9.2 %all-to-all-done = bf16[132,4,512]{2,0,1:T(8,128)(2,1)S(1)} async-done(((bf16[132,4,512]{2,0,1:T(8,128)(2,1)}), bf16[132,4,512]{2,0,1:T(8,128)(2,1)S(1)}, u32[]{:S(2)}, u32[]{:S(2)}) %all-to-all-start) | async-done | bytes 540704 | tf_op jit(solution)/shard_map/all_to_all | solution.py:104
  24.8 0.6 gather_fusion
  25.4 0.9 broadcast_select_fusion
  26.3 0.0 all-gather.3.cloned.1.call-update
  26.3 1.7 %copy.76 = bf16[8,1,4,36,768]{4,0,3,2,1:T(8,128)(2,1)} copy(bf16[8,1,4,36,768]{4,2,3,1,0:T(4,128)(2,1)S(1)} %copy-done.2) | data formatting | bytes 3538944 | tf_op jit(solution)/shard_map/optimization_barrier | solution.py:109
  28.1 0.4 collective-permute-start
  28.4 0.6 gather_fusion.1
  29.1 0.6 fusion.9
  29.7 0.7 convolution_convert_fusion.3
  30.5 37.9 %collective-permute-done = bf16[8,1,4,36,768]{4,0,3,2,1:T(8,128)(2,1)} collective-permute-done((bf16[8,1,4,36,768]{4,0,3,2,1:T(8,128)(2,1)}, bf16[8,1,4,36,768]{4,0,3,2,1:T(8,128)(2,1)}, u32[]{:S(2)}, u32[]{:S(2)}) %collective-permute-start) | collective-permute-done | bytes 1769504 | tf_op jit(solution)/shard_map/ppermute | solution.py:111
  68.4 1.6 %copy.80.own_ref = bf16[8,1,4,36,768]{4,3,2,1,0:T(8,128)(2,1)} copy(bf16[8,1,4,36,768]{4,2,3,1,0:T(4,128)(2,1)S(1)} %copy-done.2) | data formatting | bytes 3538944 | tf_op args[3]
  69.9 0.6 broadcast_in_dim.124
  70.5 3.1 %copy.81.far_ref = bf16[8,1,4,36,768]{4,3,2,1,0:T(8,128)(2,1)} copy(bf16[8,1,4,36,768]{4,0,3,2,1:T(8,128)(2,1)} %collective-permute-done) | data formatting | bytes 3538944 | tf_op jit(solution)/shard_map/ppermute | solution.py:111
  73.6 1.6 %copy.82.near_ref = bf16[8,1,4,36,768]{4,3,2,1,0:T(8,128)(2,1)} copy(bf16[8,1,4,36,768]{4,0,3,2,1:T(8,128)(2,1)S(1)} %collective-permute-done.1) | data formatting | bytes 3538944 | tf_op jit(solution)/shard_map/ppermute | solution.py:110
  75.3 0.5 all-gather.3.cloned.1.call-done
  75.8 1.1 slice.30
  76.9 0.4 reshape_reshape.3
  77.2 1.0 fusion.15
  78.2 1.2 copy.90
  79.5 0.2 copy.91
  79.7 0.1 compare_reduce_fusion
  79.8 0.1 fusion.8
  79.9 0.1 convolution_convert_fusion.2
  80.1 4.4 %convolution_convert_fusion.1.g_ref = bf16[16,8,48,512]{3,2,1,0:T(8,128)(2,1)} fusion(bf16[16,132,512]{2,1,0:T(8,128)(2,1)S(1)} %copy-done.1, s32[16,8,128]{2,1,0:T(8,128)S(1)} %convolution_convert_fusion.2, pred[16,8,128]{2,1,0:T(8,128)(4,1)S(1)} %bitcast.37), kind=kOutput, calls=%fused_computation.5 | convolution fusion | flops 810024960 | bytes 8470528 | tf_op jit(solution)/shard_map/blct,btd->blcd/dot_general | solution.py:136
  84.5 4.5 %convolution_convert_fusion.s_ref = bf16[16,8,48,512]{3,2,1,0:T(8,128)(2,1)} fusion(bf16[16,132,512]{2,1,0:T(8,128)(2,1)S(1)} %copy-done.1, bf16[16,8,128]{2,1,0:T(8,128)(2,1)S(1)} %bitcast.41, s32[16,8,128]{2,1,0:T(8,128)S(1)} %convolution_convert_fusion.2, pred[16,8,128]{2,1,0:T(8,128)(4,1)S(1)} %bitcast.38), kind=kOutput, calls=%fused_computation.4 | convolution fusion | flops 810811392 | bytes 8503296 | tf_op jit(solution)/shard_map/blct,btd->blcd/dot_general | solution.py:139
  89.0 3.1 %copy.83.near_far_ref = bf16[8,1,4,36,768]{4,3,2,1,0:T(8,128)(2,1)} copy(bf16[8,1,4,36,768]{4,0,3,2,1:T(8,128)(2,1)} %collective-permute-done.2) | data formatting | bytes 3538944 | tf_op jit(solution)/shard_map/ppermute | solution.py:112
  92.1 19.1 %shard_map.86 = (f32[8,768,512]{2,1,0:T(8,128)}, f32[8,768,1]{2,1,0:T(8,128)}) custom-call(bf16[8,1,4,36,768]{4,3,2,1,0:T(8,128)(2,1)} %copy.80.own_ref, bf16[8,1,4,36,768]{4,3,2,1,0:T(8,128)(2,1)} %copy.81.far_ref, bf16[8,1,4,36,768]{4,3,2,1,0:T(8,128)(2,1)} %copy.82.near_ref, bf16[8,1,4,36,768]{4,3,2,1,0:T(8,128)(2,1)} %copy.83.near_far_ref, ...), custom_call_target="tpu_custom_call" | custom-call | tf_op jit(solution)/shard_map/pallas_call | solution.py:63
  111.3 2.8 %reduce = f32[8,768]{1,0:T(8,128)S(1)} reduce(f32[8,768,1]{2,1,0:T(8,128)} %get-tuple-element.9, f32[]{:T(128)} %constant.49), dimensions={2}, to_apply=%get-tuple-element.9.reduce_sub_computation | reduce | bytes 49156 | tf_op jit(solution)/shard_map/pallas_call | solution.py:63
  114.1 0.1 reshape.89
  114.2 0.6 gather_fusion.2
  114.8 0.1 bitcast_select_fusion
  114.9 0.7 reshape.122
  115.6 5.5 %all-to-all-start.1 = ((f32[16,1,288]{2,1,0:T(1,128)}), f32[16,1,288]{2,1,0:T(1,128)S(1)}, u32[]{:S(2)}, u32[]{:S(2)}) async-start(f32[16,1,288]{2,1,0:T(1,128)} %reshape.122), calls=%async_computation.1 | async-start | bytes 49152 | tf_op jit(solution)/shard_map/all_to_all | solution.py:149
  121.2 6.5 %all-to-all-done.1 = f32[16,1,288]{2,1,0:T(1,128)S(1)} async-done(((f32[16,1,288]{2,1,0:T(1,128)}), f32[16,1,288]{2,1,0:T(1,128)S(1)}, u32[]{:S(2)}, u32[]{:S(2)}) %all-to-all-start.1) | async-done | bytes 18464 | tf_op jit(solution)/shard_map/all_to_all | solution.py:149
  127.7 0.5 broadcast.100
  128.2 0.7 reduce.1
  128.9 0.1 reshape.123
  129.0 0.1 copy.86
  129.1 0.8 select_reduce_fusion
  130.0 0.7 select_reduce_fusion.1
  (37 shorter events, 0.2 us)
Async XLA Ops:
  7.2 8.4 %copy-start = (s32[4]{0:T(128)S(1)}, s32[4]{0:T(128)}, u32[]{:S(2)}) copy-start(s32[4]{0:T(128)} %constant.47.clone) | copy-start | bytes 52
  11.2 15.1 %copy-start.2 = (bf16[8,1,4,36,768]{4,2,3,1,0:T(4,128)(2,1)S(1)}, bf16[8,1,4,36,768]{4,2,3,1,0:T(4,128)(2,1)}, u32[]{:S(2)}) copy-start(bf16[8,1,4,36,768]{4,2,3,1,0:T(4,128)(2,1)} %param.10) | copy-start | bytes 5308420
  11.2 13.5 %all-to-all-start = ((bf16[132,4,512]{2,0,1:T(8,128)(2,1)}), bf16[132,4,512]{2,0,1:T(8,128)(2,1)S(1)}, u32[]{:S(2)}, u32[]{:S(2)}) async-start(bf16[132,4,512]{2,0,1:T(8,128)(2,1)} %pad_maximum_fusion), calls=%async_computation | async-start | bytes 1114112 | tf_op jit(solution)/shard_map/all_to_all | solution.py:104
  15.6 60.2 %all-gather.3.cloned.1.call-start = ((), (), s32[]{:S(2)}) async-start(), calls=%async_computation.2 | async-start | bytes 2785280 | tf_op jit(solution)/shard_map/all_gather | solution.py:113
  26.3 2.8 %copy-start.4 = (s32[128,8]{0,1:T(8,128)S(1)}, s32[128,8]{0,1:T(8,128)}, u32[]{:S(2)}) copy-start(s32[128,8]{0,1:T(8,128)} %param.9) | copy-start | bytes 12292
  28.1 40.3 %collective-permute-start = (bf16[8,1,4,36,768]{4,0,3,2,1:T(8,128)(2,1)}, bf16[8,1,4,36,768]{4,0,3,2,1:T(8,128)(2,1)}, u32[]{:S(2)}, u32[]{:S(2)}) collective-permute-start(bf16[8,1,4,36,768]{4,0,3,2,1:T(8,128)(2,1)} %copy.76), channel_id=1, source_target_pairs={{0,2},{1,3},{2,0},{3,1},{4,6},{5,7},{6,4},{7,5},{8,10},{9,11},{10,... | collective-permute-start | bytes 5308424 | tf_op jit(solution)/shard_map/ppermute | solution.py:111
  28.4 45.2 %collective-permute-start.1 = (bf16[8,1,4,36,768]{4,0,3,2,1:T(8,128)(2,1)}, bf16[8,1,4,36,768]{4,0,3,2,1:T(8,128)(2,1)S(1)}, u32[]{:S(2)}, u32[]{:S(2)}) collective-permute-start(bf16[8,1,4,36,768]{4,0,3,2,1:T(8,128)(2,1)} %copy.76), channel_id=1, source_target_pairs={{0,1},{1,0},{2,3},{3,2},{4,5},{5,4},{6,7},{7,6},{8,9},{9,8},{10,11... | collective-permute-start | bytes 5308424 | tf_op jit(solution)/shard_map/ppermute | solution.py:110
  68.3 20.6 %collective-permute-start.2 = (bf16[8,1,4,36,768]{4,0,3,2,1:T(8,128)(2,1)}, bf16[8,1,4,36,768]{4,0,3,2,1:T(8,128)(2,1)}, u32[]{:S(2)}, u32[]{:S(2)}) collective-permute-start(bf16[8,1,4,36,768]{4,0,3,2,1:T(8,128)(2,1)} %collective-permute-done), channel_id=1, source_target_pairs={{0,1},{1,0},{2,3},{3,2},{4,5},{5,4},{6,7},{7,6},{8,9},{9,8},{10,11... | collective-permute-start | bytes 5308424 | tf_op jit(solution)/shard_map/ppermute | solution.py:112
  75.8 4.3 %copy-start.1 = (bf16[16,132,512]{2,1,0:T(8,128)(2,1)S(1)}, bf16[16,132,512]{2,1,0:T(8,128)(2,1)}, u32[]{:S(2)}) copy-start(bf16[16,132,512]{2,1,0:T(8,128)(2,1)} %all-gather.3.cloned.1.call-done) | copy-start | bytes 6488068
  111.3 3.5 %copy-start.6 = (pred[16]{0:T(512)(128)(4,1)S(1)}, pred[16]{0:T(512)(128)(4,1)}, u32[]{:S(2)}) copy-start(pred[16]{0:T(512)(128)(4,1)} %broadcast_in_dim.124) | copy-start | bytes 52
  111.3 9.9 %copy-start.5 = (s32[128,32]{0,1:T(8,128)S(1)}, s32[128,32]{0,1:T(8,128)}, u32[]{:S(2)}) copy-start(s32[128,32]{0,1:T(8,128)} %convolution_convert_fusion.3) | copy-start | bytes 49156
  111.3 17.9 %copy-start.3 = (pred[128,8,32]{0,2,1:T(8,128)(4,1)S(1)}, pred[128,8,32]{0,2,1:T(8,128)(4,1)}, u32[]{:S(2)}) copy-start(pred[128,8,32]{0,2,1:T(8,128)(4,1)} %get-tuple-element.15) | copy-start | bytes 98308
  115.6 12.1 %all-to-all-start.1 = ((f32[16,1,288]{2,1,0:T(1,128)}), f32[16,1,288]{2,1,0:T(1,128)S(1)}, u32[]{:S(2)}, u32[]{:S(2)}) async-start(f32[16,1,288]{2,1,0:T(1,128)} %reshape.122), calls=%async_computation.1 | async-start | bytes 49152 | tf_op jit(solution)/shard_map/all_to_all | solution.py:149
Sparse Core Ops, SparseCore 0:
  26.4 49.3 all-gather.2

commit v2 on v1

--- a/solution.py
+++ b/solution.py
@@ -6,13 +6,13 @@
 from jax.sharding import PartitionSpec as P
 
 
-def expert_body(own_ref, far_ref, near_ref, near_far_ref, s_ref, g_ref, w_ref, wg_ref, slot_ref, h_scr):
+def expert_body(own_ref, far_ref, near_ref, near_far_ref, tok_ref, sel_ref, gate_ref, w_ref,
+                wg_ref, slot_ref, h_scr, s_scr, g_scr):
     expert = pl.program_id(0)
     chunk = pl.program_id(1)
     sources, capacity, hidden_width = own_ref.shape[2:]
-    blocks, padded = s_ref.shape[0], s_ref.shape[2]
-    col_width = s_ref.shape[3]
-    rows = blocks * padded
+    blocks, _, padded, _ = sel_ref.shape
+    col_width = tok_ref.shape[2]
     pieces = (own_ref, far_ref, near_ref, near_far_ref)
 
     @pl.when((expert == 0) & (chunk == 0))
@@ -24,10 +24,14 @@
             row = (src * len(pieces) + j) * padded
             h_scr[row:row + capacity, :] = ref[0, 0, src]
 
+    for blk in range(blocks):
+        rows = jnp.dot(sel_ref[blk, 0], tok_ref[blk], preferred_element_type=jnp.float32)
+        g_scr[blk * padded:(blk + 1) * padded, :] = rows.astype(jnp.bfloat16)
+        s_scr[blk * padded:(blk + 1) * padded, :] = (gate_ref[blk, 0] * rows).astype(jnp.bfloat16)
+
     h = h_scr[...]
     part = lax.dot_general(
-        h, s_ref[:, 0].reshape(rows, col_width), (((0,), (0,)), ((), ())),
-        preferred_element_type=jnp.float32,
+        h, s_scr[...], (((0,), (0,)), ((), ())), preferred_element_type=jnp.float32
     )
 
     @pl.when(chunk == 0)
@@ -39,13 +43,13 @@
         wg_ref[0] = wg_ref[0] + part
 
     out = jnp.dot(h, w_ref[0], preferred_element_type=jnp.float32)
-    g = g_ref[:, 0].reshape(rows, col_width).astype(jnp.float32)
-    slot_ref[0] = jnp.sum(g * out, axis=1, keepdims=True)
+    slot_ref[0] = jnp.sum(g_scr[...].astype(jnp.float32) * out, axis=1, keepdims=True)
 
 
-def expert_kernel(pieces, scaled_rows, grad_rows, weight):
+def expert_kernel(pieces, tokens, select, gate_slot, weight):
     local_count, _, source_count, capacity, hidden_width = pieces[0].shape
-    block_count, _, padded, col_width = scaled_rows.shape
+    block_count, tok_rows, col_width = tokens.shape
+    padded = select.shape[2]
     per_source = block_count // source_count
     chunk = source_count
     for size in (4, 2, 1):
@@ -53,19 +57,18 @@
             chunk = size
             break
     steps = source_count // chunk
-    rows = chunk * per_source * padded
+    blocks = chunk * per_source
+    rows = blocks * padded
     piece_spec = pl.BlockSpec(
         (1, 1, chunk, capacity, hidden_width), lambda l, r: (l, 0, r, 0, 0)
-    )
-    row_spec = pl.BlockSpec(
-        (chunk * per_source, 1, padded, col_width), lambda l, r: (r, l, 0, 0)
     )
     return pl.pallas_call(
         expert_body,
         grid=(local_count, steps),
         in_specs=[piece_spec] * len(pieces) + [
-            row_spec,
-            row_spec,
+            pl.BlockSpec((blocks, tok_rows, col_width), lambda l, r: (r, 0, 0)),
+            pl.BlockSpec((blocks, 1, padded, tok_rows), lambda l, r: (r, l, 0, 0)),
+            pl.BlockSpec((blocks, 1, padded, 1), lambda l, r: (r, l, 0, 0)),
             pl.BlockSpec((1, hidden_width, col_width), lambda l, r: (l, 0, 0)),
         ],
         out_specs=[
@@ -76,8 +79,12 @@
             jax.ShapeDtypeStruct((local_count, hidden_width, col_width), jnp.float32),
             jax.ShapeDtypeStruct((local_count, block_count * padded, 1), jnp.float32),
         ],
-        scratch_shapes=[pltpu.VMEM((rows, hidden_width), jnp.bfloat16)],
-    )(*pieces, scaled_rows, grad_rows, weight)
+        scratch_shapes=[
+            pltpu.VMEM((rows, hidden_width), jnp.bfloat16),
+            pltpu.VMEM((rows, col_width), jnp.bfloat16),
+            pltpu.VMEM((rows, col_width), jnp.bfloat16),
+        ],
+    )(*pieces, tokens, select, gate_slot, weight)
 
 
 def per_device(out_grad, gate_weights, expert_ids, hidden, down_weight):
@@ -132,15 +139,10 @@
     rank_t = rank.transpose(0, 2, 1)
     gate_t = gate_hit.transpose(0, 2, 1)
     select = chose_t[:, :, None, :] & (rank_t[:, :, None, :] == slot_ids[None, None, :, None])
-    select_gate = jnp.where(select, gate_t[:, :, None, :], 0.0).astype(bf16)
-    grad_rows = jnp.einsum(
-        "blct,btd->blcd", select.astype(bf16), grad_all, preferred_element_type=f32
-    ).astype(bf16)
-    scaled = jnp.einsum(
-        "blct,btd->blcd", select_gate, grad_all, preferred_element_type=f32
-    ).astype(bf16)
-
-    weight_grad, slot_part = expert_kernel((hidden, far, near, near_far), scaled, grad_rows, down_weight)
+    gate_slot = jnp.sum(jnp.where(select, gate_t[:, :, None, :], 0.0), axis=3, keepdims=True)
+    weight_grad, slot_part = expert_kernel(
+        (hidden, far, near, near_far), grad_all, select.astype(bf16), gate_slot, down_weight
+    )
     slot_part = slot_part.reshape(local_count, block_count, padded)[:, :, :capacity]
     slot_part = slot_part.transpose(1, 0, 2).reshape(peer_count, shards, local_count, capacity)
     piece_of = jnp.array([0, 2, 1, 3], jnp.int32)[jnp.arange(shards, dtype=jnp.int32) ^ my_dp]

time: 138 us -> 131 us (0.949)
  matrix products: 9.75 us -> 0.88 us
  other arithmetic: 9.26 us -> 11.2 us
  local copies, waits for them, and re-layouts: 20.8 us -> 22.7 us
    dot_general x2 -> x0, matrix products: 8.87 us -> none  [the longest x1 4.48 us: per_device(): jnp.einsum('blct,btd->blcd', select_gate, grad_all, preferred_element_typ...]
    broadcast_in_dim x0 -> x1, local copies, waits for them, and re-layouts: none -> 2.29 us  [per_device(): jnp.sum(jnp.where(select, gate_t[:, :, None, :], 0.0), axis=3, keepdims=T...]
    convert_element_type x0 -> x1, other arithmetic: none -> 1.9 us  [per_device(): select.astype(bf16)]
    reduce_sum x0 -> x1, other arithmetic: none -> 1.44 us  [per_device(): jnp.sum(jnp.where(select, gate_t[:, :, None, :], 0.0), axis=3, keepdims=T...]
    unnamed x20 -> x22, local copies, waits for them, and re-layouts: 5.13 us -> 4.12 us
  transfers between devices with their start and end apart: 6 -> 6, of which waited for: 4 -> 4; matrix products, arithmetic and copies ran while one was open for 17% -> 16% of each run, Pallas kernels for 0% -> 0%
where the time goes in v2:
time: 131 us
  waiting for transfers between devices  54.1 us (41%)
  local copies, waits for them, and re-layouts  22.7 us (17%)
  Pallas kernels  18.2 us (14%)
  between operations  14.3 us (11%)
  other arithmetic  11.2 us (9%)
  starting transfers between devices  9.41 us (7%)
    ppermute x1, waiting for transfers between devices, per_device(): far = lax.ppermute(hidden_sent, 'dp', [(j, j ^ 2) for j in range(shards)])  37.1 us
    pallas_call x1, Pallas kernels, expert_kernel(): pl.pallas_call(expert_body, grid=(local_count, steps), in_specs=[piece_sp...  18.2 us
    all_to_all x1, waiting for transfers between devices, per_device(): cols = lax.all_to_all(cols, 'dp', split_axis=1, concat_axis=0, tiled=True)  9.17 us
    all_to_all x1, waiting for transfers between devices, per_device(): lax.all_to_all(send_back, ('expert', 'dp'), split_axis=0, concat_axis=0,...  6.52 us
    all_to_all x1, starting transfers between devices, per_device(): lax.all_to_all(send_back, ('expert', 'dp'), split_axis=0, concat_axis=0,...  4.7 us
    all_to_all x1, starting transfers between devices, per_device(): cols = lax.all_to_all(cols, 'dp', split_axis=1, concat_axis=0, tiled=True)  4.34 us
    unnamed x22, local copies, waits for them, and re-layouts  4.12 us
    ppermute x1, local copies, waits for them, and re-layouts, per_device(): near_far = lax.ppermute(far, 'dp', [(j, j ^ 1) for j in range(shards)])  3.13 us
  transfers between devices with their start and end apart: 6, of which 4 were waited for; matrix products, arithmetic and copies ran while one was open for 16% of the time, Pallas kernels for 0%

profile of v2, /device:TPU:0, one launch (start us, length us, event | category | flops | bytes accessed | tf_op | source)
XLA Modules:
  0.0 130.8 jit_solution(1284462179009908956)
XLA Ops:
  7.2 1.3 %copy.78 = bf16[128,2048]{0,1:T(8,128)(2,1)S(1)} copy(bf16[128,2048]{1,0:T(8,128)(2,1)} %param.7) | data formatting | bytes 1048576 | tf_op args[0]
  8.5 0.2 copy.80
  8.8 0.1 copy.79
  8.9 0.1 broadcast_in_dim.115
  9.1 0.9 pad_maximum_fusion
  9.9 4.3 %all-to-all-start = ((bf16[132,4,512]{2,0,1:T(8,128)(2,1)}), bf16[132,4,512]{2,0,1:T(8,128)(2,1)S(1)}, u32[]{:S(2)}, u32[]{:S(2)}) async-start(bf16[132,4,512]{2,0,1:T(8,128)(2,1)} %pad_maximum_fusion), calls=%async_computation | async-start | bytes 1114112 | tf_op jit(solution)/shard_map/all_to_all | solution.py:111
  14.3 9.2 %all-to-all-done = bf16[132,4,512]{2,0,1:T(8,128)(2,1)S(1)} async-done(((bf16[132,4,512]{2,0,1:T(8,128)(2,1)}), bf16[132,4,512]{2,0,1:T(8,128)(2,1)S(1)}, u32[]{:S(2)}, u32[]{:S(2)}) %all-to-all-start) | async-done | bytes 540704 | tf_op jit(solution)/shard_map/all_to_all | solution.py:111
  23.5 0.6 gather_fusion
  24.1 0.9 broadcast_select_fusion
  25.0 0.0 all-gather.3.cloned.1.call-update
  25.0 1.7 %copy.81 = bf16[8,1,4,36,768]{4,0,3,2,1:T(8,128)(2,1)} copy(bf16[8,1,4,36,768]{4,2,3,1,0:T(4,128)(2,1)S(1)} %copy-done.1) | data formatting | bytes 3538944 | tf_op jit(solution)/shard_map/optimization_barrier | solution.py:116
  26.7 0.4 collective-permute-start
  27.1 1.6 %copy.85.own_ref = bf16[8,1,4,36,768]{4,3,2,1,0:T(8,128)(2,1)} copy(bf16[8,1,4,36,768]{4,2,3,1,0:T(4,128)(2,1)S(1)} %copy-done.1) | data formatting | bytes 3538944 | tf_op args[3]
  28.7 0.6 gather_fusion.1
  29.4 0.6 broadcast_in_dim.128
  30.0 37.1 %collective-permute-done = bf16[8,1,4,36,768]{4,0,3,2,1:T(8,128)(2,1)} collective-permute-done((bf16[8,1,4,36,768]{4,0,3,2,1:T(8,128)(2,1)}, bf16[8,1,4,36,768]{4,0,3,2,1:T(8,128)(2,1)}, u32[]{:S(2)}, u32[]{:S(2)}) %collective-permute-start) | collective-permute-done | bytes 1769504 | tf_op jit(solution)/shard_map/ppermute | solution.py:118
  67.0 0.6 fusion.3
  67.7 0.7 convolution_convert_fusion.1
  68.4 3.1 %copy.86.far_ref = bf16[8,1,4,36,768]{4,3,2,1,0:T(8,128)(2,1)} copy(bf16[8,1,4,36,768]{4,0,3,2,1:T(8,128)(2,1)} %collective-permute-done) | data formatting | bytes 3538944 | tf_op jit(solution)/shard_map/ppermute | solution.py:118
  71.5 1.6 %copy.87.near_ref = bf16[8,1,4,36,768]{4,3,2,1,0:T(8,128)(2,1)} copy(bf16[8,1,4,36,768]{4,0,3,2,1:T(8,128)(2,1)S(1)} %collective-permute-done.1) | data formatting | bytes 3538944 | tf_op jit(solution)/shard_map/ppermute | solution.py:117
  73.2 1.3 %all-gather.3.cloned.1.call-done = bf16[16,132,512]{2,1,0:T(8,128)(2,1)} async-done(((bf16[4,132,512]{2,1,0:T(8,128)(2,1)}), bf16[16,132,512]{2,1,0:T(8,128)(2,1)}) %all-gather.3.cloned.1.call-update) | async-done | bytes 2162704 | tf_op jit(solution)/shard_map/all_gather | solution.py:120
  74.5 0.9 slice.31
  75.4 0.4 reshape_reshape.3
  75.8 0.2 fusion.8
  76.0 0.2 copy.95
  76.2 0.2 copy.96
  76.4 0.1 compare_reduce_fusion
  76.6 0.1 fusion.2
  76.7 0.1 convolution_convert_fusion
  76.9 1.4 %select_reduce_fusion.1 = f32[16,8,48]{2,1,0:T(8,128)S(1)} fusion(f32[16,8,128]{2,1,0:T(8,128)S(1)} %bitcast.34, s32[16,8,128]{2,1,0:T(8,128)S(1)} %convolution_convert_fusion, pred[16,8,128]{2,1,0:T(8,128)(4,1)S(1)} %bitcast.32), kind=kLoop, calls=%fused_computation.4 | loop fusion | flops 3139584 | bytes 172032 | tf_op jit(solution)/shard_map/reduce_sum | solution.py:142
  78.3 2.3 %copy.89.gate_ref = f32[16,8,48,1]{3,2,1,0:T(8,128)} copy(f32[16,8,48,1]{2,1,0,3:T(8,128)S(1)} %bitcast.35) | data formatting | bytes 49152 | tf_op jit(solution)/shard_map/broadcast_in_dim | solution.py:142
  80.6 1.6 %slice.30.tok_ref = bf16[16,128,512]{2,1,0:T(8,128)(2,1)} slice(bf16[16,132,512]{2,1,0:T(8,128)(2,1)S(1)} %copy-done.2), slice={[0:16], [0:128], [0:512]} | slice | bytes 4194304 | tf_op jit(solution)/shard_map/slice | solution.py:122
  82.2 1.9 %fusion.1.sel_ref = bf16[16,8,48,128]{3,2,1,0:T(8,128)(2,1)} fusion(s32[16,8,128]{2,1,0:T(8,128)S(1)} %convolution_convert_fusion, pred[16,8,128]{2,1,0:T(8,128)(4,1)S(1)} %bitcast.33), kind=kLoop, calls=%fused_computation.7 | loop fusion | flops 2359296 | bytes 1654784 | tf_op jit(solution)/shard_map/convert_element_type | solution.py:144
  84.1 3.1 %copy.88.near_far_ref = bf16[8,1,4,36,768]{4,3,2,1,0:T(8,128)(2,1)} copy(bf16[8,1,4,36,768]{4,0,3,2,1:T(8,128)(2,1)} %collective-permute-done.2) | data formatting | bytes 3538944 | tf_op jit(solution)/shard_map/ppermute | solution.py:119
  87.2 18.2 %shard_map.86 = (f32[8,768,512]{2,1,0:T(8,128)}, f32[8,768,1]{2,1,0:T(8,128)}) custom-call(bf16[8,1,4,36,768]{4,3,2,1,0:T(8,128)(2,1)} %copy.85.own_ref, bf16[8,1,4,36,768]{4,3,2,1,0:T(8,128)(2,1)} %copy.86.far_ref, bf16[8,1,4,36,768]{4,3,2,1,0:T(8,128)(2,1)} %copy.87.near_ref, bf16[8,1,4,36,768]{4,3,2,1,0:T(8,128)(2,1)} %copy.88.near_far_ref, ...), custom_call_target="tpu_custom_call" | custom-call | tf_op jit(solution)/shard_map/pallas_call | solution.py:65
  105.4 2.8 %reduce = f32[8,768]{1,0:T(8,128)S(1)} reduce(f32[8,768,1]{2,1,0:T(8,128)} %get-tuple-element.9, f32[]{:T(128)} %constant.49), dimensions={2}, to_apply=%get-tuple-element.9.reduce_sub_computation | reduce | bytes 49156 | tf_op jit(solution)/shard_map/pallas_call | solution.py:65
  108.2 0.1 reshape.89
  108.3 0.6 gather_fusion.2
  108.9 0.1 bitcast_select_fusion
  109.0 0.7 reshape.121
  109.7 4.7 %all-to-all-start.1 = ((f32[16,1,288]{2,1,0:T(1,128)}), f32[16,1,288]{2,1,0:T(1,128)S(1)}, u32[]{:S(2)}, u32[]{:S(2)}) async-start(f32[16,1,288]{2,1,0:T(1,128)} %reshape.121), calls=%async_computation.1 | async-start | bytes 49152 | tf_op jit(solution)/shard_map/all_to_all | solution.py:151
  114.5 6.5 %all-to-all-done.1 = f32[16,1,288]{2,1,0:T(1,128)S(1)} async-done(((f32[16,1,288]{2,1,0:T(1,128)}), f32[16,1,288]{2,1,0:T(1,128)S(1)}, u32[]{:S(2)}, u32[]{:S(2)}) %all-to-all-start.1) | async-done | bytes 18464 | tf_op jit(solution)/shard_map/all_to_all | solution.py:151
  121.0 0.5 broadcast.100
  121.5 0.7 reduce.1
  122.2 0.1 reshape.122
  122.3 0.1 copy.92
  122.4 0.8 select_reduce_fusion
  123.3 0.7 select_reduce_fusion.2
  (41 shorter events, 0.2 us)
Async XLA Ops:
  7.2 7.1 %copy-start = (s32[4]{0:T(128)S(1)}, s32[4]{0:T(128)}, u32[]{:S(2)}) copy-start(s32[4]{0:T(128)} %constant.47.clone) | copy-start | bytes 52
  7.2 1.6 %copy-start.4 = (s32[128,8]{0,1:T(8,128)S(1)}, s32[128,8]{0,1:T(8,128)}, u32[]{:S(2)}) copy-start(s32[128,8]{0,1:T(8,128)} %param.9) | copy-start | bytes 12292
  7.2 1.6 %copy-start.6 = (bf16[128,8]{0,1:T(8,128)(2,1)S(1)}, bf16[128,8]{0,1:T(8,128)(2,1)}, u32[]{:S(2)}) copy-start(bf16[128,8]{0,1:T(8,128)(2,1)} %param.8) | copy-start | bytes 6148
  9.9 15.1 %copy-start.1 = (bf16[8,1,4,36,768]{4,2,3,1,0:T(4,128)(2,1)S(1)}, bf16[8,1,4,36,768]{4,2,3,1,0:T(4,128)(2,1)}, u32[]{:S(2)}) copy-start(bf16[8,1,4,36,768]{4,2,3,1,0:T(4,128)(2,1)} %param.10) | copy-start | bytes 5308420
  9.9 13.5 %all-to-all-start = ((bf16[132,4,512]{2,0,1:T(8,128)(2,1)}), bf16[132,4,512]{2,0,1:T(8,128)(2,1)S(1)}, u32[]{:S(2)}, u32[]{:S(2)}) async-start(bf16[132,4,512]{2,0,1:T(8,128)(2,1)} %pad_maximum_fusion), calls=%async_computation | async-start | bytes 1114112 | tf_op jit(solution)/shard_map/all_to_all | solution.py:111
  14.3 60.2 %all-gather.3.cloned.1.call-start = ((), (), s32[]{:S(2)}) async-start(), calls=%async_computation.2 | async-start | bytes 2785280 | tf_op jit(solution)/shard_map/all_gather | solution.py:120
  26.7 40.3 %collective-permute-start = (bf16[8,1,4,36,768]{4,0,3,2,1:T(8,128)(2,1)}, bf16[8,1,4,36,768]{4,0,3,2,1:T(8,128)(2,1)}, u32[]{:S(2)}, u32[]{:S(2)}) collective-permute-start(bf16[8,1,4,36,768]{4,0,3,2,1:T(8,128)(2,1)} %copy.81), channel_id=1, source_target_pairs={{0,2},{1,3},{2,0},{3,1},{4,6},{5,7},{6,4},{7,5},{8,10},{9,11},{10,... | collective-permute-start | bytes 5308424 | tf_op jit(solution)/shard_map/ppermute | solution.py:118
  27.1 44.4 %collective-permute-start.1 = (bf16[8,1,4,36,768]{4,0,3,2,1:T(8,128)(2,1)}, bf16[8,1,4,36,768]{4,0,3,2,1:T(8,128)(2,1)S(1)}, u32[]{:S(2)}, u32[]{:S(2)}) collective-permute-start(bf16[8,1,4,36,768]{4,0,3,2,1:T(8,128)(2,1)} %copy.81), channel_id=1, source_target_pairs={{0,1},{1,0},{2,3},{3,2},{4,5},{5,4},{6,7},{7,6},{8,9},{9,8},{10,11... | collective-permute-start | bytes 5308424 | tf_op jit(solution)/shard_map/ppermute | solution.py:117
  67.0 17.0 %collective-permute-start.2 = (bf16[8,1,4,36,768]{4,0,3,2,1:T(8,128)(2,1)}, bf16[8,1,4,36,768]{4,0,3,2,1:T(8,128)(2,1)}, u32[]{:S(2)}, u32[]{:S(2)}) collective-permute-start(bf16[8,1,4,36,768]{4,0,3,2,1:T(8,128)(2,1)} %collective-permute-done), channel_id=1, source_target_pairs={{0,1},{1,0},{2,3},{3,2},{4,5},{5,4},{6,7},{7,6},{8,9},{9,8},{10,11... | collective-permute-start | bytes 5308424 | tf_op jit(solution)/shard_map/ppermute | solution.py:119
  76.2 4.4 %copy-start.2 = (bf16[16,132,512]{2,1,0:T(8,128)(2,1)S(1)}, bf16[16,132,512]{2,1,0:T(8,128)(2,1)}, u32[]{:S(2)}) copy-start(bf16[16,132,512]{2,1,0:T(8,128)(2,1)} %all-gather.3.cloned.1.call-done) | copy-start | bytes 6488068
  105.4 3.5 %copy-start.7 = (pred[16]{0:T(512)(128)(4,1)S(1)}, pred[16]{0:T(512)(128)(4,1)}, u32[]{:S(2)}) copy-start(pred[16]{0:T(512)(128)(4,1)} %broadcast_in_dim.128) | copy-start | bytes 52
  105.4 9.1 %copy-start.5 = (s32[128,32]{0,1:T(8,128)S(1)}, s32[128,32]{0,1:T(8,128)}, u32[]{:S(2)}) copy-start(s32[128,32]{0,1:T(8,128)} %convolution_convert_fusion.1) | copy-start | bytes 49156
  105.4 17.0 %copy-start.3 = (pred[128,8,32]{0,2,1:T(8,128)(4,1)S(1)}, pred[128,8,32]{0,2,1:T(8,128)(4,1)}, u32[]{:S(2)}) copy-start(pred[128,8,32]{0,2,1:T(8,128)(4,1)} %get-tuple-element.15) | copy-start | bytes 98308
  109.7 11.3 %all-to-all-start.1 = ((f32[16,1,288]{2,1,0:T(1,128)}), f32[16,1,288]{2,1,0:T(1,128)S(1)}, u32[]{:S(2)}, u32[]{:S(2)}) async-start(f32[16,1,288]{2,1,0:T(1,128)} %reshape.121), calls=%async_computation.1 | async-start | bytes 49152 | tf_op jit(solution)/shard_map/all_to_all | solution.py:151
Sparse Core Ops, SparseCore 0:
  25.1 49.3 all-gather.2

commit v3 on v2

--- a/solution.py
+++ b/solution.py
@@ -6,13 +6,13 @@
 from jax.sharding import PartitionSpec as P
 
 
-def expert_body(own_ref, far_ref, near_ref, near_far_ref, tok_ref, sel_ref, gate_ref, w_ref,
+def expert_body(own_ref, far_ref, near_ref, near_far_ref, mine_ref, rest_ref, sel_ref, gate_ref, w_ref,
                 wg_ref, slot_ref, h_scr, s_scr, g_scr):
     expert = pl.program_id(0)
     chunk = pl.program_id(1)
     sources, capacity, hidden_width = own_ref.shape[2:]
     blocks, _, padded, _ = sel_ref.shape
-    col_width = tok_ref.shape[2]
+    col_width = mine_ref.shape[2]
     pieces = (own_ref, far_ref, near_ref, near_far_ref)
 
     @pl.when((expert == 0) & (chunk == 0))
@@ -25,7 +25,9 @@
             h_scr[row:row + capacity, :] = ref[0, 0, src]
 
     for blk in range(blocks):
-        rows = jnp.dot(sel_ref[blk, 0], tok_ref[blk], preferred_element_type=jnp.float32)
+        src, j = divmod(blk, len(pieces))
+        tok = mine_ref[src] if j == 0 else rest_ref[src, j - 1]
+        rows = jnp.dot(sel_ref[blk, 0], tok, preferred_element_type=jnp.float32)
         g_scr[blk * padded:(blk + 1) * padded, :] = rows.astype(jnp.bfloat16)
         s_scr[blk * padded:(blk + 1) * padded, :] = (gate_ref[blk, 0] * rows).astype(jnp.bfloat16)
 
@@ -43,13 +45,19 @@
         wg_ref[0] = wg_ref[0] + part
 
     out = jnp.dot(h, w_ref[0], preferred_element_type=jnp.float32)
-    slot_ref[0] = jnp.sum(g_scr[...].astype(jnp.float32) * out, axis=1, keepdims=True)
+    prod = g_scr[...].astype(jnp.float32) * out
+    ones = jnp.ones((8, col_width), jnp.float32)
+    sums = lax.dot_general(
+        ones, prod, (((1,), (1,)), ((), ())),
+        precision=lax.Precision.HIGHEST, preferred_element_type=jnp.float32,
+    )
+    slot_ref[0] = sums[0:1]
 
 
-def expert_kernel(pieces, tokens, select, gate_slot, weight):
+def expert_kernel(pieces, mine, rest, select, gate_slot, weight):
     local_count, _, source_count, capacity, hidden_width = pieces[0].shape
-    block_count, tok_rows, col_width = tokens.shape
-    padded = select.shape[2]
+    col_width = mine.shape[2]
+    block_count, _, padded, tok_rows = select.shape
     per_source = block_count // source_count
     chunk = source_count
     for size in (4, 2, 1):
@@ -66,25 +74,26 @@
         expert_body,
         grid=(local_count, steps),
         in_specs=[piece_spec] * len(pieces) + [
-            pl.BlockSpec((blocks, tok_rows, col_width), lambda l, r: (r, 0, 0)),
+            pl.BlockSpec((chunk, tok_rows, col_width), lambda l, r: (r, 0, 0)),
+            pl.BlockSpec((chunk, per_source - 1, tok_rows, col_width), lambda l, r: (r, 0, 0, 0)),
             pl.BlockSpec((blocks, 1, padded, tok_rows), lambda l, r: (r, l, 0, 0)),
             pl.BlockSpec((blocks, 1, padded, 1), lambda l, r: (r, l, 0, 0)),
             pl.BlockSpec((1, hidden_width, col_width), lambda l, r: (l, 0, 0)),
         ],
         out_specs=[
             pl.BlockSpec((1, hidden_width, col_width), lambda l, r: (l, 0, 0)),
-            pl.BlockSpec((1, rows, 1), lambda l, r: (l, r, 0)),
+            pl.BlockSpec((1, 1, rows), lambda l, r: (l, 0, r)),
         ],
         out_shape=[
             jax.ShapeDtypeStruct((local_count, hidden_width, col_width), jnp.float32),
-            jax.ShapeDtypeStruct((local_count, block_count * padded, 1), jnp.float32),
+            jax.ShapeDtypeStruct((local_count, 1, block_count * padded), jnp.float32),
         ],
         scratch_shapes=[
             pltpu.VMEM((rows, hidden_width), jnp.bfloat16),
             pltpu.VMEM((rows, col_width), jnp.bfloat16),
             pltpu.VMEM((rows, col_width), jnp.bfloat16),
         ],
-    )(*pieces, tokens, select, gate_slot, weight)
+    )(*pieces, mine, rest, select, gate_slot, weight)
 
 
 def per_device(out_grad, gate_weights, expert_ids, hidden, down_weight):
@@ -108,19 +117,20 @@
     meta = jnp.pad(meta, (0, meta_rows * col_width - meta_len)).reshape(meta_rows, 1, col_width)
     cols = out_grad.reshape(tok_rows, shards, col_width)
     cols = jnp.concatenate([cols, jnp.broadcast_to(meta, (meta_rows, shards, col_width))], axis=0)
+    mine = lax.dynamic_index_in_dim(cols, my_dp, axis=1, keepdims=False)
+    mine_all = lax.all_gather(mine, "expert", axis=0, tiled=False)
     cols = lax.all_to_all(cols, "dp", split_axis=1, concat_axis=0, tiled=True)
     cols = cols.reshape(shards, tok_rows + meta_rows, col_width)
-    piece_xor = jnp.array([0, 2, 1, 3], jnp.int32)
+    piece_xor = jnp.array([2, 1, 3], jnp.int32)
     cols = jnp.take(cols, piece_xor ^ my_dp, axis=0)
 
     hidden_sent, cols = lax.optimization_barrier((hidden, cols))
     near = lax.ppermute(hidden_sent, "dp", [(j, j ^ 1) for j in range(shards)])
     far = lax.ppermute(hidden_sent, "dp", [(j, j ^ 2) for j in range(shards)])
     near_far = lax.ppermute(far, "dp", [(j, j ^ 1) for j in range(shards)])
-    got = lax.all_gather(cols, "expert", axis=0, tiled=False)
-    got = got.reshape(block_count, tok_rows + meta_rows, col_width)
-    grad_all = got[:, :tok_rows]
-    meta_all = got[:, tok_rows:].reshape(block_count, meta_rows * col_width)[:, :meta_len]
+    rest_all = lax.all_gather(cols, "expert", axis=0, tiled=False)
+    meta_all = jnp.concatenate([mine_all[:, None, tok_rows:], rest_all[:, :, tok_rows:]], axis=1)
+    meta_all = meta_all.reshape(block_count, meta_rows * col_width)[:, :meta_len]
     meta_all = meta_all.reshape(block_count, tok_rows, 2 * top_count)
     ids_all = meta_all[:, :, :top_count].astype(jnp.int32)
     gate_all = meta_all[:, :, top_count:]
@@ -141,7 +151,7 @@
     select = chose_t[:, :, None, :] & (rank_t[:, :, None, :] == slot_ids[None, None, :, None])
     gate_slot = jnp.sum(jnp.where(select, gate_t[:, :, None, :], 0.0), axis=3, keepdims=True)
     weight_grad, slot_part = expert_kernel(
-        (hidden, far, near, near_far), grad_all, select.astype(bf16), gate_slot, down_weight
+        (hidden, far, near, near_far), mine_all, rest_all, select.astype(bf16), gate_slot, down_weight
     )
     slot_part = slot_part.reshape(local_count, block_count, padded)[:, :, :capacity]
     slot_part = slot_part.transpose(1, 0, 2).reshape(peer_count, shards, local_count, capacity)

time: 131 us -> 145 us (1.11)
  blocking collectives: 0 us -> 40.4 us
  waiting for transfers between devices: 54.1 us -> 17.2 us
  Pallas kernels: 18.2 us -> 29.6 us
  local copies, waits for them, and re-layouts: 22.7 us -> 21 us
    all_gather x0 -> x1, blocking collectives: none -> 40.4 us  [per_device(): mine_all = lax.all_gather(mine, 'expert', axis=0, tiled=False)]
    ppermute x1, waiting for transfers between devices: 37.1 us -> 0.01 us  [per_device(): far = lax.ppermute(hidden_sent, 'dp', [(j, j ^ 2) for j in range(shards)])]
    pallas_call x1, Pallas kernels: 18.2 us -> 29.6 us  [expert_kernel(): pl.pallas_call(expert_body, grid=(local_count, steps), in_specs=[piece_sp...]
    all_gather x0 -> x1, other arithmetic: none -> 3.41 us  [per_device(): mine_all = lax.all_gather(mine, 'expert', axis=0, tiled=False)]
    pallas_call x1, other arithmetic: 2.79 us -> 0.79 us  [expert_kernel(): pl.pallas_call(expert_body, grid=(local_count, steps), in_specs=[piece_sp...]
    slice x2 -> x1, local copies, waits for them, and re-layouts: 2.49 us -> 0.91 us  [per_device(): rest_all[:, :, tok_rows:]]
    unnamed x22 -> x18, local copies, waits for them, and re-layouts: 4.12 us -> 4.08 us
  transfers between devices with their start and end apart: 6 -> 6, of which waited for: 4 -> 3; matrix products, arithmetic and copies ran while one was open for 16% -> 14% of each run, Pallas kernels for 0% -> 0%
where the time goes in v3:
time: 145 us
  blocking collectives  40.4 us (28%)
  Pallas kernels  29.6 us (20%)
  local copies, waits for them, and re-layouts  21 us (14%)
  waiting for transfers between devices  17.2 us (12%)
  between operations  14.4 us (10%)
  other arithmetic  12.1 us (8%)
  starting transfers between devices  10.1 us (7%)
    all_gather x1, blocking collectives, per_device(): mine_all = lax.all_gather(mine, 'expert', axis=0, tiled=False)  40.4 us
    pallas_call x1, Pallas kernels, expert_kernel(): pl.pallas_call(expert_body, grid=(local_count, steps), in_specs=[piece_sp...  29.6 us
    all_to_all x1, waiting for transfers between devices, per_device(): cols = lax.all_to_all(cols, 'dp', split_axis=1, concat_axis=0, tiled=True)  9.17 us
    all_to_all x1, waiting for transfers between devices, per_device(): lax.all_to_all(send_back, ('expert', 'dp'), split_axis=0, concat_axis=0,...  6.53 us
    all_to_all x1, starting transfers between devices, per_device(): lax.all_to_all(send_back, ('expert', 'dp'), split_axis=0, concat_axis=0,...  5.4 us
    all_to_all x1, starting transfers between devices, per_device(): cols = lax.all_to_all(cols, 'dp', split_axis=1, concat_axis=0, tiled=True)  4.21 us
    unnamed x18, local copies, waits for them, and re-layouts  4.08 us
    all_gather x1, other arithmetic, per_device(): mine_all = lax.all_gather(mine, 'expert', axis=0, tiled=False)  3.41 us
  transfers between devices with their start and end apart: 6, of which 3 were waited for; matrix products, arithmetic and copies ran while one was open for 14% of the time, Pallas kernels for 0%

profile of v3, /device:TPU:0, one launch (start us, length us, event | category | flops | bytes accessed | tf_op | source)
XLA Modules:
  0.0 145.1 jit_solution(12218465347233720081)
XLA Ops:
  7.2 1.3 copy.108
  8.5 0.2 copy.110
  8.8 0.1 copy.109
  8.9 0.1 broadcast_in_dim.118
  9.1 0.9 pad_maximum_fusion
  9.9 4.2 %all-to-all-start = ((bf16[132,4,512]{2,0,1:T(8,128)(2,1)}), bf16[132,4,512]{2,0,1:T(8,128)(2,1)S(1)}, u32[]{:S(2)}, u32[]{:S(2)}) async-start(bf16[132,4,512]{2,0,1:T(8,128)(2,1)} %pad_maximum_fusion), calls=%async_computation | async-start | bytes 1114112 | tf_op jit(solution)/shard_map/all_to_all | solution.py:122
  14.2 9.2 %all-to-all-done = bf16[132,4,512]{2,0,1:T(8,128)(2,1)S(1)} async-done(((bf16[132,4,512]{2,0,1:T(8,128)(2,1)}), bf16[132,4,512]{2,0,1:T(8,128)(2,1)S(1)}, u32[]{:S(2)}, u32[]{:S(2)}) %all-to-all-start) | async-done | bytes 540704 | tf_op jit(solution)/shard_map/all_to_all | solution.py:122
  23.3 0.6 gather_fusion
  23.9 0.8 broadcast_select_fusion
  24.8 1.7 %copy.111 = bf16[8,1,4,36,768]{4,0,3,2,1:T(8,128)(2,1)} copy(bf16[8,1,4,36,768]{4,2,3,1,0:T(4,128)(2,1)S(1)} %copy-done.1) | data formatting | bytes 3538944 | tf_op jit(solution)/shard_map/optimization_barrier | solution.py:127
  26.5 0.4 collective-permute-start
  26.9 1.6 %copy.116.own_ref = bf16[8,1,4,36,768]{4,3,2,1,0:T(8,128)(2,1)} copy(bf16[8,1,4,36,768]{4,2,3,1,0:T(4,128)(2,1)S(1)} %copy-done.1) | data formatting | bytes 3538944 | tf_op args[3]
  28.5 0.2 copy.113
  28.8 40.4 %all-gather = bf16[528,1,512]{2,1,0:T(2,128)(2,1)S(1)} all-gather(bf16[132,1,512]{2,1,0:T(2,128)(2,1)S(1)} %copy.113), channel_id=2, replica_groups=mesh['groups'=2,'expert'=4,'dp'=4] {'expert'}, dimensions={0}, use_global_device_ids=true | all-gather | bytes 675840 | tf_op jit(solution)/shard_map/all_gather | solution.py:121
  69.1 3.4 %reduce = bf16[528,512]{1,0:T(8,128)(2,1)S(1)} reduce(bf16[528,1,512]{2,1,0:T(2,128)(2,1)S(1)} %all-gather, bf16[]{:T(256)} %constant.56), dimensions={1}, to_apply=%all-gather.reduce_sub_computation | reduce | bytes 1081346 | tf_op jit(solution)/shard_map/all_gather | solution.py:121
  72.6 0.1 reshape.113.mine_ref
  72.7 0.6 gather_fusion.1
  73.4 0.1 broadcast_in_dim.132
  73.6 0.1 convolution_convert_fusion.1
  73.8 3.2 %copy.117.far_ref = bf16[8,1,4,36,768]{4,3,2,1,0:T(8,128)(2,1)} copy(bf16[8,1,4,36,768]{4,0,3,2,1:T(8,128)(2,1)} %collective-permute-done) | data formatting | bytes 3538944 | tf_op jit(solution)/shard_map/ppermute | solution.py:129
  76.9 1.7 %copy.118.near_ref = bf16[8,1,4,36,768]{4,3,2,1,0:T(8,128)(2,1)} copy(bf16[8,1,4,36,768]{4,0,3,2,1:T(8,128)(2,1)S(1)} %collective-permute-done.1) | data formatting | bytes 3538944 | tf_op jit(solution)/shard_map/ppermute | solution.py:128
  78.7 1.5 %all-gather.4.cloned.1.call-done = bf16[12,132,512]{2,1,0:T(8,128)(2,1)} async-done(((bf16[3,132,512]{2,1,0:T(8,128)(2,1)}), bf16[12,132,512]{2,1,0:T(8,128)(2,1)}) %all-gather.4.cloned.1.call-update) | async-done | bytes 1622032 | tf_op jit(solution)/shard_map/all_gather | solution.py:131
  80.2 0.9 slice.31
  81.1 0.4 reshape_reshape.3
  81.5 0.2 fusion.9
  81.8 0.2 copy.127
  82.0 0.2 copy.128
  82.2 0.1 compare_reduce_fusion
  82.3 0.1 fusion.2
  82.4 0.1 convolution_convert_fusion
  82.6 1.4 select_reduce_fusion.1
  84.0 2.3 %copy.120.gate_ref = f32[16,8,48,1]{3,2,1,0:T(8,128)} copy(f32[16,8,48,1]{2,1,0,3:T(8,128)S(1)} %bitcast.40) | data formatting | bytes 49152 | tf_op jit(solution)/shard_map/broadcast_in_dim | solution.py:152
  86.3 1.9 %fusion.1.sel_ref = bf16[16,8,48,128]{3,2,1,0:T(8,128)(2,1)} fusion(s32[16,8,128]{2,1,0:T(8,128)S(1)} %convolution_convert_fusion, pred[16,8,128]{2,1,0:T(8,128)(4,1)S(1)} %bitcast.38), kind=kLoop, calls=%fused_computation.7 | loop fusion | flops 2359296 | bytes 1654784 | tf_op jit(solution)/shard_map/convert_element_type | solution.py:154
  88.2 3.1 %copy.119.near_far_ref = bf16[8,1,4,36,768]{4,3,2,1,0:T(8,128)(2,1)} copy(bf16[8,1,4,36,768]{4,0,3,2,1:T(8,128)(2,1)} %collective-permute-done.2) | data formatting | bytes 3538944 | tf_op jit(solution)/shard_map/ppermute | solution.py:130
  91.4 29.6 %shard_map.86 = (f32[8,768,512]{2,1,0:T(8,128)}, f32[8,1,768]{2,1,0:T(1,128)}) custom-call(bf16[8,1,4,36,768]{4,3,2,1,0:T(8,128)(2,1)} %copy.116.own_ref, bf16[8,1,4,36,768]{4,3,2,1,0:T(8,128)(2,1)} %copy.117.far_ref, bf16[8,1,4,36,768]{4,3,2,1,0:T(8,128)(2,1)} %copy.118.near_ref, bf16[8,1,4,36,768]{4,3,2,1,0:T(8,128)(2,1)} %copy.119.near_far_ref, ...), custom_call_target="tpu_custom_call" | custom-call | tf_op jit(solution)/shard_map/pallas_call | solution.py:73
  121.0 0.8 reduce.1
  121.8 0.1 reshape.86
  121.9 0.6 gather_fusion.2
  122.5 0.1 bitcast_select_fusion
  122.6 0.7 reshape.119
  123.3 5.4 %all-to-all-start.1 = ((f32[16,1,288]{2,1,0:T(1,128)}), f32[16,1,288]{2,1,0:T(1,128)S(1)}, u32[]{:S(2)}, u32[]{:S(2)}) async-start(f32[16,1,288]{2,1,0:T(1,128)} %reshape.119), calls=%async_computation.1 | async-start | bytes 49152 | tf_op jit(solution)/shard_map/all_to_all | solution.py:161
  128.7 6.5 %all-to-all-done.1 = f32[16,1,288]{2,1,0:T(1,128)S(1)} async-done(((f32[16,1,288]{2,1,0:T(1,128)}), f32[16,1,288]{2,1,0:T(1,128)S(1)}, u32[]{:S(2)}, u32[]{:S(2)}) %all-to-all-start.1) | async-done | bytes 18464 | tf_op jit(solution)/shard_map/all_to_all | solution.py:161
  135.3 0.5 broadcast.119
  135.8 0.7 reduce.2
  136.5 0.1 reshape.120
  136.6 0.1 copy.123
  136.7 0.8 select_reduce_fusion
  137.5 0.7 select_reduce_fusion.2
  (43 shorter events, 0.5 us)
Async XLA Ops:
  7.2 7.0 %copy-start.5 = (s32[3]{0:T(128)S(1)}, s32[3]{0:T(128)}, u32[]{:S(2)}) copy-start(s32[3]{0:T(128)} %constant.53.clone) | copy-start | bytes 40
  7.2 1.6 %copy-start.3 = (s32[128,8]{0,1:T(8,128)S(1)}, s32[128,8]{0,1:T(8,128)}, u32[]{:S(2)}) copy-start(s32[128,8]{0,1:T(8,128)} %param.9) | copy-start | bytes 12292
  7.2 1.6 %copy-start.4 = (bf16[128,8]{0,1:T(8,128)(2,1)S(1)}, bf16[128,8]{0,1:T(8,128)(2,1)}, u32[]{:S(2)}) copy-start(bf16[128,8]{0,1:T(8,128)(2,1)} %param.8) | copy-start | bytes 6148
  9.0 15.7 %copy-start.1 = (bf16[8,1,4,36,768]{4,2,3,1,0:T(4,128)(2,1)S(1)}, bf16[8,1,4,36,768]{4,2,3,1,0:T(4,128)(2,1)}, u32[]{:S(2)}) copy-start(bf16[8,1,4,36,768]{4,2,3,1,0:T(4,128)(2,1)} %param.10) | copy-start | bytes 5308420
  9.9 13.4 %all-to-all-start = ((bf16[132,4,512]{2,0,1:T(8,128)(2,1)}), bf16[132,4,512]{2,0,1:T(8,128)(2,1)S(1)}, u32[]{:S(2)}, u32[]{:S(2)}) async-start(bf16[132,4,512]{2,0,1:T(8,128)(2,1)} %pad_maximum_fusion), calls=%async_computation | async-start | bytes 1114112 | tf_op jit(solution)/shard_map/all_to_all | solution.py:122
  14.1 66.1 %all-gather.4.cloned.1.call-start = ((), (), s32[]{:S(2)}) async-start(), calls=%async_computation.2 | async-start | bytes 2088960 | tf_op jit(solution)/shard_map/all_gather | solution.py:131
  26.5 47.0 %collective-permute-start = (bf16[8,1,4,36,768]{4,0,3,2,1:T(8,128)(2,1)}, bf16[8,1,4,36,768]{4,0,3,2,1:T(8,128)(2,1)}, u32[]{:S(2)}, u32[]{:S(2)}) collective-permute-start(bf16[8,1,4,36,768]{4,0,3,2,1:T(8,128)(2,1)} %copy.111), channel_id=1, source_target_pairs={{0,2},{1,3},{2,0},{3,1},{4,6},{5,7},{6,4},{7,5},{8,10},{9,11},{10,... | collective-permute-start | bytes 5308424 | tf_op jit(solution)/shard_map/ppermute | solution.py:129
  28.7 44.0 %copy-start = (s32[4]{0:T(128)S(1)}, s32[4]{0:T(128)}, u32[]{:S(2)}) copy-start(s32[4]{0:T(128)} %constant.54.clone) | copy-start | bytes 52
  28.7 48.2 %collective-permute-start.1 = (bf16[8,1,4,36,768]{4,0,3,2,1:T(8,128)(2,1)}, bf16[8,1,4,36,768]{4,0,3,2,1:T(8,128)(2,1)S(1)}, u32[]{:S(2)}, u32[]{:S(2)}) collective-permute-start(bf16[8,1,4,36,768]{4,0,3,2,1:T(8,128)(2,1)} %copy.111), channel_id=1, source_target_pairs={{0,1},{1,0},{2,3},{3,2},{4,5},{5,4},{6,7},{7,6},{8,9},{9,8},{10,11... | collective-permute-start | bytes 5308424 | tf_op jit(solution)/shard_map/ppermute | solution.py:128
  72.7 4.3 %copy-start.2 = (bf16[4,132,512]{2,1,0:T(8,128)(2,1)}, bf16[4,132,512]{2,1,0:T(8,128)(2,1)S(1)}, u32[]{:S(2)}) copy-start(bf16[4,132,512]{2,1,0:T(8,128)(2,1)S(1)} %reshape.113.mine_ref) | copy-start | bytes 1622020
  73.5 14.7 %collective-permute-start.2 = (bf16[8,1,4,36,768]{4,0,3,2,1:T(8,128)(2,1)}, bf16[8,1,4,36,768]{4,0,3,2,1:T(8,128)(2,1)}, u32[]{:S(2)}, u32[]{:S(2)}) collective-permute-start(bf16[8,1,4,36,768]{4,0,3,2,1:T(8,128)(2,1)} %collective-permute-done), channel_id=1, source_target_pairs={{0,1},{1,0},{2,3},{3,2},{4,5},{5,4},{6,7},{7,6},{8,9},{9,8},{10,11... | collective-permute-start | bytes 5308424 | tf_op jit(solution)/shard_map/ppermute | solution.py:130
  123.3 12.0 %all-to-all-start.1 = ((f32[16,1,288]{2,1,0:T(1,128)}), f32[16,1,288]{2,1,0:T(1,128)S(1)}, u32[]{:S(2)}, u32[]{:S(2)}) async-start(f32[16,1,288]{2,1,0:T(1,128)} %reshape.119), calls=%async_computation.1 | async-start | bytes 49152 | tf_op jit(solution)/shard_map/all_to_all | solution.py:161
Sparse Core Ops, SparseCore 0:
  24.9 55.2 all-gather.3

commit v4 on v3

--- a/solution.py
+++ b/solution.py
@@ -45,13 +45,7 @@
         wg_ref[0] = wg_ref[0] + part
 
     out = jnp.dot(h, w_ref[0], preferred_element_type=jnp.float32)
-    prod = g_scr[...].astype(jnp.float32) * out
-    ones = jnp.ones((8, col_width), jnp.float32)
-    sums = lax.dot_general(
-        ones, prod, (((1,), (1,)), ((), ())),
-        precision=lax.Precision.HIGHEST, preferred_element_type=jnp.float32,
-    )
-    slot_ref[0] = sums[0:1]
+    slot_ref[0] = jnp.sum(g_scr[...].astype(jnp.float32) * out, axis=1, keepdims=True)
 
 
 def expert_kernel(pieces, mine, rest, select, gate_slot, weight):
@@ -82,11 +76,11 @@
         ],
         out_specs=[
             pl.BlockSpec((1, hidden_width, col_width), lambda l, r: (l, 0, 0)),
-            pl.BlockSpec((1, 1, rows), lambda l, r: (l, 0, r)),
+            pl.BlockSpec((1, rows, 1), lambda l, r: (l, r, 0)),
         ],
         out_shape=[
             jax.ShapeDtypeStruct((local_count, hidden_width, col_width), jnp.float32),
-            jax.ShapeDtypeStruct((local_count, 1, block_count * padded), jnp.float32),
+            jax.ShapeDtypeStruct((local_count, block_count * padded, 1), jnp.float32),
         ],
         scratch_shapes=[
             pltpu.VMEM((rows, hidden_width), jnp.bfloat16),
@@ -117,8 +111,19 @@
     meta = jnp.pad(meta, (0, meta_rows * col_width - meta_len)).reshape(meta_rows, 1, col_width)
     cols = out_grad.reshape(tok_rows, shards, col_width)
     cols = jnp.concatenate([cols, jnp.broadcast_to(meta, (meta_rows, shards, col_width))], axis=0)
-    mine = lax.dynamic_index_in_dim(cols, my_dp, axis=1, keepdims=False)
-    mine_all = lax.all_gather(mine, "expert", axis=0, tiled=False)
+    mine = lax.dynamic_slice_in_dim(out_grad, my_dp * col_width, col_width, axis=1)
+    mine = jnp.concatenate([mine, meta[:, 0, :]], axis=0)[:, None, :]
+    if peer_count <= 8:
+        recv = [mine] + [
+            lax.ppermute(mine, "expert", [(j, (j + k) % peer_count) for j in range(peer_count)])
+            for k in range(1, peer_count)
+        ]
+        order = (lax.axis_index("expert") - jnp.arange(peer_count, dtype=jnp.int32)) % peer_count
+        mine_all = jnp.take(jnp.stack(recv), order, axis=0)
+    else:
+        mine_all = lax.all_gather(mine, "expert", axis=0, tiled=False)
+    mine_all = mine_all.reshape(peer_count, tok_rows + meta_rows, col_width)
+    cols, mine_all = lax.optimization_barrier((cols, mine_all))
     cols = lax.all_to_all(cols, "dp", split_axis=1, concat_axis=0, tiled=True)
     cols = cols.reshape(shards, tok_rows + meta_rows, col_width)
     piece_xor = jnp.array([2, 1, 3], jnp.int32)

time: 145 us -> 145 us (level)
  waiting for transfers between devices: 17.2 us -> 58.7 us
  blocking collectives: 40.4 us -> 0 us
  Pallas kernels: 29.6 us -> 18.2 us
  starting transfers between devices: 10.1 us -> 17.1 us
  local copies, waits for them, and re-layouts: 21 us -> 23.5 us
    all_gather x1 -> x0, blocking collectives: 40.4 us -> none  [per_device(): mine_all = lax.all_gather(mine, 'expert', axis=0, tiled=False)]
    ppermute x1, waiting for transfers between devices: 0.01 us -> 37.7 us  [per_device(): far = lax.ppermute(hidden_sent, 'dp', [(j, j ^ 2) for j in range(shards)])]
    pallas_call x1, Pallas kernels: 29.6 us -> 18.2 us  [expert_kernel(): pl.pallas_call(expert_body, grid=(local_count, steps), in_specs=[piece_sp...]
    ppermute x0 -> x3, starting transfers between devices: none -> 7.01 us  [per_device(): lax.ppermute(mine, 'expert', [(j, (j + k) % peer_count) for j in range(pe...]
    ppermute x0 -> x3, waiting for transfers between devices: none -> 5.36 us  [per_device(): lax.ppermute(mine, 'expert', [(j, (j + k) % peer_count) for j in range(pe...]
    all_gather x1 -> x0, other arithmetic: 3.41 us -> none  [per_device(): mine_all = lax.all_gather(mine, 'expert', axis=0, tiled=False)]
    pallas_call x1, other arithmetic: 0.79 us -> 2.77 us  [expert_kernel(): pl.pallas_call(expert_body, grid=(local_count, steps), in_specs=[piece_sp...]
    all_gather x1, waiting for transfers between devices: 1.52 us -> 0.01 us  [per_device(): rest_all = lax.all_gather(cols, 'expert', axis=0, tiled=False)]
  transfers between devices with their start and end apart: 6 -> 9, of which waited for: 3 -> 5; matrix products, arithmetic and copies ran while one was open for 14% -> 15% of each run, Pallas kernels for 0% -> 0%
where the time goes in v4:
time: 145 us; the launch traced here: 144 us
  waiting for transfers between devices  58.7 us (40%)
  local copies, waits for them, and re-layouts  23.5 us (16%)
  Pallas kernels  18.2 us (13%)
  starting transfers between devices  17.1 us (12%)
  between operations  14.4 us (10%)
  other arithmetic  12.3 us (8%)
    ppermute x1, waiting for transfers between devices, per_device(): far = lax.ppermute(hidden_sent, 'dp', [(j, j ^ 2) for j in range(shards)])  37.7 us
    pallas_call x1, Pallas kernels, expert_kernel(): pl.pallas_call(expert_body, grid=(local_count, steps), in_specs=[piece_sp...  18.2 us
    all_to_all x1, waiting for transfers between devices, per_device(): cols = lax.all_to_all(cols, 'dp', split_axis=1, concat_axis=0, tiled=True)  9.07 us
    ppermute x3, starting transfers between devices, per_device(): lax.ppermute(mine, 'expert', [(j, (j + k) % peer_count) for j in range(pe...  7.01 us
    all_to_all x1, waiting for transfers between devices, per_device(): lax.all_to_all(send_back, ('expert', 'dp'), split_axis=0, concat_axis=0,...  6.53 us
    all_to_all x1, starting transfers between devices, per_device(): lax.all_to_all(send_back, ('expert', 'dp'), split_axis=0, concat_axis=0,...  6.07 us
    ppermute x3, waiting for transfers between devices, per_device(): lax.ppermute(mine, 'expert', [(j, (j + k) % peer_count) for j in range(pe...  5.36 us
    unnamed x16, local copies, waits for them, and re-layouts  4.01 us
  transfers between devices with their start and end apart: 9, of which 5 were waited for; matrix products, arithmetic and copies ran while one was open for 15% of the time, Pallas kernels for 0%

profile of v4, /device:TPU:0, one launch (start us, length us, event | category | flops | bytes accessed | tf_op | source)
XLA Modules:
  0.0 144.5 jit_solution(12280383420950202611)
XLA Ops:
  7.2 0.7 convert_element_type.22
  7.9 0.7 pad_maximum_fusion.3
  8.5 0.1 copy.79
  8.8 0.9 constant_dynamic-slice_fusion
  9.7 3.1 %collective-permute-start = (bf16[132,1,512]{2,0,1:T(8,128)(2,1)S(1)}, bf16[132,1,512]{2,0,1:T(8,128)(2,1)S(1)}, u32[]{:S(2)}, u32[]{:S(2)}) collective-permute-start(bf16[132,1,512]{2,0,1:T(8,128)(2,1)S(1)} %get-tuple-element.19), channel_id=1, source_target_pairs={{0,4},{4,8},{8,12},{12,0},{1,5},{5,9},{9,13},{13,1},{2,6},{6,10},{... | collective-permute-start | bytes 405512 | tf_op jit(solution)/shard_map/ppermute | solution.py:118
  12.8 2.6 %collective-permute-start.1 = (bf16[132,1,512]{2,0,1:T(8,128)(2,1)S(1)}, bf16[132,1,512]{2,0,1:T(8,128)(2,1)S(1)}, u32[]{:S(2)}, u32[]{:S(2)}) collective-permute-start(bf16[132,1,512]{2,0,1:T(8,128)(2,1)S(1)} %get-tuple-element.19), channel_id=1, source_target_pairs={{0,8},{4,12},{8,0},{12,4},{1,9},{5,13},{9,1},{13,5},{2,10},{6,14},... | collective-permute-start | bytes 405512 | tf_op jit(solution)/shard_map/ppermute | solution.py:118
  15.4 1.3 collective-permute-start.2
  16.8 1.3 copy.78
  18.1 0.2 copy.80
  18.3 0.9 pad_maximum_fusion
  19.2 0.2 collective-permute-done
  19.4 5.1 %collective-permute-done.1 = bf16[132,1,512]{2,0,1:T(8,128)(2,1)S(1)} collective-permute-done((bf16[132,1,512]{2,0,1:T(8,128)(2,1)S(1)}, bf16[132,1,512]{2,0,1:T(8,128)(2,1)S(1)}, u32[]{:S(2)}, u32[]{:S(2)}) %collective-permute-start.1) | collective-permute-done | bytes 135200 | tf_op jit(solution)/shard_map/ppermute | solution.py:118
  24.7 0.6 gather_fusion
  25.3 0.1 broadcast_select_fusion.mine_ref
  25.4 3.6 %all-to-all-start = ((bf16[132,4,512]{2,0,1:T(8,128)(2,1)}), bf16[132,4,512]{2,0,1:T(8,128)(2,1)S(1)}, u32[]{:S(2)}, u32[]{:S(2)}) async-start(bf16[132,4,512]{2,0,1:T(8,128)(2,1)} %pad_maximum_fusion), calls=%async_computation | async-start | bytes 1114112 | tf_op jit(solution)/shard_map/all_to_all | solution.py:127
  29.1 9.1 %all-to-all-done = bf16[132,4,512]{2,0,1:T(8,128)(2,1)S(1)} async-done(((bf16[132,4,512]{2,0,1:T(8,128)(2,1)}), bf16[132,4,512]{2,0,1:T(8,128)(2,1)S(1)}, u32[]{:S(2)}, u32[]{:S(2)}) %all-to-all-start) | async-done | bytes 540704 | tf_op jit(solution)/shard_map/all_to_all | solution.py:127
  38.2 0.6 gather_fusion.1
  38.8 0.9 broadcast_select_fusion.1
  39.7 1.7 %copy.81 = bf16[8,1,4,36,768]{4,0,3,2,1:T(8,128)(2,1)} copy(bf16[8,1,4,36,768]{4,2,3,1,0:T(4,128)(2,1)S(1)} %copy-done.1) | data formatting | bytes 3538944 | tf_op jit(solution)/shard_map/optimization_barrier | solution.py:132
  41.5 0.4 collective-permute-start.3
  41.8 1.5 %copy.85.own_ref = bf16[8,1,4,36,768]{4,3,2,1,0:T(8,128)(2,1)} copy(bf16[8,1,4,36,768]{4,2,3,1,0:T(4,128)(2,1)S(1)} %copy-done.1) | data formatting | bytes 3538944 | tf_op args[3]
  43.4 0.6 gather_fusion.2
  44.2 37.7 %collective-permute-done.3 = bf16[8,1,4,36,768]{4,0,3,2,1:T(8,128)(2,1)} collective-permute-done((bf16[8,1,4,36,768]{4,0,3,2,1:T(8,128)(2,1)}, bf16[8,1,4,36,768]{4,0,3,2,1:T(8,128)(2,1)}, u32[]{:S(2)}, u32[]{:S(2)}) %collective-permute-start.3) | collective-permute-done | bytes 1769504 | tf_op jit(solution)/shard_map/ppermute | solution.py:134
  81.9 0.1 convolution_convert_fusion.1
  82.1 3.1 %copy.86.far_ref = bf16[8,1,4,36,768]{4,3,2,1,0:T(8,128)(2,1)} copy(bf16[8,1,4,36,768]{4,0,3,2,1:T(8,128)(2,1)} %collective-permute-done.3) | data formatting | bytes 3538944 | tf_op jit(solution)/shard_map/ppermute | solution.py:134
  85.2 3.1 %copy.87.near_ref = bf16[8,1,4,36,768]{4,3,2,1,0:T(8,128)(2,1)} copy(bf16[8,1,4,36,768]{4,0,3,2,1:T(8,128)(2,1)} %collective-permute-done.4) | data formatting | bytes 3538944 | tf_op jit(solution)/shard_map/ppermute | solution.py:133
  88.3 0.9 slice.32
  89.3 0.4 reshape_reshape.3
  89.7 0.2 fusion.13
  89.9 0.2 copy.95
  90.1 0.2 copy.96
  90.3 0.1 compare_reduce_fusion
  90.5 0.1 fusion.2
  90.6 0.1 convolution_convert_fusion
  90.7 1.4 select_reduce_fusion.1
  92.2 2.3 %copy.89.gate_ref = f32[16,8,48,1]{3,2,1,0:T(8,128)} copy(f32[16,8,48,1]{2,1,0,3:T(8,128)S(1)} %bitcast.51) | data formatting | bytes 49152 | tf_op jit(solution)/shard_map/broadcast_in_dim | solution.py:157
  94.5 1.9 %fusion.1.sel_ref = bf16[16,8,48,128]{3,2,1,0:T(8,128)(2,1)} fusion(s32[16,8,128]{2,1,0:T(8,128)S(1)} %convolution_convert_fusion, pred[16,8,128]{2,1,0:T(8,128)(4,1)S(1)} %bitcast.49), kind=kLoop, calls=%fused_computation.8 | loop fusion | flops 2359296 | bytes 1654784 | tf_op jit(solution)/shard_map/convert_element_type | solution.py:159
  96.4 3.1 %copy.88.near_far_ref = bf16[8,1,4,36,768]{4,3,2,1,0:T(8,128)(2,1)} copy(bf16[8,1,4,36,768]{4,0,3,2,1:T(8,128)(2,1)} %collective-permute-done.5) | data formatting | bytes 3538944 | tf_op jit(solution)/shard_map/ppermute | solution.py:135
  99.5 18.2 %shard_map.86 = (f32[8,768,512]{2,1,0:T(8,128)}, f32[8,768,1]{2,1,0:T(8,128)}) custom-call(bf16[8,1,4,36,768]{4,3,2,1,0:T(8,128)(2,1)} %copy.85.own_ref, bf16[8,1,4,36,768]{4,3,2,1,0:T(8,128)(2,1)} %copy.86.far_ref, bf16[8,1,4,36,768]{4,3,2,1,0:T(8,128)(2,1)} %copy.87.near_ref, bf16[8,1,4,36,768]{4,3,2,1,0:T(8,128)(2,1)} %copy.88.near_far_ref, ...), custom_call_target="tpu_custom_call" | custom-call | tf_op jit(solution)/shard_map/pallas_call | solution.py:67
  117.8 2.8 %reduce = f32[8,768]{1,0:T(8,128)S(1)} reduce(f32[8,768,1]{2,1,0:T(8,128)} %get-tuple-element.13, f32[]{:T(128)} %constant.82), dimensions={2}, to_apply=%get-tuple-element.13.reduce_sub_computation | reduce | bytes 49156 | tf_op jit(solution)/shard_map/pallas_call | solution.py:67
  120.7 0.6 gather_fusion.3
  121.3 0.7 reshape.186
  122.0 6.1 %all-to-all-start.1 = ((f32[16,1,288]{2,1,0:T(1,128)}), f32[16,1,288]{2,1,0:T(1,128)S(1)}, u32[]{:S(2)}, u32[]{:S(2)}) async-start(f32[16,1,288]{2,1,0:T(1,128)} %reshape.186), calls=%async_computation.1 | async-start | bytes 49152 | tf_op jit(solution)/shard_map/all_to_all | solution.py:166
  128.2 6.5 %all-to-all-done.1 = f32[16,1,288]{2,1,0:T(1,128)S(1)} async-done(((f32[16,1,288]{2,1,0:T(1,128)}), f32[16,1,288]{2,1,0:T(1,128)S(1)}, u32[]{:S(2)}, u32[]{:S(2)}) %all-to-all-start.1) | async-done | bytes 18464 | tf_op jit(solution)/shard_map/all_to_all | solution.py:166
  134.7 0.5 broadcast.210
  135.2 0.7 reduce.1
  136.1 0.8 select_reduce_fusion
  137.0 0.7 select_reduce_fusion.2
  (50 shorter events, 1.0 us)
Async XLA Ops:
  9.7 9.7 %collective-permute-start = (bf16[132,1,512]{2,0,1:T(8,128)(2,1)S(1)}, bf16[132,1,512]{2,0,1:T(8,128)(2,1)S(1)}, u32[]{:S(2)}, u32[]{:S(2)}) collective-permute-start(bf16[132,1,512]{2,0,1:T(8,128)(2,1)S(1)} %get-tuple-element.19), channel_id=1, source_target_pairs={{0,4},{4,8},{8,12},{12,0},{1,5},{5,9},{9,13},{13,1},{2,6},{6,10},{... | collective-permute-start | bytes 405512 | tf_op jit(solution)/shard_map/ppermute | solution.py:118
  12.8 11.8 %collective-permute-start.1 = (bf16[132,1,512]{2,0,1:T(8,128)(2,1)S(1)}, bf16[132,1,512]{2,0,1:T(8,128)(2,1)S(1)}, u32[]{:S(2)}, u32[]{:S(2)}) collective-permute-start(bf16[132,1,512]{2,0,1:T(8,128)(2,1)S(1)} %get-tuple-element.19), channel_id=1, source_target_pairs={{0,8},{4,12},{8,0},{12,4},{1,9},{5,13},{9,1},{13,5},{2,10},{6,14},... | collective-permute-start | bytes 405512 | tf_op jit(solution)/shard_map/ppermute | solution.py:118
  15.4 9.2 %collective-permute-start.2 = (bf16[132,1,512]{2,0,1:T(8,128)(2,1)S(1)}, bf16[132,1,512]{2,0,1:T(8,128)(2,1)S(1)}, u32[]{:S(2)}, u32[]{:S(2)}) collective-permute-start(bf16[132,1,512]{2,0,1:T(8,128)(2,1)S(1)} %get-tuple-element.19), channel_id=1, source_target_pairs={{0,12},{4,0},{8,4},{12,8},{1,13},{5,1},{9,5},{13,9},{2,14},{6,2},{... | collective-permute-start | bytes 405512 | tf_op jit(solution)/shard_map/ppermute | solution.py:118
  24.6 4.5 %copy-start.4 = (s32[3]{0:T(128)S(1)}, s32[3]{0:T(128)}, u32[]{:S(2)}) copy-start(s32[3]{0:T(128)} %constant.79.clone) | copy-start | bytes 40
  25.2 14.4 %copy-start.1 = (bf16[8,1,4,36,768]{4,2,3,1,0:T(4,128)(2,1)S(1)}, bf16[8,1,4,36,768]{4,2,3,1,0:T(4,128)(2,1)}, u32[]{:S(2)}) copy-start(bf16[8,1,4,36,768]{4,2,3,1,0:T(4,128)(2,1)} %param.10) | copy-start | bytes 5308420
  25.4 56.7 %copy-start.2 = (bf16[4,132,512]{2,1,0:T(8,128)(2,1)}, bf16[4,132,512]{2,1,0:T(8,128)(2,1)S(1)}, u32[]{:S(2)}) copy-start(bf16[4,132,512]{2,1,0:T(8,128)(2,1)S(1)} %broadcast_select_fusion.mine_ref) | copy-start | bytes 1622020
  25.4 12.8 %all-to-all-start = ((bf16[132,4,512]{2,0,1:T(8,128)(2,1)}), bf16[132,4,512]{2,0,1:T(8,128)(2,1)S(1)}, u32[]{:S(2)}, u32[]{:S(2)}) async-start(bf16[132,4,512]{2,0,1:T(8,128)(2,1)} %pad_maximum_fusion), calls=%async_computation | async-start | bytes 1114112 | tf_op jit(solution)/shard_map/all_to_all | solution.py:127
  29.0 59.3 %all-gather.3.cloned.1.call-start = ((), (), s32[]{:S(2)}) async-start(), calls=%async_computation.2 | async-start | bytes 2088960 | tf_op jit(solution)/shard_map/all_gather | solution.py:136
  41.4 1.9 %copy-start = (s32[4]{0:T(128)S(1)}, s32[4]{0:T(128)}, u32[]{:S(2)}) copy-start(s32[4]{0:T(128)} %constant.80.clone) | copy-start | bytes 52
  41.5 2.7 %copy-start.3 = (s32[128,8]{0,1:T(8,128)S(1)}, s32[128,8]{0,1:T(8,128)}, u32[]{:S(2)}) copy-start(s32[128,8]{0,1:T(8,128)} %param.9) | copy-start | bytes 12292
  41.5 40.5 %collective-permute-start.3 = (bf16[8,1,4,36,768]{4,0,3,2,1:T(8,128)(2,1)}, bf16[8,1,4,36,768]{4,0,3,2,1:T(8,128)(2,1)}, u32[]{:S(2)}, u32[]{:S(2)}) collective-permute-start(bf16[8,1,4,36,768]{4,0,3,2,1:T(8,128)(2,1)} %copy.81), channel_id=1, source_target_pairs={{0,2},{1,3},{2,0},{3,1},{4,6},{5,7},{6,4},{7,5},{8,10},{9,11},{10,... | collective-permute-start | bytes 5308424 | tf_op jit(solution)/shard_map/ppermute | solution.py:134
  41.8 43.4 %collective-permute-start.4 = (bf16[8,1,4,36,768]{4,0,3,2,1:T(8,128)(2,1)}, bf16[8,1,4,36,768]{4,0,3,2,1:T(8,128)(2,1)}, u32[]{:S(2)}, u32[]{:S(2)}) collective-permute-start(bf16[8,1,4,36,768]{4,0,3,2,1:T(8,128)(2,1)} %copy.81), channel_id=1, source_target_pairs={{0,1},{1,0},{2,3},{3,2},{4,5},{5,4},{6,7},{7,6},{8,9},{9,8},{10,11... | collective-permute-start | bytes 5308424 | tf_op jit(solution)/shard_map/ppermute | solution.py:133
  81.9 14.5 %collective-permute-start.5 = (bf16[8,1,4,36,768]{4,0,3,2,1:T(8,128)(2,1)}, bf16[8,1,4,36,768]{4,0,3,2,1:T(8,128)(2,1)}, u32[]{:S(2)}, u32[]{:S(2)}) collective-permute-start(bf16[8,1,4,36,768]{4,0,3,2,1:T(8,128)(2,1)} %collective-permute-done.3), channel_id=1, source_target_pairs={{0,1},{1,0},{2,3},{3,2},{4,5},{5,4},{6,7},{7,6},{8,9},{9,8},{10,11... | collective-permute-start | bytes 5308424 | tf_op jit(solution)/shard_map/ppermute | solution.py:135
  122.0 12.6 %all-to-all-start.1 = ((f32[16,1,288]{2,1,0:T(1,128)}), f32[16,1,288]{2,1,0:T(1,128)S(1)}, u32[]{:S(2)}, u32[]{:S(2)}) async-start(f32[16,1,288]{2,1,0:T(1,128)} %reshape.186), calls=%async_computation.1 | async-start | bytes 49152 | tf_op jit(solution)/shard_map/all_to_all | solution.py:166
Sparse Core Ops, SparseCore 0:
  39.8 39.9 all-gather.2

commit v5 on v2

--- a/solution.py
+++ b/solution.py
@@ -25,9 +25,11 @@
             h_scr[row:row + capacity, :] = ref[0, 0, src]
 
     for blk in range(blocks):
-        rows = jnp.dot(sel_ref[blk, 0], tok_ref[blk], preferred_element_type=jnp.float32)
+        sel = sel_ref[blk, 0]
+        rows = jnp.dot(sel, tok_ref[blk], preferred_element_type=jnp.float32)
+        gate = jnp.sum(sel.astype(jnp.float32) * gate_ref[blk, 0], axis=1, keepdims=True)
         g_scr[blk * padded:(blk + 1) * padded, :] = rows.astype(jnp.bfloat16)
-        s_scr[blk * padded:(blk + 1) * padded, :] = (gate_ref[blk, 0] * rows).astype(jnp.bfloat16)
+        s_scr[blk * padded:(blk + 1) * padded, :] = (gate * rows).astype(jnp.bfloat16)
 
     h = h_scr[...]
     part = lax.dot_general(
@@ -46,10 +48,10 @@
     slot_ref[0] = jnp.sum(g_scr[...].astype(jnp.float32) * out, axis=1, keepdims=True)
 
 
-def expert_kernel(pieces, tokens, select, gate_slot, weight):
+def expert_kernel(pieces, tokens, select, gate_row, weight):
     local_count, _, source_count, capacity, hidden_width = pieces[0].shape
-    block_count, tok_rows, col_width = tokens.shape
-    padded = select.shape[2]
+    col_width = tokens.shape[2]
+    block_count, _, padded, tok_rows = select.shape
     per_source = block_count // source_count
     chunk = source_count
     for size in (4, 2, 1):
@@ -68,7 +70,7 @@
         in_specs=[piece_spec] * len(pieces) + [
             pl.BlockSpec((blocks, tok_rows, col_width), lambda l, r: (r, 0, 0)),
             pl.BlockSpec((blocks, 1, padded, tok_rows), lambda l, r: (r, l, 0, 0)),
-            pl.BlockSpec((blocks, 1, padded, 1), lambda l, r: (r, l, 0, 0)),
+            pl.BlockSpec((blocks, 1, 1, tok_rows), lambda l, r: (r, l, 0, 0)),
             pl.BlockSpec((1, hidden_width, col_width), lambda l, r: (l, 0, 0)),
         ],
         out_specs=[
@@ -84,7 +86,7 @@
             pltpu.VMEM((rows, col_width), jnp.bfloat16),
             pltpu.VMEM((rows, col_width), jnp.bfloat16),
         ],
-    )(*pieces, tokens, select, gate_slot, weight)
+    )(*pieces, tokens, select, gate_row, weight)
 
 
 def per_device(out_grad, gate_weights, expert_ids, hidden, down_weight):
@@ -139,9 +141,9 @@
     rank_t = rank.transpose(0, 2, 1)
     gate_t = gate_hit.transpose(0, 2, 1)
     select = chose_t[:, :, None, :] & (rank_t[:, :, None, :] == slot_ids[None, None, :, None])
-    gate_slot = jnp.sum(jnp.where(select, gate_t[:, :, None, :], 0.0), axis=3, keepdims=True)
+    gate_row = gate_t[:, :, None, :]
     weight_grad, slot_part = expert_kernel(
-        (hidden, far, near, near_far), grad_all, select.astype(bf16), gate_slot, down_weight
+        (hidden, far, near, near_far), got, select.astype(bf16), gate_row, down_weight
     )
     slot_part = slot_part.reshape(local_count, block_count, padded)[:, :, :capacity]
     slot_part = slot_part.transpose(1, 0, 2).reshape(peer_count, shards, local_count, capacity)

time: 131 us -> 125 us (0.954)
  local copies, waits for them, and re-layouts: 22.7 us -> 18.4 us
  waiting for transfers between devices: 54.1 us -> 55.7 us
  other arithmetic: 11.2 us -> 9.81 us
    broadcast_in_dim x1 -> x0, local copies, waits for them, and re-layouts: 2.29 us -> none  [per_device(): jnp.sum(jnp.where(select, gate_t[:, :, None, :], 0.0), axis=3, keepdims=T...]
    slice x1 -> x0, local copies, waits for them, and re-layouts: 1.57 us -> none  [per_device(): grad_all = got[:, :tok_rows]]
    ppermute x1, local copies, waits for them, and re-layouts: 1.65 us -> 3.09 us  [per_device(): near = lax.ppermute(hidden_sent, 'dp', [(j, j ^ 1) for j in range(shards)])]
    reduce_sum x1 -> x0, other arithmetic: 1.44 us -> none  [per_device(): jnp.sum(jnp.where(select, gate_t[:, :, None, :], 0.0), axis=3, keepdims=T...]
    ppermute x1, local copies, waits for them, and re-layouts: 3.09 us -> 1.7 us  [per_device(): far = lax.ppermute(hidden_sent, 'dp', [(j, j ^ 2) for j in range(shards)])]
    unnamed x22 -> x14, local copies, waits for them, and re-layouts: 4.12 us -> 4.11 us
  transfers between devices with their start and end apart: 6 -> 6, of which waited for: 4 -> 4; matrix products, arithmetic and copies ran while one was open for 16% -> 11% of each run, Pallas kernels for 0% -> 0%
where the time goes in v5:
time: 125 us
  waiting for transfers between devices  55.7 us (45%)
  local copies, waits for them, and re-layouts  18.4 us (15%)
  Pallas kernels  18 us (14%)
  between operations  14.3 us (11%)
  other arithmetic  9.81 us (8%)
  starting transfers between devices  8.24 us (7%)
    ppermute x1, waiting for transfers between devices, per_device(): far = lax.ppermute(hidden_sent, 'dp', [(j, j ^ 2) for j in range(shards)])  37.4 us
    pallas_call x1, Pallas kernels, expert_kernel(): pl.pallas_call(expert_body, grid=(local_count, steps), in_specs=[piece_sp...  18 us
    all_to_all x1, waiting for transfers between devices, per_device(): cols = lax.all_to_all(cols, 'dp', split_axis=1, concat_axis=0, tiled=True)  9.17 us
    all_to_all x1, waiting for transfers between devices, per_device(): lax.all_to_all(send_back, ('expert', 'dp'), split_axis=0, concat_axis=0,...  6.53 us
    all_to_all x1, starting transfers between devices, per_device(): cols = lax.all_to_all(cols, 'dp', split_axis=1, concat_axis=0, tiled=True)  4.34 us
    unnamed x14, local copies, waits for them, and re-layouts  4.11 us
    all_to_all x1, starting transfers between devices, per_device(): lax.all_to_all(send_back, ('expert', 'dp'), split_axis=0, concat_axis=0,...  3.53 us
    ppermute x1, local copies, waits for them, and re-layouts, per_device(): near_far = lax.ppermute(far, 'dp', [(j, j ^ 1) for j in range(shards)])  3.16 us
  transfers between devices with their start and end apart: 6, of which 4 were waited for; matrix products, arithmetic and copies ran while one was open for 11% of the time, Pallas kernels for 0%

profile of v5, /device:TPU:0, one launch (start us, length us, event | category | flops | bytes accessed | tf_op | source)
XLA Modules:
  0.0 124.7 jit_solution(11976605782857053108)
XLA Ops:
  7.2 0.0 copy-start
  7.2 1.3 %copy.73 = bf16[128,2048]{0,1:T(8,128)(2,1)S(1)} copy(bf16[128,2048]{1,0:T(8,128)(2,1)} %param.7) | data formatting | bytes 1048576 | tf_op args[0]
  8.5 0.2 copy.75
  8.8 0.1 copy.74
  8.9 0.1 broadcast_in_dim.102
  9.1 0.9 pad_maximum_fusion
  9.9 4.3 %all-to-all-start = ((bf16[132,4,512]{2,0,1:T(8,128)(2,1)}), bf16[132,4,512]{2,0,1:T(8,128)(2,1)S(1)}, u32[]{:S(2)}, u32[]{:S(2)}) async-start(bf16[132,4,512]{2,0,1:T(8,128)(2,1)} %pad_maximum_fusion), calls=%async_computation | async-start | bytes 1114112 | tf_op jit(solution)/shard_map/all_to_all | solution.py:113
  14.3 9.2 %all-to-all-done = bf16[132,4,512]{2,0,1:T(8,128)(2,1)S(1)} async-done(((bf16[132,4,512]{2,0,1:T(8,128)(2,1)}), bf16[132,4,512]{2,0,1:T(8,128)(2,1)S(1)}, u32[]{:S(2)}, u32[]{:S(2)}) %all-to-all-start) | async-done | bytes 540704 | tf_op jit(solution)/shard_map/all_to_all | solution.py:113
  23.5 0.6 gather_fusion
  24.1 0.9 broadcast_select_fusion
  25.0 0.0 all-gather.3.cloned.1.call-update
  25.0 1.7 %copy.76 = bf16[8,1,4,36,768]{4,0,3,2,1:T(8,128)(2,1)} copy(bf16[8,1,4,36,768]{4,2,3,1,0:T(4,128)(2,1)S(1)} %copy-done.1) | data formatting | bytes 3538944 | tf_op jit(solution)/shard_map/optimization_barrier | solution.py:118
  26.8 0.4 collective-permute-start
  27.1 1.6 %copy.80.own_ref = bf16[8,1,4,36,768]{4,3,2,1,0:T(8,128)(2,1)} copy(bf16[8,1,4,36,768]{4,2,3,1,0:T(4,128)(2,1)S(1)} %copy-done.1) | data formatting | bytes 3538944 | tf_op args[3]
  28.7 0.6 gather_fusion.1
  29.4 0.1 broadcast_in_dim.113
  29.5 37.4 %collective-permute-done = bf16[8,1,4,36,768]{4,0,3,2,1:T(8,128)(2,1)S(1)} collective-permute-done((bf16[8,1,4,36,768]{4,0,3,2,1:T(8,128)(2,1)}, bf16[8,1,4,36,768]{4,0,3,2,1:T(8,128)(2,1)S(1)}, u32[]{:S(2)}, u32[]{:S(2)}) %collective-permute-start) | collective-permute-done | bytes 1769504 | tf_op jit(solution)/shard_map/ppermute | solution.py:120
  66.9 0.0 collective-permute-start.2
  67.0 0.1 convolution_convert_fusion.1
  67.1 1.7 %copy.81.far_ref = bf16[8,1,4,36,768]{4,3,2,1,0:T(8,128)(2,1)} copy(bf16[8,1,4,36,768]{4,0,3,2,1:T(8,128)(2,1)S(1)} %collective-permute-done) | data formatting | bytes 3538944 | tf_op jit(solution)/shard_map/ppermute | solution.py:120
  68.8 0.0 collective-permute-done.1
  68.8 3.1 %copy.82.near_ref = bf16[8,1,4,36,768]{4,3,2,1,0:T(8,128)(2,1)} copy(bf16[8,1,4,36,768]{4,0,3,2,1:T(8,128)(2,1)} %collective-permute-done.1) | data formatting | bytes 3538944 | tf_op jit(solution)/shard_map/ppermute | solution.py:119
  71.9 2.6 %all-gather.3.cloned.1.call-done.tok_ref = bf16[16,132,512]{2,1,0:T(8,128)(2,1)} async-done(((bf16[4,132,512]{2,1,0:T(8,128)(2,1)}), bf16[16,132,512]{2,1,0:T(8,128)(2,1)}) %all-gather.3.cloned.1.call-update) | async-done | bytes 2162704 | tf_op jit(solution)/shard_map/all_gather | solution.py:122
  74.5 0.9 slice.26
  75.4 0.4 reshape_reshape.3
  75.8 0.2 fusion.8
  76.0 0.2 copy.89
  76.2 0.2 copy.90
  76.4 0.1 compare_reduce_fusion
  76.6 0.8 fusion.2
  77.3 0.1 convolution_convert_fusion
  77.5 1.9 %fusion.1.sel_ref = bf16[16,8,48,128]{3,2,1,0:T(8,128)(2,1)} fusion(s32[16,8,128]{2,1,0:T(8,128)S(1)} %convolution_convert_fusion, pred[16,8,128]{2,1,0:T(8,128)(4,1)S(1)} %bitcast.36), kind=kLoop, calls=%fused_computation.6 | loop fusion | flops 2359296 | bytes 1654784 | tf_op jit(solution)/shard_map/convert_element_type | solution.py:146
  79.4 0.0 collective-permute-done.2
  79.4 3.2 %copy.83.near_far_ref = bf16[8,1,4,36,768]{4,3,2,1,0:T(8,128)(2,1)} copy(bf16[8,1,4,36,768]{4,0,3,2,1:T(8,128)(2,1)} %collective-permute-done.2) | data formatting | bytes 3538944 | tf_op jit(solution)/shard_map/ppermute | solution.py:121
  82.6 18.0 %shard_map.86 = (f32[8,768,512]{2,1,0:T(8,128)}, f32[8,768,1]{2,1,0:T(8,128)}) custom-call(bf16[8,1,4,36,768]{4,3,2,1,0:T(8,128)(2,1)} %copy.80.own_ref, bf16[8,1,4,36,768]{4,3,2,1,0:T(8,128)(2,1)} %copy.81.far_ref, bf16[8,1,4,36,768]{4,3,2,1,0:T(8,128)(2,1)} %copy.82.near_ref, bf16[8,1,4,36,768]{4,3,2,1,0:T(8,128)(2,1)} %copy.83.near_far_ref, ...), custom_call_target="tpu_custom_call" | custom-call | tf_op jit(solution)/shard_map/pallas_call | solution.py:67
  100.5 2.8 %reduce = f32[8,768]{1,0:T(8,128)S(1)} reduce(f32[8,768,1]{2,1,0:T(8,128)} %get-tuple-element.9, f32[]{:T(128)} %constant.49), dimensions={2}, to_apply=%get-tuple-element.9.reduce_sub_computation | reduce | bytes 49156 | tf_op jit(solution)/shard_map/pallas_call | solution.py:67
  103.3 0.1 reshape.88
  103.5 0.6 gather_fusion.2
  104.0 0.1 bitcast_select_fusion
  104.1 0.7 reshape.120
  104.8 3.5 %all-to-all-start.1 = ((f32[16,1,288]{2,1,0:T(1,128)}), f32[16,1,288]{2,1,0:T(1,128)S(1)}, u32[]{:S(2)}, u32[]{:S(2)}) async-start(f32[16,1,288]{2,1,0:T(1,128)} %reshape.120), calls=%async_computation.1 | async-start | bytes 49152 | tf_op jit(solution)/shard_map/all_to_all | solution.py:153
  108.4 6.5 %all-to-all-done.1 = f32[16,1,288]{2,1,0:T(1,128)S(1)} async-done(((f32[16,1,288]{2,1,0:T(1,128)}), f32[16,1,288]{2,1,0:T(1,128)S(1)}, u32[]{:S(2)}, u32[]{:S(2)}) %all-to-all-start.1) | async-done | bytes 18464 | tf_op jit(solution)/shard_map/all_to_all | solution.py:153
  114.9 0.5 broadcast.99
  115.5 0.7 reduce.1
  116.2 0.1 reshape.121
  116.3 0.1 copy.86
  116.3 0.8 select_reduce_fusion
  117.2 0.7 select_reduce_fusion.1
  (30 shorter events, 0.2 us)
Async XLA Ops:
  7.2 7.1 %copy-start = (s32[4]{0:T(128)S(1)}, s32[4]{0:T(128)}, u32[]{:S(2)}) copy-start(s32[4]{0:T(128)} %constant.47.clone) | copy-start | bytes 52
  7.2 1.6 %copy-start.2 = (s32[128,8]{0,1:T(8,128)S(1)}, s32[128,8]{0,1:T(8,128)}, u32[]{:S(2)}) copy-start(s32[128,8]{0,1:T(8,128)} %param.9) | copy-start | bytes 12292
  7.2 1.6 %copy-start.3 = (bf16[128,8]{0,1:T(8,128)(2,1)S(1)}, bf16[128,8]{0,1:T(8,128)(2,1)}, u32[]{:S(2)}) copy-start(bf16[128,8]{0,1:T(8,128)(2,1)} %param.8) | copy-start | bytes 6148
  9.9 15.1 %copy-start.1 = (bf16[8,1,4,36,768]{4,2,3,1,0:T(4,128)(2,1)S(1)}, bf16[8,1,4,36,768]{4,2,3,1,0:T(4,128)(2,1)}, u32[]{:S(2)}) copy-start(bf16[8,1,4,36,768]{4,2,3,1,0:T(4,128)(2,1)} %param.10) | copy-start | bytes 5308420
  9.9 13.5 %all-to-all-start = ((bf16[132,4,512]{2,0,1:T(8,128)(2,1)}), bf16[132,4,512]{2,0,1:T(8,128)(2,1)S(1)}, u32[]{:S(2)}, u32[]{:S(2)}) async-start(bf16[132,4,512]{2,0,1:T(8,128)(2,1)} %pad_maximum_fusion), calls=%async_computation | async-start | bytes 1114112 | tf_op jit(solution)/shard_map/all_to_all | solution.py:113
  14.3 60.2 %all-gather.3.cloned.1.call-start = ((), (), s32[]{:S(2)}) async-start(), calls=%async_computation.2 | async-start | bytes 2785280 | tf_op jit(solution)/shard_map/all_gather | solution.py:122
  26.8 40.2 %collective-permute-start = (bf16[8,1,4,36,768]{4,0,3,2,1:T(8,128)(2,1)}, bf16[8,1,4,36,768]{4,0,3,2,1:T(8,128)(2,1)S(1)}, u32[]{:S(2)}, u32[]{:S(2)}) collective-permute-start(bf16[8,1,4,36,768]{4,0,3,2,1:T(8,128)(2,1)} %copy.76), channel_id=1, source_target_pairs={{0,2},{1,3},{2,0},{3,1},{4,6},{5,7},{6,4},{7,5},{8,10},{9,11},{10,... | collective-permute-start | bytes 5308424 | tf_op jit(solution)/shard_map/ppermute | solution.py:120
  27.1 41.7 %collective-permute-start.1 = (bf16[8,1,4,36,768]{4,0,3,2,1:T(8,128)(2,1)}, bf16[8,1,4,36,768]{4,0,3,2,1:T(8,128)(2,1)}, u32[]{:S(2)}, u32[]{:S(2)}) collective-permute-start(bf16[8,1,4,36,768]{4,0,3,2,1:T(8,128)(2,1)} %copy.76), channel_id=1, source_target_pairs={{0,1},{1,0},{2,3},{3,2},{4,5},{5,4},{6,7},{7,6},{8,9},{9,8},{10,11... | collective-permute-start | bytes 5308424 | tf_op jit(solution)/shard_map/ppermute | solution.py:119
  66.9 12.5 %collective-permute-start.2 = (bf16[8,1,4,36,768]{4,0,3,2,1:T(8,128)(2,1)S(1)}, bf16[8,1,4,36,768]{4,0,3,2,1:T(8,128)(2,1)}, u32[]{:S(2)}, u32[]{:S(2)}) collective-permute-start(bf16[8,1,4,36,768]{4,0,3,2,1:T(8,128)(2,1)S(1)} %collective-permute-done), channel_id=1, source_target_pairs={{0,1},{1,0},{2,3},{3,2},{4,5},{5,4},{6,7},{7,6},{8,9},{9,8},{10,11... | collective-permute-start | bytes 5308424 | tf_op jit(solution)/shard_map/ppermute | solution.py:121
  104.8 10.1 %all-to-all-start.1 = ((f32[16,1,288]{2,1,0:T(1,128)}), f32[16,1,288]{2,1,0:T(1,128)S(1)}, u32[]{:S(2)}, u32[]{:S(2)}) async-start(f32[16,1,288]{2,1,0:T(1,128)} %reshape.120), calls=%async_computation.1 | async-start | bytes 49152 | tf_op jit(solution)/shard_map/all_to_all | solution.py:153
Sparse Core Ops, SparseCore 0:
  25.1 49.3 all-gather.2

commit v6 on v5

--- a/solution.py
+++ b/solution.py
@@ -117,8 +117,15 @@
 
     hidden_sent, cols = lax.optimization_barrier((hidden, cols))
     near = lax.ppermute(hidden_sent, "dp", [(j, j ^ 1) for j in range(shards)])
-    far = lax.ppermute(hidden_sent, "dp", [(j, j ^ 2) for j in range(shards)])
-    near_far = lax.ppermute(far, "dp", [(j, j ^ 1) for j in range(shards)])
+    cut = local_count // 2 if local_count > 1 else local_count
+    far_parts = [
+        lax.ppermute(part, "dp", [(j, j ^ 2) for j in range(shards)])
+        for part in (hidden_sent[:cut], hidden_sent[cut:]) if part.shape[0] > 0
+    ]
+    near_far = jnp.concatenate(
+        [lax.ppermute(part, "dp", [(j, j ^ 1) for j in range(shards)]) for part in far_parts], axis=0
+    )
+    far = jnp.concatenate(far_parts, axis=0)
     got = lax.all_gather(cols, "expert", axis=0, tiled=False)
     got = got.reshape(block_count, tok_rows + meta_rows, col_width)
     grad_all = got[:, :tok_rows]

time: 125 us -> 129 us (1.032)
  starting transfers between devices: 8.24 us -> 12.4 us
  waiting for transfers between devices: 55.7 us -> 51.6 us
  other arithmetic: 9.81 us -> 12.9 us
    concatenate x0 -> x2, other arithmetic: none -> 3.08 us  [the longest x1 1.55 us: per_device(): far = jnp.concatenate(far_parts, axis=0)]
    all_gather x1, waiting for transfers between devices: 2.57 us -> 0.01 us  [per_device(): got = lax.all_gather(cols, 'expert', axis=0, tiled=False)]
    all_to_all x1, starting transfers between devices: 3.53 us -> 6.03 us  [per_device(): lax.all_to_all(send_back, ('expert', 'dp'), split_axis=0, concat_axis=0,...]
    slice x0 -> x1, local copies, waits for them, and re-layouts: none -> 1.8 us  [per_device(): hidden_sent[:cut]]
    ppermute x2 -> x4, starting transfers between devices: 0.36 us -> 2.03 us  [the longest x2 2.03 us: per_device(): lax.ppermute(part, 'dp', [(j, j ^ 2) for j in range(shards)])]
    ppermute x2 -> x4, waiting for transfers between devices: 37.4 us -> 35.8 us  [the longest x2 35.8 us: per_device(): lax.ppermute(part, 'dp', [(j, j ^ 2) for j in range(shards)])]
    ppermute x1, local copies, waits for them, and re-layouts: 3.09 us -> 1.62 us  [per_device(): near = lax.ppermute(hidden_sent, 'dp', [(j, j ^ 1) for j in range(shards)])]
    ppermute x2 -> x4, local copies, waits for them, and re-layouts: 4.86 us -> 5.08 us  [the longest x2 2.54 us: per_device(): lax.ppermute(part, 'dp', [(j, j ^ 2) for j in range(shards)])]
  transfers between devices with their start and end apart: 6 -> 8, of which waited for: 4 -> 4; matrix products, arithmetic and copies ran while one was open for 11% -> 12% of each run, Pallas kernels for 0% -> 0%
where the time goes in v6:
time: 129 us; the launch traced here: 128 us
  waiting for transfers between devices  51.6 us (40%)
  local copies, waits for them, and re-layouts  18.9 us (15%)
  Pallas kernels  18 us (14%)
  between operations  14.3 us (11%)
  other arithmetic  12.9 us (10%)
  starting transfers between devices  12.4 us (10%)
    ppermute x2, waiting for transfers between devices, per_device(): lax.ppermute(part, 'dp', [(j, j ^ 2) for j in range(shards)])  35.8 us
    pallas_call x1, Pallas kernels, expert_kernel(): pl.pallas_call(expert_body, grid=(local_count, steps), in_specs=[piece_sp...  18 us
    all_to_all x1, waiting for transfers between devices, per_device(): cols = lax.all_to_all(cols, 'dp', split_axis=1, concat_axis=0, tiled=True)  9.17 us
    all_to_all x1, waiting for transfers between devices, per_device(): lax.all_to_all(send_back, ('expert', 'dp'), split_axis=0, concat_axis=0,...  6.53 us
    all_to_all x1, starting transfers between devices, per_device(): lax.all_to_all(send_back, ('expert', 'dp'), split_axis=0, concat_axis=0,...  6.03 us
    all_to_all x1, starting transfers between devices, per_device(): cols = lax.all_to_all(cols, 'dp', split_axis=1, concat_axis=0, tiled=True)  4.34 us
    unnamed x14, local copies, waits for them, and re-layouts  4.11 us
    pallas_call x1, other arithmetic, expert_kernel(): pl.pallas_call(expert_body, grid=(local_count, steps), in_specs=[piece_sp...  2.77 us
  transfers between devices with their start and end apart: 8, of which 4 were waited for; matrix products, arithmetic and copies ran while one was open for 12% of the time, Pallas kernels for 0%

profile of v6, /device:TPU:0, one launch (start us, length us, event | category | flops | bytes accessed | tf_op | source)
XLA Modules:
  0.0 128.4 jit_solution(12257389164233666092)
XLA Ops:
  7.2 1.3 %copy.79 = bf16[128,2048]{0,1:T(8,128)(2,1)S(1)} copy(bf16[128,2048]{1,0:T(8,128)(2,1)} %param.7) | data formatting | bytes 1048576 | tf_op args[0]
  8.5 0.2 copy.81
  8.8 0.1 copy.80
  8.9 0.1 broadcast_in_dim.102
  9.1 0.9 pad_maximum_fusion.2
  9.9 4.3 %all-to-all-start = ((bf16[132,4,512]{2,0,1:T(8,128)(2,1)}), bf16[132,4,512]{2,0,1:T(8,128)(2,1)S(1)}, u32[]{:S(2)}, u32[]{:S(2)}) async-start(bf16[132,4,512]{2,0,1:T(8,128)(2,1)} %pad_maximum_fusion.2), calls=%async_computation | async-start | bytes 1114112 | tf_op jit(solution)/shard_map/all_to_all | solution.py:113
  14.3 9.2 %all-to-all-done = bf16[132,4,512]{2,0,1:T(8,128)(2,1)S(1)} async-done(((bf16[132,4,512]{2,0,1:T(8,128)(2,1)}), bf16[132,4,512]{2,0,1:T(8,128)(2,1)S(1)}, u32[]{:S(2)}, u32[]{:S(2)}) %all-to-all-start) | async-done | bytes 540704 | tf_op jit(solution)/shard_map/all_to_all | solution.py:113
  23.5 0.6 gather_fusion
  24.1 1.0 broadcast_select_fusion
  25.0 1.8 %fusion.8 = (bf16[4,1,4,36,768]{4,2,3,1,0:T(4,128)(2,1)}, bf16[4,1,4,36,768]{4,2,3,1,0:T(4,128)(2,1)}) fusion(bf16[8,1,4,36,768]{4,2,3,1,0:T(4,128)(2,1)S(1)} %copy-done.1), kind=kLoop, calls=%fused_computation.38 | loop fusion | bytes 3538944 | tf_op jit(solution)/shard_map/slice | solution.py:123
  26.8 0.4 collective-permute-start
  27.2 1.7 %collective-permute-start.1 = (bf16[4,1,4,36,768]{4,2,3,1,0:T(4,128)(2,1)}, bf16[4,1,4,36,768]{4,2,3,1,0:T(4,128)(2,1)}, u32[]{:S(2)}, u32[]{:S(2)}) collective-permute-start(bf16[4,1,4,36,768]{4,2,3,1,0:T(4,128)(2,1)} %get-tuple-element.13), channel_id=1, source_target_pairs={{0,2},{1,3},{2,0},{3,1},{4,6},{5,7},{6,4},{7,5},{8,10},{9,11},{10,... | collective-permute-start | bytes 2654216 | tf_op jit(solution)/shard_map/ppermute | solution.py:122
  28.9 1.7 %copy.84 = bf16[8,1,4,36,768]{4,0,3,2,1:T(8,128)(2,1)} copy(bf16[8,1,4,36,768]{4,2,3,1,0:T(4,128)(2,1)S(1)} %copy-done.1) | data formatting | bytes 3538944 | tf_op jit(solution)/shard_map/optimization_barrier | solution.py:118
  30.6 0.6 gather_fusion.1
  31.3 18.5 %collective-permute-done = bf16[4,1,4,36,768]{4,2,3,1,0:T(4,128)(2,1)} collective-permute-done((bf16[4,1,4,36,768]{4,2,3,1,0:T(4,128)(2,1)}, bf16[4,1,4,36,768]{4,2,3,1,0:T(4,128)(2,1)}, u32[]{:S(2)}, u32[]{:S(2)}) %collective-permute-start) | collective-permute-done | bytes 884768 | tf_op jit(solution)/shard_map/ppermute | solution.py:122
  49.7 17.4 %collective-permute-done.1 = bf16[4,1,4,36,768]{4,2,3,1,0:T(4,128)(2,1)} collective-permute-done((bf16[4,1,4,36,768]{4,2,3,1,0:T(4,128)(2,1)}, bf16[4,1,4,36,768]{4,2,3,1,0:T(4,128)(2,1)}, u32[]{:S(2)}, u32[]{:S(2)}) %collective-permute-start.1) | collective-permute-done | bytes 884768 | tf_op jit(solution)/shard_map/ppermute | solution.py:122
  67.1 1.6 %copy.89.own_ref = bf16[8,1,4,36,768]{4,3,2,1,0:T(8,128)(2,1)} copy(bf16[8,1,4,36,768]{4,2,3,1,0:T(4,128)(2,1)S(1)} %copy-done.1) | data formatting | bytes 3538944 | tf_op args[3]
  68.7 0.1 broadcast_in_dim.113
  68.9 0.1 convolution_convert_fusion.1
  69.0 1.3 copy.82
  70.3 1.3 copy.83
  71.6 1.6 %pad_maximum_fusion.far_ref = bf16[8,1,4,36,768]{4,3,2,1,0:T(8,128)(2,1)} fusion(bf16[4,1,4,36,768]{4,3,2,1,0:T(8,128)(2,1)S(1)} %copy.83, bf16[4,1,4,36,768]{4,3,2,1,0:T(8,128)(2,1)S(1)} %copy.82), kind=kLoop, calls=%fused_computation.7 | loop fusion | flops 884736 | bytes 3538944 | tf_op jit(solution)/shard_map/concatenate | solution.py:128
  73.1 1.3 copy.85
  74.4 1.3 copy.86
  75.7 1.6 %copy.90.near_ref = bf16[8,1,4,36,768]{4,3,2,1,0:T(8,128)(2,1)} copy(bf16[8,1,4,36,768]{4,0,3,2,1:T(8,128)(2,1)S(1)} %collective-permute-done.2) | data formatting | bytes 3538944 | tf_op jit(solution)/shard_map/ppermute | solution.py:119
  77.3 1.5 %pad_maximum_fusion.1.near_far_ref = bf16[8,1,4,36,768]{4,3,2,1,0:T(8,128)(2,1)} fusion(bf16[4,1,4,36,768]{4,3,2,1,0:T(8,128)(2,1)S(1)} %copy.86, bf16[4,1,4,36,768]{4,3,2,1,0:T(8,128)(2,1)S(1)} %copy.85), kind=kLoop, calls=%fused_computation.8 | loop fusion | flops 884736 | bytes 3538944 | tf_op jit(solution)/shard_map/concatenate | solution.py:125
  78.8 0.9 slice.34
  79.8 0.4 reshape_reshape.3
  80.1 0.2 fusion.9
  80.4 0.2 copy.96
  80.6 0.1 compare_reduce_fusion
  80.7 0.1 convolution_convert_fusion
  80.9 0.2 copy.97
  81.1 0.8 fusion.2
  81.8 1.9 %fusion.1.sel_ref = bf16[16,8,48,128]{3,2,1,0:T(8,128)(2,1)} fusion(s32[16,8,128]{2,1,0:T(8,128)S(1)} %convolution_convert_fusion, pred[16,8,128]{2,1,0:T(8,128)(4,1)S(1)} %bitcast.36), kind=kLoop, calls=%fused_computation.6 | loop fusion | flops 2359296 | bytes 1654784 | tf_op jit(solution)/shard_map/convert_element_type | solution.py:153
  83.7 18.0 %shard_map.86 = (f32[8,768,512]{2,1,0:T(8,128)}, f32[8,768,1]{2,1,0:T(8,128)}) custom-call(bf16[8,1,4,36,768]{4,3,2,1,0:T(8,128)(2,1)} %copy.89.own_ref, bf16[8,1,4,36,768]{4,3,2,1,0:T(8,128)(2,1)} %pad_maximum_fusion.far_ref, bf16[8,1,4,36,768]{4,3,2,1,0:T(8,128)(2,1)} %copy.90.near_ref, bf16[8,1,4,36,768]{4,3,2,1,0:T(8,128)(2,1)} %pad_maximum_fusion.1.near_far_ref, ...), custom_call_target="tpu_custom_call" | custom-call | tf_op jit(solution)/shard_map/pallas_call | solution.py:67
  101.7 2.8 %reduce = f32[8,768]{1,0:T(8,128)S(1)} reduce(f32[8,768,1]{2,1,0:T(8,128)} %get-tuple-element.9, f32[]{:T(128)} %constant.49), dimensions={2}, to_apply=%get-tuple-element.9.reduce_sub_computation | reduce | bytes 49156 | tf_op jit(solution)/shard_map/pallas_call | solution.py:67
  104.5 0.1 reshape.88
  104.6 0.6 gather_fusion.2
  105.2 0.1 bitcast_select_fusion
  105.3 0.7 reshape.120
  106.0 6.0 %all-to-all-start.1 = ((f32[16,1,288]{2,1,0:T(1,128)}), f32[16,1,288]{2,1,0:T(1,128)S(1)}, u32[]{:S(2)}, u32[]{:S(2)}) async-start(f32[16,1,288]{2,1,0:T(1,128)} %reshape.120), calls=%async_computation.1 | async-start | bytes 49152 | tf_op jit(solution)/shard_map/all_to_all | solution.py:160
  112.1 6.5 %all-to-all-done.1 = f32[16,1,288]{2,1,0:T(1,128)S(1)} async-done(((f32[16,1,288]{2,1,0:T(1,128)}), f32[16,1,288]{2,1,0:T(1,128)S(1)}, u32[]{:S(2)}, u32[]{:S(2)}) %all-to-all-start.1) | async-done | bytes 18464 | tf_op jit(solution)/shard_map/all_to_all | solution.py:160
  118.6 0.5 broadcast.99
  119.1 0.7 reduce.1
  119.9 0.1 copy.93
  120.0 0.8 select_reduce_fusion
  120.9 0.7 select_reduce_fusion.1
  (39 shorter events, 0.3 us)
Async XLA Ops:
  7.2 7.1 %copy-start = (s32[4]{0:T(128)S(1)}, s32[4]{0:T(128)}, u32[]{:S(2)}) copy-start(s32[4]{0:T(128)} %constant.47.clone) | copy-start | bytes 52
  7.2 1.6 %copy-start.2 = (s32[128,8]{0,1:T(8,128)S(1)}, s32[128,8]{0,1:T(8,128)}, u32[]{:S(2)}) copy-start(s32[128,8]{0,1:T(8,128)} %param.9) | copy-start | bytes 12292
  7.2 1.6 %copy-start.3 = (bf16[128,8]{0,1:T(8,128)(2,1)S(1)}, bf16[128,8]{0,1:T(8,128)(2,1)}, u32[]{:S(2)}) copy-start(bf16[128,8]{0,1:T(8,128)(2,1)} %param.8) | copy-start | bytes 6148
  9.9 15.1 %copy-start.1 = (bf16[8,1,4,36,768]{4,2,3,1,0:T(4,128)(2,1)S(1)}, bf16[8,1,4,36,768]{4,2,3,1,0:T(4,128)(2,1)}, u32[]{:S(2)}) copy-start(bf16[8,1,4,36,768]{4,2,3,1,0:T(4,128)(2,1)} %param.10) | copy-start | bytes 5308420
  9.9 13.5 %all-to-all-start = ((bf16[132,4,512]{2,0,1:T(8,128)(2,1)}), bf16[132,4,512]{2,0,1:T(8,128)(2,1)S(1)}, u32[]{:S(2)}, u32[]{:S(2)}) async-start(bf16[132,4,512]{2,0,1:T(8,128)(2,1)} %pad_maximum_fusion.2), calls=%async_computation | async-start | bytes 1114112 | tf_op jit(solution)/shard_map/all_to_all | solution.py:113
  14.3 64.6 %all-gather.3.cloned.1.call-start = ((), (), s32[]{:S(2)}) async-start(), calls=%async_computation.2 | async-start | bytes 2785280 | tf_op jit(solution)/shard_map/all_gather | solution.py:129
  26.8 22.9 %collective-permute-start = (bf16[4,1,4,36,768]{4,2,3,1,0:T(4,128)(2,1)}, bf16[4,1,4,36,768]{4,2,3,1,0:T(4,128)(2,1)}, u32[]{:S(2)}, u32[]{:S(2)}) collective-permute-start(bf16[4,1,4,36,768]{4,2,3,1,0:T(4,128)(2,1)} %get-tuple-element.12), channel_id=1, source_target_pairs={{0,2},{1,3},{2,0},{3,1},{4,6},{5,7},{6,4},{7,5},{8,10},{9,11},{10,... | collective-permute-start | bytes 2654216 | tf_op jit(solution)/shard_map/ppermute | solution.py:122
  27.2 39.9 %collective-permute-start.1 = (bf16[4,1,4,36,768]{4,2,3,1,0:T(4,128)(2,1)}, bf16[4,1,4,36,768]{4,2,3,1,0:T(4,128)(2,1)}, u32[]{:S(2)}, u32[]{:S(2)}) collective-permute-start(bf16[4,1,4,36,768]{4,2,3,1,0:T(4,128)(2,1)} %get-tuple-element.13), channel_id=1, source_target_pairs={{0,2},{1,3},{2,0},{3,1},{4,6},{5,7},{6,4},{7,5},{8,10},{9,11},{10,... | collective-permute-start | bytes 2654216 | tf_op jit(solution)/shard_map/ppermute | solution.py:122
  30.6 45.1 %collective-permute-start.2 = (bf16[8,1,4,36,768]{4,0,3,2,1:T(8,128)(2,1)}, bf16[8,1,4,36,768]{4,0,3,2,1:T(8,128)(2,1)S(1)}, u32[]{:S(2)}, u32[]{:S(2)}) collective-permute-start(bf16[8,1,4,36,768]{4,0,3,2,1:T(8,128)(2,1)} %copy.84), channel_id=1, source_target_pairs={{0,1},{1,0},{2,3},{3,2},{4,5},{5,4},{6,7},{7,6},{8,9},{9,8},{10,11... | collective-permute-start | bytes 5308424 | tf_op jit(solution)/shard_map/ppermute | solution.py:119
  49.7 23.4 %collective-permute-start.3 = (bf16[4,1,4,36,768]{4,2,3,1,0:T(4,128)(2,1)}, bf16[4,1,4,36,768]{4,2,3,1,0:T(4,128)(2,1)}, u32[]{:S(2)}, u32[]{:S(2)}) collective-permute-start(bf16[4,1,4,36,768]{4,2,3,1,0:T(4,128)(2,1)} %collective-permute-done), channel_id=1, source_target_pairs={{0,1},{1,0},{2,3},{3,2},{4,5},{5,4},{6,7},{7,6},{8,9},{9,8},{10,11... | collective-permute-start | bytes 2654216 | tf_op jit(solution)/shard_map/ppermute | solution.py:126
  67.1 7.3 %collective-permute-start.4 = (bf16[4,1,4,36,768]{4,2,3,1,0:T(4,128)(2,1)}, bf16[4,1,4,36,768]{4,2,3,1,0:T(4,128)(2,1)}, u32[]{:S(2)}, u32[]{:S(2)}) collective-permute-start(bf16[4,1,4,36,768]{4,2,3,1,0:T(4,128)(2,1)} %collective-permute-done.1), channel_id=1, source_target_pairs={{0,1},{1,0},{2,3},{3,2},{4,5},{5,4},{6,7},{7,6},{8,9},{9,8},{10,11... | collective-permute-start | bytes 2654216 | tf_op jit(solution)/shard_map/ppermute | solution.py:126
  106.0 12.6 %all-to-all-start.1 = ((f32[16,1,288]{2,1,0:T(1,128)}), f32[16,1,288]{2,1,0:T(1,128)S(1)}, u32[]{:S(2)}, u32[]{:S(2)}) async-start(f32[16,1,288]{2,1,0:T(1,128)} %reshape.120), calls=%async_computation.1 | async-start | bytes 49152 | tf_op jit(solution)/shard_map/all_to_all | solution.py:160
Sparse Core Ops, SparseCore 0:
  25.1 49.3 all-gather.2

commit v7 on v5

--- a/solution.py
+++ b/solution.py
@@ -11,7 +11,8 @@
     expert = pl.program_id(0)
     chunk = pl.program_id(1)
     sources, capacity, hidden_width = own_ref.shape[2:]
-    blocks, _, padded, _ = sel_ref.shape
+    blocks = sel_ref.shape[0]
+    padded = s_scr.shape[0] // blocks
     col_width = tok_ref.shape[2]
     pieces = (own_ref, far_ref, near_ref, near_far_ref)
 
@@ -24,10 +25,12 @@
             row = (src * len(pieces) + j) * padded
             h_scr[row:row + capacity, :] = ref[0, 0, src]
 
+    slot_iota = lax.broadcasted_iota(jnp.int32, (padded, tok_ref.shape[1]), 0)
     for blk in range(blocks):
-        sel = sel_ref[blk, 0]
+        hit = sel_ref[blk, 0] == slot_iota
+        sel = hit.astype(jnp.bfloat16)
         rows = jnp.dot(sel, tok_ref[blk], preferred_element_type=jnp.float32)
-        gate = jnp.sum(sel.astype(jnp.float32) * gate_ref[blk, 0], axis=1, keepdims=True)
+        gate = jnp.sum(jnp.where(hit, gate_ref[blk, 0], 0.0), axis=1, keepdims=True)
         g_scr[blk * padded:(blk + 1) * padded, :] = rows.astype(jnp.bfloat16)
         s_scr[blk * padded:(blk + 1) * padded, :] = (gate * rows).astype(jnp.bfloat16)
 
@@ -45,13 +48,15 @@
         wg_ref[0] = wg_ref[0] + part
 
     out = jnp.dot(h, w_ref[0], preferred_element_type=jnp.float32)
-    slot_ref[0] = jnp.sum(g_scr[...].astype(jnp.float32) * out, axis=1, keepdims=True)
+    col = jnp.sum(g_scr[...].astype(jnp.float32) * out, axis=1, keepdims=True)
+    wide = jnp.broadcast_to(col, (col.shape[0], 128))
+    slot_ref[0] = jnp.transpose(wide)[0:1, :]
 
 
-def expert_kernel(pieces, tokens, select, gate_row, weight):
+def expert_kernel(pieces, tokens, slot_row, gate_row, weight, padded):
     local_count, _, source_count, capacity, hidden_width = pieces[0].shape
     col_width = tokens.shape[2]
-    block_count, _, padded, tok_rows = select.shape
+    block_count, _, _, tok_rows = slot_row.shape
     per_source = block_count // source_count
     chunk = source_count
     for size in (4, 2, 1):
@@ -69,24 +74,24 @@
         grid=(local_count, steps),
         in_specs=[piece_spec] * len(pieces) + [
             pl.BlockSpec((blocks, tok_rows, col_width), lambda l, r: (r, 0, 0)),
-            pl.BlockSpec((blocks, 1, padded, tok_rows), lambda l, r: (r, l, 0, 0)),
+            pl.BlockSpec((blocks, 1, 1, tok_rows), lambda l, r: (r, l, 0, 0)),
             pl.BlockSpec((blocks, 1, 1, tok_rows), lambda l, r: (r, l, 0, 0)),
             pl.BlockSpec((1, hidden_width, col_width), lambda l, r: (l, 0, 0)),
         ],
         out_specs=[
             pl.BlockSpec((1, hidden_width, col_width), lambda l, r: (l, 0, 0)),
-            pl.BlockSpec((1, rows, 1), lambda l, r: (l, r, 0)),
+            pl.BlockSpec((1, 1, rows), lambda l, r: (l, 0, r)),
         ],
         out_shape=[
             jax.ShapeDtypeStruct((local_count, hidden_width, col_width), jnp.float32),
-            jax.ShapeDtypeStruct((local_count, block_count * padded, 1), jnp.float32),
+            jax.ShapeDtypeStruct((local_count, 1, block_count * padded), jnp.float32),
         ],
         scratch_shapes=[
             pltpu.VMEM((rows, hidden_width), jnp.bfloat16),
             pltpu.VMEM((rows, col_width), jnp.bfloat16),
             pltpu.VMEM((rows, col_width), jnp.bfloat16),
         ],
-    )(*pieces, tokens, select, gate_row, weight)
+    )(*pieces, tokens, slot_row, gate_row, weight)
 
 
 def per_device(out_grad, gate_weights, expert_ids, hidden, down_weight):
@@ -140,10 +145,10 @@
     chose_t = chose.transpose(0, 2, 1)
     rank_t = rank.transpose(0, 2, 1)
     gate_t = gate_hit.transpose(0, 2, 1)
-    select = chose_t[:, :, None, :] & (rank_t[:, :, None, :] == slot_ids[None, None, :, None])
+    slot_row = jnp.where(chose_t, rank_t, -1)[:, :, None, :]
     gate_row = gate_t[:, :, None, :]
     weight_grad, slot_part = expert_kernel(
-        (hidden, far, near, near_far), got, select.astype(bf16), gate_row, down_weight
+        (hidden, far, near, near_far), got, slot_row, gate_row, down_weight, padded
     )
     slot_part = slot_part.reshape(local_count, block_count, padded)[:, :, :capacity]
     slot_part = slot_part.transpose(1, 0, 2).reshape(peer_count, shards, local_count, capacity)

time: 125 us -> 123 us (0.984)
  other arithmetic: 9.81 us -> 5.9 us
    pallas_call x1, other arithmetic: 2.77 us -> 0.79 us  [expert_kernel(): pl.pallas_call(expert_body, grid=(local_count, steps), in_specs=[piece_sp...]
    convert_element_type x1 -> x0, other arithmetic: 1.91 us -> none  [per_device(): select.astype(bf16)]
  transfers between devices with their start and end apart: 6 -> 6, of which waited for: 4 -> 4; matrix products, arithmetic and copies ran while one was open for 11% -> 10% of each run, Pallas kernels for 0% -> 0%
where the time goes in v7:
time: 123 us; the launch traced here: 122 us
  waiting for transfers between devices  55.8 us (45%)
  Pallas kernels  18.9 us (15%)
  local copies, waits for them, and re-layouts  18.3 us (15%)
  between operations  14.3 us (12%)
  starting transfers between devices  8.25 us (7%)
  other arithmetic  5.9 us (5%)
    ppermute x1, waiting for transfers between devices, per_device(): far = lax.ppermute(hidden_sent, 'dp', [(j, j ^ 2) for j in range(shards)])  37.6 us
    pallas_call x1, Pallas kernels, expert_kernel(): pl.pallas_call(expert_body, grid=(local_count, steps), in_specs=[piece_sp...  18.9 us
    all_to_all x1, waiting for transfers between devices, per_device(): cols = lax.all_to_all(cols, 'dp', split_axis=1, concat_axis=0, tiled=True)  9.17 us
    all_to_all x1, waiting for transfers between devices, per_device(): lax.all_to_all(send_back, ('expert', 'dp'), split_axis=0, concat_axis=0,...  6.53 us
    all_to_all x1, starting transfers between devices, per_device(): cols = lax.all_to_all(cols, 'dp', split_axis=1, concat_axis=0, tiled=True)  4.34 us
    unnamed x14, local copies, waits for them, and re-layouts  4.04 us
    all_to_all x1, starting transfers between devices, per_device(): lax.all_to_all(send_back, ('expert', 'dp'), split_axis=0, concat_axis=0,...  3.54 us
    ppermute x1, local copies, waits for them, and re-layouts, per_device(): near_far = lax.ppermute(far, 'dp', [(j, j ^ 1) for j in range(shards)])  3.18 us
  transfers between devices with their start and end apart: 6, of which 4 were waited for; matrix products, arithmetic and copies ran while one was open for 10% of the time, Pallas kernels for 0%

profile of v7, /device:TPU:0, one launch (start us, length us, event | category | flops | bytes accessed | tf_op | source)
XLA Modules:
  0.0 122.4 jit_solution(12806043815758205597)
XLA Ops:
  7.2 0.0 copy-start
  7.2 1.3 %copy.73 = bf16[128,2048]{0,1:T(8,128)(2,1)S(1)} copy(bf16[128,2048]{1,0:T(8,128)(2,1)} %param.7) | data formatting | bytes 1048576 | tf_op args[0]
  8.5 0.2 copy.75
  8.8 0.1 copy.74
  8.9 0.1 broadcast_in_dim.106
  9.1 0.9 pad_maximum_fusion
  9.9 4.3 %all-to-all-start = ((bf16[132,4,512]{2,0,1:T(8,128)(2,1)}), bf16[132,4,512]{2,0,1:T(8,128)(2,1)S(1)}, u32[]{:S(2)}, u32[]{:S(2)}) async-start(bf16[132,4,512]{2,0,1:T(8,128)(2,1)} %pad_maximum_fusion), calls=%async_computation | async-start | bytes 1114112 | tf_op jit(solution)/shard_map/all_to_all | solution.py:118
  14.3 9.2 %all-to-all-done = bf16[132,4,512]{2,0,1:T(8,128)(2,1)S(1)} async-done(((bf16[132,4,512]{2,0,1:T(8,128)(2,1)}), bf16[132,4,512]{2,0,1:T(8,128)(2,1)S(1)}, u32[]{:S(2)}, u32[]{:S(2)}) %all-to-all-start) | async-done | bytes 540704 | tf_op jit(solution)/shard_map/all_to_all | solution.py:118
  23.5 0.6 gather_fusion
  24.1 0.9 broadcast_select_fusion
  25.0 0.0 all-gather.3.cloned.1.call-update
  25.0 1.7 %copy.76 = bf16[8,1,4,36,768]{4,0,3,2,1:T(8,128)(2,1)} copy(bf16[8,1,4,36,768]{4,2,3,1,0:T(4,128)(2,1)S(1)} %copy-done.1) | data formatting | bytes 3538944 | tf_op jit(solution)/shard_map/optimization_barrier | solution.py:123
  26.8 0.4 collective-permute-start
  27.1 0.0 collective-permute-start.1
  27.1 1.5 %copy.80.own_ref = bf16[8,1,4,36,768]{4,3,2,1,0:T(8,128)(2,1)} copy(bf16[8,1,4,36,768]{4,2,3,1,0:T(4,128)(2,1)S(1)} %copy-done.1) | data formatting | bytes 3538944 | tf_op args[3]
  28.7 0.6 gather_fusion.1
  29.3 37.6 %collective-permute-done = bf16[8,1,4,36,768]{4,0,3,2,1:T(8,128)(2,1)S(1)} collective-permute-done((bf16[8,1,4,36,768]{4,0,3,2,1:T(8,128)(2,1)}, bf16[8,1,4,36,768]{4,0,3,2,1:T(8,128)(2,1)S(1)}, u32[]{:S(2)}, u32[]{:S(2)}) %collective-permute-start) | collective-permute-done | bytes 1769504 | tf_op jit(solution)/shard_map/ppermute | solution.py:125
  66.9 0.0 collective-permute-start.2
  67.0 0.1 broadcast_in_dim.119
  67.1 0.1 convolution_convert_fusion.1
  67.2 1.7 %copy.81.far_ref = bf16[8,1,4,36,768]{4,3,2,1,0:T(8,128)(2,1)} copy(bf16[8,1,4,36,768]{4,0,3,2,1:T(8,128)(2,1)S(1)} %collective-permute-done) | data formatting | bytes 3538944 | tf_op jit(solution)/shard_map/ppermute | solution.py:125
  68.9 0.0 collective-permute-done.1
  68.9 3.1 %copy.82.near_ref = bf16[8,1,4,36,768]{4,3,2,1,0:T(8,128)(2,1)} copy(bf16[8,1,4,36,768]{4,0,3,2,1:T(8,128)(2,1)} %collective-permute-done.1) | data formatting | bytes 3538944 | tf_op jit(solution)/shard_map/ppermute | solution.py:124
  72.0 2.5 %all-gather.3.cloned.1.call-done.tok_ref = bf16[16,132,512]{2,1,0:T(8,128)(2,1)} async-done(((bf16[4,132,512]{2,1,0:T(8,128)(2,1)}), bf16[16,132,512]{2,1,0:T(8,128)(2,1)}) %all-gather.3.cloned.1.call-update) | async-done | bytes 2162704 | tf_op jit(solution)/shard_map/all_gather | solution.py:127
  74.5 0.9 slice.26
  75.4 0.4 reshape_reshape.3
  75.8 0.2 fusion.7
  76.0 0.2 copy.89
  76.2 0.2 copy.90
  76.4 0.1 compare_reduce_fusion
  76.6 0.7 fusion.1
  77.3 0.8 fusion
  78.1 0.0 collective-permute-done.2
  78.1 3.2 %copy.83.near_far_ref = bf16[8,1,4,36,768]{4,3,2,1,0:T(8,128)(2,1)} copy(bf16[8,1,4,36,768]{4,0,3,2,1:T(8,128)(2,1)} %collective-permute-done.2) | data formatting | bytes 3538944 | tf_op jit(solution)/shard_map/ppermute | solution.py:126
  81.3 18.9 %shard_map.86 = (f32[8,768,512]{2,1,0:T(8,128)}, f32[8,1,768]{2,1,0:T(1,128)}) custom-call(bf16[8,1,4,36,768]{4,3,2,1,0:T(8,128)(2,1)} %copy.80.own_ref, bf16[8,1,4,36,768]{4,3,2,1,0:T(8,128)(2,1)} %copy.81.far_ref, bf16[8,1,4,36,768]{4,3,2,1,0:T(8,128)(2,1)} %copy.82.near_ref, bf16[8,1,4,36,768]{4,3,2,1,0:T(8,128)(2,1)} %copy.83.near_far_ref, ...), custom_call_target="tpu_custom_call" | custom-call | tf_op jit(solution)/shard_map/pallas_call | solution.py:72
  100.2 0.8 reduce
  101.0 0.1 reshape.86
  101.1 0.6 gather_fusion.2
  101.7 0.1 bitcast_select_fusion
  101.8 0.7 reshape.118
  102.5 3.5 %all-to-all-start.1 = ((f32[16,1,288]{2,1,0:T(1,128)}), f32[16,1,288]{2,1,0:T(1,128)S(1)}, u32[]{:S(2)}, u32[]{:S(2)}) async-start(f32[16,1,288]{2,1,0:T(1,128)} %reshape.118), calls=%async_computation.1 | async-start | bytes 49152 | tf_op jit(solution)/shard_map/all_to_all | solution.py:158
  106.1 6.5 %all-to-all-done.1 = f32[16,1,288]{2,1,0:T(1,128)S(1)} async-done(((f32[16,1,288]{2,1,0:T(1,128)}), f32[16,1,288]{2,1,0:T(1,128)S(1)}, u32[]{:S(2)}, u32[]{:S(2)}) %all-to-all-start.1) | async-done | bytes 18464 | tf_op jit(solution)/shard_map/all_to_all | solution.py:158
  112.6 0.5 broadcast.97
  113.1 0.7 reduce.1
  113.8 0.1 reshape.119
  113.9 0.1 copy.86
  114.0 0.8 select_reduce_fusion
  114.9 0.7 select_reduce_fusion.1
  (29 shorter events, 0.2 us)
Async XLA Ops:
  7.2 7.1 %copy-start = (s32[4]{0:T(128)S(1)}, s32[4]{0:T(128)}, u32[]{:S(2)}) copy-start(s32[4]{0:T(128)} %constant.49.clone) | copy-start | bytes 52
  7.2 1.6 %copy-start.2 = (s32[128,8]{0,1:T(8,128)S(1)}, s32[128,8]{0,1:T(8,128)}, u32[]{:S(2)}) copy-start(s32[128,8]{0,1:T(8,128)} %param.9) | copy-start | bytes 12292
  7.2 1.6 %copy-start.3 = (bf16[128,8]{0,1:T(8,128)(2,1)S(1)}, bf16[128,8]{0,1:T(8,128)(2,1)}, u32[]{:S(2)}) copy-start(bf16[128,8]{0,1:T(8,128)(2,1)} %param.8) | copy-start | bytes 6148
  9.9 15.1 %copy-start.1 = (bf16[8,1,4,36,768]{4,2,3,1,0:T(4,128)(2,1)S(1)}, bf16[8,1,4,36,768]{4,2,3,1,0:T(4,128)(2,1)}, u32[]{:S(2)}) copy-start(bf16[8,1,4,36,768]{4,2,3,1,0:T(4,128)(2,1)} %param.10) | copy-start | bytes 5308420
  9.9 13.5 %all-to-all-start = ((bf16[132,4,512]{2,0,1:T(8,128)(2,1)}), bf16[132,4,512]{2,0,1:T(8,128)(2,1)S(1)}, u32[]{:S(2)}, u32[]{:S(2)}) async-start(bf16[132,4,512]{2,0,1:T(8,128)(2,1)} %pad_maximum_fusion), calls=%async_computation | async-start | bytes 1114112 | tf_op jit(solution)/shard_map/all_to_all | solution.py:118
  14.3 60.2 %all-gather.3.cloned.1.call-start = ((), (), s32[]{:S(2)}) async-start(), calls=%async_computation.2 | async-start | bytes 2785280 | tf_op jit(solution)/shard_map/all_gather | solution.py:127
  26.8 40.2 %collective-permute-start = (bf16[8,1,4,36,768]{4,0,3,2,1:T(8,128)(2,1)}, bf16[8,1,4,36,768]{4,0,3,2,1:T(8,128)(2,1)S(1)}, u32[]{:S(2)}, u32[]{:S(2)}) collective-permute-start(bf16[8,1,4,36,768]{4,0,3,2,1:T(8,128)(2,1)} %copy.76), channel_id=1, source_target_pairs={{0,2},{1,3},{2,0},{3,1},{4,6},{5,7},{6,4},{7,5},{8,10},{9,11},{10,... | collective-permute-start | bytes 5308424 | tf_op jit(solution)/shard_map/ppermute | solution.py:125
  27.1 41.8 %collective-permute-start.1 = (bf16[8,1,4,36,768]{4,0,3,2,1:T(8,128)(2,1)}, bf16[8,1,4,36,768]{4,0,3,2,1:T(8,128)(2,1)}, u32[]{:S(2)}, u32[]{:S(2)}) collective-permute-start(bf16[8,1,4,36,768]{4,0,3,2,1:T(8,128)(2,1)} %copy.76), channel_id=1, source_target_pairs={{0,1},{1,0},{2,3},{3,2},{4,5},{5,4},{6,7},{7,6},{8,9},{9,8},{10,11... | collective-permute-start | bytes 5308424 | tf_op jit(solution)/shard_map/ppermute | solution.py:124
  66.9 11.2 %collective-permute-start.2 = (bf16[8,1,4,36,768]{4,0,3,2,1:T(8,128)(2,1)S(1)}, bf16[8,1,4,36,768]{4,0,3,2,1:T(8,128)(2,1)}, u32[]{:S(2)}, u32[]{:S(2)}) collective-permute-start(bf16[8,1,4,36,768]{4,0,3,2,1:T(8,128)(2,1)S(1)} %collective-permute-done), channel_id=1, source_target_pairs={{0,1},{1,0},{2,3},{3,2},{4,5},{5,4},{6,7},{7,6},{8,9},{9,8},{10,11... | collective-permute-start | bytes 5308424 | tf_op jit(solution)/shard_map/ppermute | solution.py:126
  102.5 10.1 %all-to-all-start.1 = ((f32[16,1,288]{2,1,0:T(1,128)}), f32[16,1,288]{2,1,0:T(1,128)S(1)}, u32[]{:S(2)}, u32[]{:S(2)}) async-start(f32[16,1,288]{2,1,0:T(1,128)} %reshape.118), calls=%async_computation.1 | async-start | bytes 49152 | tf_op jit(solution)/shard_map/all_to_all | solution.py:158
Sparse Core Ops, SparseCore 0:
  25.1 49.3 all-gather.2

commit v8 on v7

--- a/solution.py
+++ b/solution.py
@@ -23,7 +23,7 @@
     for src in range(sources):
         for j, ref in enumerate(pieces):
             row = (src * len(pieces) + j) * padded
-            h_scr[row:row + capacity, :] = ref[0, 0, src]
+            h_scr[row:row + capacity, :] = ref[0, 0, src].astype(jnp.float32)
 
     slot_iota = lax.broadcasted_iota(jnp.int32, (padded, tok_ref.shape[1]), 0)
     for blk in range(blocks):
@@ -31,12 +31,15 @@
         sel = hit.astype(jnp.bfloat16)
         rows = jnp.dot(sel, tok_ref[blk], preferred_element_type=jnp.float32)
         gate = jnp.sum(jnp.where(hit, gate_ref[blk, 0], 0.0), axis=1, keepdims=True)
-        g_scr[blk * padded:(blk + 1) * padded, :] = rows.astype(jnp.bfloat16)
-        s_scr[blk * padded:(blk + 1) * padded, :] = (gate * rows).astype(jnp.bfloat16)
+        g_scr[blk * padded:(blk + 1) * padded, :] = rows
+        s_scr[blk * padded:(blk + 1) * padded, :] = (
+            (gate * rows).astype(jnp.bfloat16).astype(jnp.float32)
+        )
 
-    h = h_scr[...]
+    h = h_scr[...].astype(jnp.bfloat16)
     part = lax.dot_general(
-        h, s_scr[...], (((0,), (0,)), ((), ())), preferred_element_type=jnp.float32
+        h, s_scr[...].astype(jnp.bfloat16), (((0,), (0,)), ((), ())),
+        preferred_element_type=jnp.float32,
     )
 
     @pl.when(chunk == 0)
@@ -48,7 +51,7 @@
         wg_ref[0] = wg_ref[0] + part
 
     out = jnp.dot(h, w_ref[0], preferred_element_type=jnp.float32)
-    col = jnp.sum(g_scr[...].astype(jnp.float32) * out, axis=1, keepdims=True)
+    col = jnp.sum(g_scr[...] * out, axis=1, keepdims=True)
     wide = jnp.broadcast_to(col, (col.shape[0], 128))
     slot_ref[0] = jnp.transpose(wide)[0:1, :]
 
@@ -87,9 +90,9 @@
             jax.ShapeDtypeStruct((local_count, 1, block_count * padded), jnp.float32),
         ],
         scratch_shapes=[
-            pltpu.VMEM((rows, hidden_width), jnp.bfloat16),
-            pltpu.VMEM((rows, col_width), jnp.bfloat16),
-            pltpu.VMEM((rows, col_width), jnp.bfloat16),
+            pltpu.VMEM((rows, hidden_width), jnp.float32),
+            pltpu.VMEM((rows, col_width), jnp.float32),
+            pltpu.VMEM((rows, col_width), jnp.float32),
         ],
     )(*pieces, tokens, slot_row, gate_row, weight)
 
@@ -140,7 +143,7 @@
     rank = jnp.einsum(
         "bul,ut->btl", chose.astype(bf16), before, preferred_element_type=f32
     ).astype(jnp.int32)
-    padded = -(-capacity // 16) * 16
+    padded = -(-capacity // 8) * 8
     slot_ids = jnp.arange(padded, dtype=jnp.int32)
     chose_t = chose.transpose(0, 2, 1)
     rank_t = rank.transpose(0, 2, 1)

time: 123 us -> 122 us (level)
  no operation moved by 1% of the time
where the time goes in v8:
time: 122 us; the launch traced here: 121 us
  waiting for transfers between devices  55.8 us (46%)
  local copies, waits for them, and re-layouts  18.3 us (15%)
  Pallas kernels  17.8 us (15%)
  between operations  14.3 us (12%)
  starting transfers between devices  8.25 us (7%)
  other arithmetic  5.88 us (5%)
    ppermute x1, waiting for transfers between devices, per_device(): far = lax.ppermute(hidden_sent, 'dp', [(j, j ^ 2) for j in range(shards)])  37.6 us
    pallas_call x1, Pallas kernels, expert_kernel(): pl.pallas_call(expert_body, grid=(local_count, steps), in_specs=[piece_sp...  17.8 us
    all_to_all x1, waiting for transfers between devices, per_device(): cols = lax.all_to_all(cols, 'dp', split_axis=1, concat_axis=0, tiled=True)  9.17 us
    all_to_all x1, waiting for transfers between devices, per_device(): lax.all_to_all(send_back, ('expert', 'dp'), split_axis=0, concat_axis=0,...  6.53 us
    all_to_all x1, starting transfers between devices, per_device(): cols = lax.all_to_all(cols, 'dp', split_axis=1, concat_axis=0, tiled=True)  4.34 us
    unnamed x14, local copies, waits for them, and re-layouts  4.04 us
    all_to_all x1, starting transfers between devices, per_device(): lax.all_to_all(send_back, ('expert', 'dp'), split_axis=0, concat_axis=0,...  3.54 us
    ppermute x1, local copies, waits for them, and re-layouts, per_device(): near_far = lax.ppermute(far, 'dp', [(j, j ^ 1) for j in range(shards)])  3.18 us
  transfers between devices with their start and end apart: 6, of which 4 were waited for; matrix products, arithmetic and copies ran while one was open for 10% of the time, Pallas kernels for 0%

profile of v8, /device:TPU:0, one launch (start us, length us, event | category | flops | bytes accessed | tf_op | source)
XLA Modules:
  0.0 121.2 jit_solution(3785413941331462559)
XLA Ops:
  7.2 0.0 copy-start
  7.2 1.3 %copy.73 = bf16[128,2048]{0,1:T(8,128)(2,1)S(1)} copy(bf16[128,2048]{1,0:T(8,128)(2,1)} %param.7) | data formatting | bytes 1048576 | tf_op args[0]
  8.5 0.2 copy.75
  8.8 0.1 copy.74
  8.9 0.1 broadcast_in_dim.106
  9.1 0.9 pad_maximum_fusion
  9.9 4.3 %all-to-all-start = ((bf16[132,4,512]{2,0,1:T(8,128)(2,1)}), bf16[132,4,512]{2,0,1:T(8,128)(2,1)S(1)}, u32[]{:S(2)}, u32[]{:S(2)}) async-start(bf16[132,4,512]{2,0,1:T(8,128)(2,1)} %pad_maximum_fusion), calls=%async_computation | async-start | bytes 1114112 | tf_op jit(solution)/shard_map/all_to_all | solution.py:121
  14.3 9.2 %all-to-all-done = bf16[132,4,512]{2,0,1:T(8,128)(2,1)S(1)} async-done(((bf16[132,4,512]{2,0,1:T(8,128)(2,1)}), bf16[132,4,512]{2,0,1:T(8,128)(2,1)S(1)}, u32[]{:S(2)}, u32[]{:S(2)}) %all-to-all-start) | async-done | bytes 540704 | tf_op jit(solution)/shard_map/all_to_all | solution.py:121
  23.5 0.6 gather_fusion
  24.1 0.9 broadcast_select_fusion
  25.0 0.0 all-gather.3.cloned.1.call-update
  25.0 1.7 %copy.76 = bf16[8,1,4,36,768]{4,0,3,2,1:T(8,128)(2,1)} copy(bf16[8,1,4,36,768]{4,2,3,1,0:T(4,128)(2,1)S(1)} %copy-done.1) | data formatting | bytes 3538944 | tf_op jit(solution)/shard_map/optimization_barrier | solution.py:126
  26.8 0.4 collective-permute-start
  27.1 0.0 collective-permute-start.1
  27.1 1.5 %copy.80.own_ref = bf16[8,1,4,36,768]{4,3,2,1,0:T(8,128)(2,1)} copy(bf16[8,1,4,36,768]{4,2,3,1,0:T(4,128)(2,1)S(1)} %copy-done.1) | data formatting | bytes 3538944 | tf_op args[3]
  28.7 0.6 gather_fusion.1
  29.3 37.6 %collective-permute-done = bf16[8,1,4,36,768]{4,0,3,2,1:T(8,128)(2,1)S(1)} collective-permute-done((bf16[8,1,4,36,768]{4,0,3,2,1:T(8,128)(2,1)}, bf16[8,1,4,36,768]{4,0,3,2,1:T(8,128)(2,1)S(1)}, u32[]{:S(2)}, u32[]{:S(2)}) %collective-permute-start) | collective-permute-done | bytes 1769504 | tf_op jit(solution)/shard_map/ppermute | solution.py:128
  66.9 0.0 collective-permute-start.2
  67.0 0.1 broadcast_in_dim.119
  67.1 0.1 convolution_convert_fusion.1
  67.2 1.7 %copy.81.far_ref = bf16[8,1,4,36,768]{4,3,2,1,0:T(8,128)(2,1)} copy(bf16[8,1,4,36,768]{4,0,3,2,1:T(8,128)(2,1)S(1)} %collective-permute-done) | data formatting | bytes 3538944 | tf_op jit(solution)/shard_map/ppermute | solution.py:128
  68.9 0.0 collective-permute-done.1
  68.9 3.1 %copy.82.near_ref = bf16[8,1,4,36,768]{4,3,2,1,0:T(8,128)(2,1)} copy(bf16[8,1,4,36,768]{4,0,3,2,1:T(8,128)(2,1)} %collective-permute-done.1) | data formatting | bytes 3538944 | tf_op jit(solution)/shard_map/ppermute | solution.py:127
  72.0 2.5 %all-gather.3.cloned.1.call-done.tok_ref = bf16[16,132,512]{2,1,0:T(8,128)(2,1)} async-done(((bf16[4,132,512]{2,1,0:T(8,128)(2,1)}), bf16[16,132,512]{2,1,0:T(8,128)(2,1)}) %all-gather.3.cloned.1.call-update) | async-done | bytes 2162704 | tf_op jit(solution)/shard_map/all_gather | solution.py:130
  74.5 0.9 slice.26
  75.4 0.4 reshape_reshape.3
  75.8 0.2 fusion.7
  76.0 0.2 copy.89
  76.2 0.2 copy.90
  76.4 0.1 compare_reduce_fusion
  76.6 0.7 fusion.1
  77.3 0.8 fusion
  78.1 0.0 collective-permute-done.2
  78.1 3.2 %copy.83.near_far_ref = bf16[8,1,4,36,768]{4,3,2,1,0:T(8,128)(2,1)} copy(bf16[8,1,4,36,768]{4,0,3,2,1:T(8,128)(2,1)} %collective-permute-done.2) | data formatting | bytes 3538944 | tf_op jit(solution)/shard_map/ppermute | solution.py:129
  81.3 17.8 %shard_map.86 = (f32[8,768,512]{2,1,0:T(8,128)}, f32[8,1,640]{2,1,0:T(1,128)}) custom-call(bf16[8,1,4,36,768]{4,3,2,1,0:T(8,128)(2,1)} %copy.80.own_ref, bf16[8,1,4,36,768]{4,3,2,1,0:T(8,128)(2,1)} %copy.81.far_ref, bf16[8,1,4,36,768]{4,3,2,1,0:T(8,128)(2,1)} %copy.82.near_ref, bf16[8,1,4,36,768]{4,3,2,1,0:T(8,128)(2,1)} %copy.83.near_far_ref, ...), custom_call_target="tpu_custom_call" | custom-call | tf_op jit(solution)/shard_map/pallas_call | solution.py:75
  99.0 0.8 reduce
  99.8 0.1 reshape.86
  100.0 0.6 gather_fusion.2
  100.5 0.1 bitcast_select_fusion
  100.6 0.7 reshape.118
  101.3 3.5 %all-to-all-start.1 = ((f32[16,1,288]{2,1,0:T(1,128)}), f32[16,1,288]{2,1,0:T(1,128)S(1)}, u32[]{:S(2)}, u32[]{:S(2)}) async-start(f32[16,1,288]{2,1,0:T(1,128)} %reshape.118), calls=%async_computation.1 | async-start | bytes 49152 | tf_op jit(solution)/shard_map/all_to_all | solution.py:161
  104.9 6.5 %all-to-all-done.1 = f32[16,1,288]{2,1,0:T(1,128)S(1)} async-done(((f32[16,1,288]{2,1,0:T(1,128)}), f32[16,1,288]{2,1,0:T(1,128)S(1)}, u32[]{:S(2)}, u32[]{:S(2)}) %all-to-all-start.1) | async-done | bytes 18464 | tf_op jit(solution)/shard_map/all_to_all | solution.py:161
  111.5 0.5 broadcast.97
  112.0 0.7 reduce.1
  112.7 0.1 reshape.119
  112.8 0.1 copy.86
  112.9 0.8 select_reduce_fusion
  113.7 0.7 select_reduce_fusion.1
  (29 shorter events, 0.2 us)
Async XLA Ops:
  7.2 7.1 %copy-start = (s32[4]{0:T(128)S(1)}, s32[4]{0:T(128)}, u32[]{:S(2)}) copy-start(s32[4]{0:T(128)} %constant.49.clone) | copy-start | bytes 52
  7.2 1.6 %copy-start.2 = (s32[128,8]{0,1:T(8,128)S(1)}, s32[128,8]{0,1:T(8,128)}, u32[]{:S(2)}) copy-start(s32[128,8]{0,1:T(8,128)} %param.9) | copy-start | bytes 12292
  7.2 1.6 %copy-start.3 = (bf16[128,8]{0,1:T(8,128)(2,1)S(1)}, bf16[128,8]{0,1:T(8,128)(2,1)}, u32[]{:S(2)}) copy-start(bf16[128,8]{0,1:T(8,128)(2,1)} %param.8) | copy-start | bytes 6148
  9.9 15.1 %copy-start.1 = (bf16[8,1,4,36,768]{4,2,3,1,0:T(4,128)(2,1)S(1)}, bf16[8,1,4,36,768]{4,2,3,1,0:T(4,128)(2,1)}, u32[]{:S(2)}) copy-start(bf16[8,1,4,36,768]{4,2,3,1,0:T(4,128)(2,1)} %param.10) | copy-start | bytes 5308420
  9.9 13.5 %all-to-all-start = ((bf16[132,4,512]{2,0,1:T(8,128)(2,1)}), bf16[132,4,512]{2,0,1:T(8,128)(2,1)S(1)}, u32[]{:S(2)}, u32[]{:S(2)}) async-start(bf16[132,4,512]{2,0,1:T(8,128)(2,1)} %pad_maximum_fusion), calls=%async_computation | async-start | bytes 1114112 | tf_op jit(solution)/shard_map/all_to_all | solution.py:121
  14.3 60.2 %all-gather.3.cloned.1.call-start = ((), (), s32[]{:S(2)}) async-start(), calls=%async_computation.2 | async-start | bytes 2785280 | tf_op jit(solution)/shard_map/all_gather | solution.py:130
  26.8 40.2 %collective-permute-start = (bf16[8,1,4,36,768]{4,0,3,2,1:T(8,128)(2,1)}, bf16[8,1,4,36,768]{4,0,3,2,1:T(8,128)(2,1)S(1)}, u32[]{:S(2)}, u32[]{:S(2)}) collective-permute-start(bf16[8,1,4,36,768]{4,0,3,2,1:T(8,128)(2,1)} %copy.76), channel_id=1, source_target_pairs={{0,2},{1,3},{2,0},{3,1},{4,6},{5,7},{6,4},{7,5},{8,10},{9,11},{10,... | collective-permute-start | bytes 5308424 | tf_op jit(solution)/shard_map/ppermute | solution.py:128
  27.1 41.8 %collective-permute-start.1 = (bf16[8,1,4,36,768]{4,0,3,2,1:T(8,128)(2,1)}, bf16[8,1,4,36,768]{4,0,3,2,1:T(8,128)(2,1)}, u32[]{:S(2)}, u32[]{:S(2)}) collective-permute-start(bf16[8,1,4,36,768]{4,0,3,2,1:T(8,128)(2,1)} %copy.76), channel_id=1, source_target_pairs={{0,1},{1,0},{2,3},{3,2},{4,5},{5,4},{6,7},{7,6},{8,9},{9,8},{10,11... | collective-permute-start | bytes 5308424 | tf_op jit(solution)/shard_map/ppermute | solution.py:127
  66.9 11.2 %collective-permute-start.2 = (bf16[8,1,4,36,768]{4,0,3,2,1:T(8,128)(2,1)S(1)}, bf16[8,1,4,36,768]{4,0,3,2,1:T(8,128)(2,1)}, u32[]{:S(2)}, u32[]{:S(2)}) collective-permute-start(bf16[8,1,4,36,768]{4,0,3,2,1:T(8,128)(2,1)S(1)} %collective-permute-done), channel_id=1, source_target_pairs={{0,1},{1,0},{2,3},{3,2},{4,5},{5,4},{6,7},{7,6},{8,9},{9,8},{10,11... | collective-permute-start | bytes 5308424 | tf_op jit(solution)/shard_map/ppermute | solution.py:129
  101.3 10.1 %all-to-all-start.1 = ((f32[16,1,288]{2,1,0:T(1,128)}), f32[16,1,288]{2,1,0:T(1,128)S(1)}, u32[]{:S(2)}, u32[]{:S(2)}) async-start(f32[16,1,288]{2,1,0:T(1,128)} %reshape.118), calls=%async_computation.1 | async-start | bytes 49152 | tf_op jit(solution)/shard_map/all_to_all | solution.py:161
Sparse Core Ops, SparseCore 0:
  25.1 49.3 all-gather.2

commit v9 on v8

--- a/solution.py
+++ b/solution.py
@@ -157,11 +157,8 @@
     slot_part = slot_part.transpose(1, 0, 2).reshape(peer_count, shards, local_count, capacity)
     piece_of = jnp.array([0, 2, 1, 3], jnp.int32)[jnp.arange(shards, dtype=jnp.int32) ^ my_dp]
     slot_part = jnp.take(slot_part, piece_of, axis=1)
-    send_back = slot_part.reshape(block_count, local_count, capacity)
-    returned = lax.all_to_all(
-        send_back, ("expert", "dp"), split_axis=0, concat_axis=0, tiled=True
-    )
-    returned = returned.reshape(peer_count, shards, local_count, capacity)
+    returned = lax.all_to_all(slot_part, "expert", split_axis=0, concat_axis=0, tiled=True)
+    returned = lax.all_to_all(returned, "dp", split_axis=1, concat_axis=1, tiled=True)
     slot_grad = jnp.sum(returned, axis=1).reshape(expert_count, capacity)
 
     own_hit = expert_ids[:, :, None] == jnp.arange(expert_count, dtype=jnp.int32)[None, None, :]

time: 122 us -> 131 us (1.074)
  starting transfers between devices: 8.25 us -> 13.2 us
  waiting for transfers between devices: 55.8 us -> 58.8 us
    all_to_all x1 -> x2, starting transfers between devices: 3.54 us -> 8.45 us  [the longest x1 5.2 us: per_device(): lax.all_to_all(slot_part, 'expert', split_axis=0, concat_axis=0, tiled=True)]
    all_to_all x1 -> x2, waiting for transfers between devices: 6.53 us -> 9.28 us  [the longest x1 5.48 us: per_device(): lax.all_to_all(slot_part, 'expert', split_axis=0, concat_axis=0, tiled=True)]
    ppermute x1, waiting for transfers between devices: 37.6 us -> 39.8 us  [per_device(): far = lax.ppermute(hidden_sent, 'dp', [(j, j ^ 2) for j in range(shards)])]
    all_gather x1, waiting for transfers between devices: 2.49 us -> 0.54 us  [per_device(): got = lax.all_gather(cols, 'expert', axis=0, tiled=False)]
    unnamed x14 -> x16, local copies, waits for them, and re-layouts: 4.04 us -> 4.91 us
  transfers between devices with their start and end apart: 6 -> 7, of which waited for: 4 -> 5; matrix products, arithmetic and copies ran while one was open for 10% -> 10% of each run, Pallas kernels for 0% -> 0%
where the time goes in v9:
time: 131 us
  waiting for transfers between devices  58.8 us (45%)
  local copies, waits for them, and re-layouts  19.1 us (15%)
  Pallas kernels  17.8 us (14%)
  between operations  14.3 us (11%)
  starting transfers between devices  13.2 us (10%)
  other arithmetic  6.57 us (5%)
    ppermute x1, waiting for transfers between devices, per_device(): far = lax.ppermute(hidden_sent, 'dp', [(j, j ^ 2) for j in range(shards)])  39.8 us
    pallas_call x1, Pallas kernels, expert_kernel(): pl.pallas_call(expert_body, grid=(local_count, steps), in_specs=[piece_sp...  17.8 us
    all_to_all x1, waiting for transfers between devices, per_device(): cols = lax.all_to_all(cols, 'dp', split_axis=1, concat_axis=0, tiled=True)  9.17 us
    all_to_all x1, waiting for transfers between devices, per_device(): lax.all_to_all(slot_part, 'expert', split_axis=0, concat_axis=0, tiled=True)  5.48 us
    all_to_all x1, starting transfers between devices, per_device(): lax.all_to_all(slot_part, 'expert', split_axis=0, concat_axis=0, tiled=True)  5.2 us
    unnamed x16, local copies, waits for them, and re-layouts  4.91 us
    all_to_all x1, starting transfers between devices, per_device(): cols = lax.all_to_all(cols, 'dp', split_axis=1, concat_axis=0, tiled=True)  4.34 us
    all_to_all x1, waiting for transfers between devices, per_device(): lax.all_to_all(returned, 'dp', split_axis=1, concat_axis=1, tiled=True)  3.8 us
  transfers between devices with their start and end apart: 7, of which 5 were waited for; matrix products, arithmetic and copies ran while one was open for 10% of the time, Pallas kernels for 0%

profile of v9, /device:TPU:0, one launch (start us, length us, event | category | flops | bytes accessed | tf_op | source)
XLA Modules:
  0.0 130.6 jit_solution(12174293362353834550)
XLA Ops:
  7.2 0.0 copy-start
  7.2 1.3 %copy.88 = bf16[128,2048]{0,1:T(8,128)(2,1)S(1)} copy(bf16[128,2048]{1,0:T(8,128)(2,1)} %param.7) | data formatting | bytes 1048576 | tf_op args[0]
  8.5 0.2 copy.90
  8.8 0.1 copy.89
  8.9 0.1 broadcast_in_dim.102
  9.1 0.9 pad_maximum_fusion
  9.9 4.3 %all-to-all-start = ((bf16[132,4,512]{2,0,1:T(8,128)(2,1)}), bf16[132,4,512]{2,0,1:T(8,128)(2,1)S(1)}, u32[]{:S(2)}, u32[]{:S(2)}) async-start(bf16[132,4,512]{2,0,1:T(8,128)(2,1)} %pad_maximum_fusion), calls=%async_computation | async-start | bytes 1114112 | tf_op jit(solution)/shard_map/all_to_all | solution.py:121
  14.3 9.2 %all-to-all-done = bf16[132,4,512]{2,0,1:T(8,128)(2,1)S(1)} async-done(((bf16[132,4,512]{2,0,1:T(8,128)(2,1)}), bf16[132,4,512]{2,0,1:T(8,128)(2,1)S(1)}, u32[]{:S(2)}, u32[]{:S(2)}) %all-to-all-start) | async-done | bytes 540704 | tf_op jit(solution)/shard_map/all_to_all | solution.py:121
  23.5 0.6 gather_fusion
  24.1 0.9 broadcast_select_fusion
  25.0 0.0 all-gather.3.cloned.1.call-update
  25.0 1.7 %copy.91 = bf16[8,1,4,36,768]{4,0,3,2,1:T(8,128)(2,1)} copy(bf16[8,1,4,36,768]{4,2,3,1,0:T(4,128)(2,1)S(1)} %copy-done.1) | data formatting | bytes 3538944 | tf_op jit(solution)/shard_map/optimization_barrier | solution.py:126
  26.8 0.4 collective-permute-start
  27.1 39.8 %collective-permute-done = bf16[8,1,4,36,768]{4,0,3,2,1:T(8,128)(2,1)S(1)} collective-permute-done((bf16[8,1,4,36,768]{4,0,3,2,1:T(8,128)(2,1)}, bf16[8,1,4,36,768]{4,0,3,2,1:T(8,128)(2,1)S(1)}, u32[]{:S(2)}, u32[]{:S(2)}) %collective-permute-start) | collective-permute-done | bytes 1769504 | tf_op jit(solution)/shard_map/ppermute | solution.py:128
  66.9 1.5 %copy.95.own_ref = bf16[8,1,4,36,768]{4,3,2,1,0:T(8,128)(2,1)} copy(bf16[8,1,4,36,768]{4,2,3,1,0:T(4,128)(2,1)S(1)} %copy-done.1) | data formatting | bytes 3538944 | tf_op args[3]
  68.5 0.6 gather_fusion.1
  69.2 1.7 %copy.96.far_ref = bf16[8,1,4,36,768]{4,3,2,1,0:T(8,128)(2,1)} copy(bf16[8,1,4,36,768]{4,0,3,2,1:T(8,128)(2,1)S(1)} %collective-permute-done) | data formatting | bytes 3538944 | tf_op jit(solution)/shard_map/ppermute | solution.py:128
  70.8 3.1 %copy.97.near_ref = bf16[8,1,4,36,768]{4,3,2,1,0:T(8,128)(2,1)} copy(bf16[8,1,4,36,768]{4,0,3,2,1:T(8,128)(2,1)} %collective-permute-done.1) | data formatting | bytes 3538944 | tf_op jit(solution)/shard_map/ppermute | solution.py:127
  73.9 0.5 all-gather.3.cloned.1.call-done.tok_ref
  74.5 0.9 slice.26
  75.4 0.4 reshape_reshape.3
  75.8 0.2 fusion.7
  76.0 0.2 copy.105
  76.2 0.2 copy.106
  76.4 0.1 compare_reduce_fusion
  76.6 0.7 fusion.1
  77.3 0.8 fusion
  78.1 3.2 %copy.98.near_far_ref = bf16[8,1,4,36,768]{4,3,2,1,0:T(8,128)(2,1)} copy(bf16[8,1,4,36,768]{4,0,3,2,1:T(8,128)(2,1)} %collective-permute-done.2) | data formatting | bytes 3538944 | tf_op jit(solution)/shard_map/ppermute | solution.py:129
  81.3 17.8 %shard_map.86 = (f32[8,768,512]{2,1,0:T(8,128)}, f32[8,1,640]{2,1,0:T(1,128)}) custom-call(bf16[8,1,4,36,768]{4,3,2,1,0:T(8,128)(2,1)} %copy.95.own_ref, bf16[8,1,4,36,768]{4,3,2,1,0:T(8,128)(2,1)} %copy.96.far_ref, bf16[8,1,4,36,768]{4,3,2,1,0:T(8,128)(2,1)} %copy.97.near_ref, bf16[8,1,4,36,768]{4,3,2,1,0:T(8,128)(2,1)} %copy.98.near_far_ref, ...), custom_call_target="tpu_custom_call" | custom-call | tf_op jit(solution)/shard_map/pallas_call | solution.py:75
  99.0 0.8 reduce
  99.8 0.1 reshape.80
  100.0 0.6 gather_fusion.2
  100.5 0.1 select_bitcast_fusion
  100.6 0.7 reshape.111
  101.3 5.2 %all-to-all-start.1 = ((f32[4,1,1152]{2,1,0:T(1,128)}), f32[4,1,1152]{2,1,0:T(1,128)S(1)}, u32[]{:S(2)}, u32[]{:S(2)}) async-start(f32[4,1,1152]{2,1,0:T(1,128)} %reshape.111), calls=%async_computation.1 | async-start | bytes 36864 | tf_op jit(solution)/shard_map/all_to_all | solution.py:160
  106.5 0.1 convolution_convert_fusion.1
  106.7 5.5 %all-to-all-done.1 = f32[4,1,1152]{2,1,0:T(1,128)S(1)} async-done(((f32[4,1,1152]{2,1,0:T(1,128)}), f32[4,1,1152]{2,1,0:T(1,128)S(1)}, u32[]{:S(2)}, u32[]{:S(2)}) %all-to-all-start.1) | async-done | bytes 18464 | tf_op jit(solution)/shard_map/all_to_all | solution.py:160
  112.1 0.5 broadcast.99
  112.7 0.7 reduce.1
  113.4 0.1 reshape.112
  113.5 0.7 reshape.113
  114.2 3.3 %all-to-all-start.2 = ((f32[4,1,1152]{2,1,0:T(1,128)}), f32[4,1,1152]{2,1,0:T(1,128)S(1)}, u32[]{:S(2)}, u32[]{:S(2)}) async-start(f32[4,1,1152]{2,1,0:T(1,128)} %reshape.113), calls=%async_computation.2 | async-start | bytes 36864 | tf_op jit(solution)/shard_map/all_to_all | solution.py:161
  117.5 3.8 %all-to-all-done.2 = f32[4,1,1152]{2,1,0:T(1,128)S(1)} async-done(((f32[4,1,1152]{2,1,0:T(1,128)}), f32[4,1,1152]{2,1,0:T(1,128)S(1)}, u32[]{:S(2)}, u32[]{:S(2)}) %all-to-all-start.2) | async-done | bytes 18464 | tf_op jit(solution)/shard_map/all_to_all | solution.py:161
  121.3 0.7 reduce.2
  122.0 0.1 reshape.114
  122.1 0.1 copy.102
  122.2 0.8 select_reduce_fusion
  123.1 0.7 select_reduce_fusion.1
  (33 shorter events, 0.2 us)
Async XLA Ops:
  7.2 7.1 %copy-start = (s32[4]{0:T(128)S(1)}, s32[4]{0:T(128)}, u32[]{:S(2)}) copy-start(s32[4]{0:T(128)} %constant.49.clone) | copy-start | bytes 52
  7.2 1.6 %copy-start.2 = (s32[128,8]{0,1:T(8,128)S(1)}, s32[128,8]{0,1:T(8,128)}, u32[]{:S(2)}) copy-start(s32[128,8]{0,1:T(8,128)} %param.9) | copy-start | bytes 12292
  7.2 1.6 %copy-start.3 = (bf16[128,8]{0,1:T(8,128)(2,1)S(1)}, bf16[128,8]{0,1:T(8,128)(2,1)}, u32[]{:S(2)}) copy-start(bf16[128,8]{0,1:T(8,128)(2,1)} %param.8) | copy-start | bytes 6148
  9.9 15.1 %copy-start.1 = (bf16[8,1,4,36,768]{4,2,3,1,0:T(4,128)(2,1)S(1)}, bf16[8,1,4,36,768]{4,2,3,1,0:T(4,128)(2,1)}, u32[]{:S(2)}) copy-start(bf16[8,1,4,36,768]{4,2,3,1,0:T(4,128)(2,1)} %param.10) | copy-start | bytes 5308420
  9.9 13.5 %all-to-all-start = ((bf16[132,4,512]{2,0,1:T(8,128)(2,1)}), bf16[132,4,512]{2,0,1:T(8,128)(2,1)S(1)}, u32[]{:S(2)}, u32[]{:S(2)}) async-start(bf16[132,4,512]{2,0,1:T(8,128)(2,1)} %pad_maximum_fusion), calls=%async_computation | async-start | bytes 1114112 | tf_op jit(solution)/shard_map/all_to_all | solution.py:121
  14.3 60.2 %all-gather.3.cloned.1.call-start = ((), (), s32[]{:S(2)}) async-start(), calls=%async_computation.3 | async-start | bytes 2785280 | tf_op jit(solution)/shard_map/all_gather | solution.py:130
  26.8 40.2 %collective-permute-start = (bf16[8,1,4,36,768]{4,0,3,2,1:T(8,128)(2,1)}, bf16[8,1,4,36,768]{4,0,3,2,1:T(8,128)(2,1)S(1)}, u32[]{:S(2)}, u32[]{:S(2)}) collective-permute-start(bf16[8,1,4,36,768]{4,0,3,2,1:T(8,128)(2,1)} %copy.91), channel_id=1, source_target_pairs={{0,2},{1,3},{2,0},{3,1},{4,6},{5,7},{6,4},{7,5},{8,10},{9,11},{10,... | collective-permute-start | bytes 5308424 | tf_op jit(solution)/shard_map/ppermute | solution.py:128
  27.1 43.7 %collective-permute-start.1 = (bf16[8,1,4,36,768]{4,0,3,2,1:T(8,128)(2,1)}, bf16[8,1,4,36,768]{4,0,3,2,1:T(8,128)(2,1)}, u32[]{:S(2)}, u32[]{:S(2)}) collective-permute-start(bf16[8,1,4,36,768]{4,0,3,2,1:T(8,128)(2,1)} %copy.91), channel_id=1, source_target_pairs={{0,1},{1,0},{2,3},{3,2},{4,5},{5,4},{6,7},{7,6},{8,9},{9,8},{10,11... | collective-permute-start | bytes 5308424 | tf_op jit(solution)/shard_map/ppermute | solution.py:127
  66.9 11.2 %collective-permute-start.2 = (bf16[8,1,4,36,768]{4,0,3,2,1:T(8,128)(2,1)S(1)}, bf16[8,1,4,36,768]{4,0,3,2,1:T(8,128)(2,1)}, u32[]{:S(2)}, u32[]{:S(2)}) collective-permute-start(bf16[8,1,4,36,768]{4,0,3,2,1:T(8,128)(2,1)S(1)} %collective-permute-done), channel_id=1, source_target_pairs={{0,1},{1,0},{2,3},{3,2},{4,5},{5,4},{6,7},{7,6},{8,9},{9,8},{10,11... | collective-permute-start | bytes 5308424 | tf_op jit(solution)/shard_map/ppermute | solution.py:129
  101.3 10.8 %all-to-all-start.1 = ((f32[4,1,1152]{2,1,0:T(1,128)}), f32[4,1,1152]{2,1,0:T(1,128)S(1)}, u32[]{:S(2)}, u32[]{:S(2)}) async-start(f32[4,1,1152]{2,1,0:T(1,128)} %reshape.111), calls=%async_computation.1 | async-start | bytes 36864 | tf_op jit(solution)/shard_map/all_to_all | solution.py:160
  114.2 7.1 %all-to-all-start.2 = ((f32[4,1,1152]{2,1,0:T(1,128)}), f32[4,1,1152]{2,1,0:T(1,128)S(1)}, u32[]{:S(2)}, u32[]{:S(2)}) async-start(f32[4,1,1152]{2,1,0:T(1,128)} %reshape.113), calls=%async_computation.2 | async-start | bytes 36864 | tf_op jit(solution)/shard_map/all_to_all | solution.py:161
Sparse Core Ops, SparseCore 0:
  25.1 49.3 all-gather.2

commit v10 on v8

--- a/solution.py
+++ b/solution.py
@@ -10,9 +10,10 @@
                 wg_ref, slot_ref, h_scr, s_scr, g_scr):
     expert = pl.program_id(0)
     chunk = pl.program_id(1)
-    sources, capacity, hidden_width = own_ref.shape[2:]
     blocks = sel_ref.shape[0]
     padded = s_scr.shape[0] // blocks
+    sources = blocks // 4
+    capacity = own_ref.shape[0] // sources
     col_width = tok_ref.shape[2]
     pieces = (own_ref, far_ref, near_ref, near_far_ref)
 
@@ -23,7 +24,7 @@
     for src in range(sources):
         for j, ref in enumerate(pieces):
             row = (src * len(pieces) + j) * padded
-            h_scr[row:row + capacity, :] = ref[0, 0, src].astype(jnp.float32)
+            h_scr[row:row + capacity, :] = ref[src * capacity:(src + 1) * capacity, :].astype(jnp.float32)
 
     slot_iota = lax.broadcasted_iota(jnp.int32, (padded, tok_ref.shape[1]), 0)
     for blk in range(blocks):
@@ -56,8 +57,8 @@
     slot_ref[0] = jnp.transpose(wide)[0:1, :]
 
 
-def expert_kernel(pieces, tokens, slot_row, gate_row, weight, padded):
-    local_count, _, source_count, capacity, hidden_width = pieces[0].shape
+def expert_kernel(pieces, tokens, slot_row, gate_row, weight, padded, shape):
+    local_count, _, source_count, capacity, hidden_width = shape
     col_width = tokens.shape[2]
     block_count, _, _, tok_rows = slot_row.shape
     per_source = block_count // source_count
@@ -70,7 +71,7 @@
     blocks = chunk * per_source
     rows = blocks * padded
     piece_spec = pl.BlockSpec(
-        (1, 1, chunk, capacity, hidden_width), lambda l, r: (l, 0, r, 0, 0)
+        (chunk * capacity, hidden_width), lambda l, r: (l * steps + r, 0)
     )
     return pl.pallas_call(
         expert_body,
@@ -123,6 +124,8 @@
     piece_xor = jnp.array([0, 2, 1, 3], jnp.int32)
     cols = jnp.take(cols, piece_xor ^ my_dp, axis=0)
 
+    hidden_shape = hidden.shape
+    hidden = hidden.reshape(-1, hidden_width)
     hidden_sent, cols = lax.optimization_barrier((hidden, cols))
     near = lax.ppermute(hidden_sent, "dp", [(j, j ^ 1) for j in range(shards)])
     far = lax.ppermute(hidden_sent, "dp", [(j, j ^ 2) for j in range(shards)])
@@ -151,7 +154,7 @@
     slot_row = jnp.where(chose_t, rank_t, -1)[:, :, None, :]
     gate_row = gate_t[:, :, None, :]
     weight_grad, slot_part = expert_kernel(
-        (hidden, far, near, near_far), got, slot_row, gate_row, down_weight, padded
+        (hidden, far, near, near_far), got, slot_row, gate_row, down_weight, padded, hidden_shape
     )
     slot_part = slot_part.reshape(local_count, block_count, padded)[:, :, :capacity]
     slot_part = slot_part.transpose(1, 0, 2).reshape(peer_count, shards, local_count, capacity)

time: 122 us -> 118 us (0.967)
  local copies, waits for them, and re-layouts: 18.3 us -> 10.2 us
  waiting for transfers between devices: 55.8 us -> 60.7 us
    ppermute x3 -> x0, local copies, waits for them, and re-layouts: 7.94 us -> none  [the longest x1 3.18 us: per_device(): near_far = lax.ppermute(far, 'dp', [(j, j ^ 1) for j in range(shards)])]
    all_gather x1, waiting for transfers between devices: 2.49 us -> 9.04 us  [per_device(): got = lax.all_gather(cols, 'expert', axis=0, tiled=False)]
    all_to_all x1, waiting for transfers between devices: 9.17 us -> 6.02 us  [per_device(): cols = lax.all_to_all(cols, 'dp', split_axis=1, concat_axis=0, tiled=True)]
    optimization_barrier x1 -> x0, local copies, waits for them, and re-layouts: 1.75 us -> none  [per_device(): hidden_sent, cols = lax.optimization_barrier((hidden, cols))]
    ppermute x1, waiting for transfers between devices: 37.6 us -> 39 us  [per_device(): far = lax.ppermute(hidden_sent, 'dp', [(j, j ^ 2) for j in range(shards)])]
    reshape x0 -> x1, local copies, waits for them, and re-layouts: none -> 1.39 us  [per_device(): hidden = hidden.reshape(-1, hidden_width)]
  transfers between devices with their start and end apart: 6 -> 6, of which waited for: 4 -> 4; matrix products, arithmetic and copies ran while one was open for 10% -> 7% of each run, Pallas kernels for 0% -> 0%
where the time goes in v10:
time: 118 us
  waiting for transfers between devices  60.7 us (51%)
  Pallas kernels  17.8 us (15%)
  between operations  14.3 us (12%)
  local copies, waits for them, and re-layouts  10.2 us (9%)
  starting transfers between devices  8.19 us (7%)
  other arithmetic  5.89 us (5%)
    ppermute x1, waiting for transfers between devices, per_device(): far = lax.ppermute(hidden_sent, 'dp', [(j, j ^ 2) for j in range(shards)])  39 us
    pallas_call x1, Pallas kernels, expert_kernel(): pl.pallas_call(expert_body, grid=(local_count, steps), in_specs=[piece_sp...  17.8 us
    all_gather x1, waiting for transfers between devices, per_device(): got = lax.all_gather(cols, 'expert', axis=0, tiled=False)  9.04 us
    all_to_all x1, waiting for transfers between devices, per_device(): lax.all_to_all(send_back, ('expert', 'dp'), split_axis=0, concat_axis=0,...  6.53 us
    all_to_all x1, waiting for transfers between devices, per_device(): cols = lax.all_to_all(cols, 'dp', split_axis=1, concat_axis=0, tiled=True)  6.02 us
    unnamed x14, local copies, waits for them, and re-layouts  4.24 us
    all_to_all x1, starting transfers between devices, per_device(): cols = lax.all_to_all(cols, 'dp', split_axis=1, concat_axis=0, tiled=True)  4.21 us
    all_to_all x1, starting transfers between devices, per_device(): lax.all_to_all(send_back, ('expert', 'dp'), split_axis=0, concat_axis=0,...  3.55 us
  transfers between devices with their start and end apart: 6, of which 4 were waited for; matrix products, arithmetic and copies ran while one was open for 7% of the time, Pallas kernels for 0%

profile of v10, /device:TPU:0, one launch (start us, length us, event | category | flops | bytes accessed | tf_op | source)
XLA Modules:
  0.0 117.9 jit_solution(9925632820321345994)
XLA Ops:
  7.2 0.0 copy-start.2
  7.2 0.0 copy-start.3
  7.2 1.3 %copy.53 = bf16[128,2048]{0,1:T(8,128)(2,1)S(1)} copy(bf16[128,2048]{1,0:T(8,128)(2,1)} %param.7) | data formatting | bytes 1048576 | tf_op args[0]
  8.5 0.2 copy.55
  8.7 0.0 copy-done.2
  8.8 0.1 copy.54
  8.9 0.1 broadcast_in_dim.106
  9.0 0.9 pad_maximum_fusion
  9.9 4.2 %all-to-all-start = ((bf16[132,4,512]{2,0,1:T(8,128)(2,1)}), bf16[132,4,512]{2,0,1:T(8,128)(2,1)S(1)}, u32[]{:S(2)}, u32[]{:S(2)}) async-start(bf16[132,4,512]{2,0,1:T(8,128)(2,1)} %pad_maximum_fusion), calls=%async_computation | async-start | bytes 1114112 | tf_op jit(solution)/shard_map/all_to_all | solution.py:122
  14.1 1.7 %copy.52 = bf16[8,1,4,36,768]{4,3,2,0,1:T(8,128)(2,1)S(1)} copy(bf16[8,1,4,36,768]{4,2,3,1,0:T(4,128)(2,1)} %param.10) | data formatting | bytes 3538944 | tf_op args[3]
  15.8 0.0 copy-start
  15.9 1.4 %reshape.86.own_ref = bf16[1152,768]{1,0:T(8,128)(2,1)} reshape(bf16[8,1,4,36,768]{4,3,2,0,1:T(8,128)(2,1)S(1)} %copy.52) | data formatting | bytes 3538944 | tf_op jit(solution)/shard_map/reshape | solution.py:128
  17.3 6.0 %all-to-all-done = bf16[132,4,512]{2,0,1:T(8,128)(2,1)S(1)} async-done(((bf16[132,4,512]{2,0,1:T(8,128)(2,1)}), bf16[132,4,512]{2,0,1:T(8,128)(2,1)S(1)}, u32[]{:S(2)}, u32[]{:S(2)}) %all-to-all-start) | async-done | bytes 540704 | tf_op jit(solution)/shard_map/all_to_all | solution.py:122
  23.3 0.6 gather_fusion
  23.9 0.9 broadcast_select_fusion
  24.8 0.0 all-gather.3.cloned.1.call-update
  24.8 0.4 collective-permute-start
  25.3 0.6 gather_fusion.1
  25.9 0.0 collective-permute-start.1
  25.9 39.0 %collective-permute-done.far_ref = bf16[1152,768]{1,0:T(8,128)(2,1)} collective-permute-done((bf16[1152,768]{1,0:T(8,128)(2,1)S(1)}, bf16[1152,768]{1,0:T(8,128)(2,1)}, u32[]{:S(2)}, u32[]{:S(2)}) %collective-permute-start) | collective-permute-done | bytes 1769504 | tf_op jit(solution)/shard_map/ppermute | solution.py:131
  65.0 0.0 collective-permute-start.2
  65.0 0.1 broadcast_in_dim.119
  65.1 0.1 convolution_convert_fusion.1
  65.3 9.0 %all-gather.3.cloned.1.call-done.tok_ref = bf16[16,132,512]{2,1,0:T(8,128)(2,1)} async-done(((bf16[4,132,512]{2,1,0:T(8,128)(2,1)}), bf16[16,132,512]{2,1,0:T(8,128)(2,1)}) %all-gather.3.cloned.1.call-update) | async-done | bytes 2162704 | tf_op jit(solution)/shard_map/all_gather | solution.py:133
  74.3 0.9 slice.26
  75.2 0.4 reshape_reshape.3
  75.6 0.2 fusion.7
  75.9 0.2 copy.63
  76.1 0.2 copy.64
  76.3 0.1 compare_reduce_fusion
  76.4 0.7 fusion.1
  77.2 0.8 fusion
  77.9 0.0 collective-permute-done.1.near_ref
  77.9 0.0 collective-permute-done.2.near_far_ref
  77.9 17.8 %shard_map.86 = (f32[8,768,512]{2,1,0:T(8,128)}, f32[8,1,640]{2,1,0:T(1,128)}) custom-call(bf16[1152,768]{1,0:T(8,128)(2,1)} %reshape.86.own_ref, bf16[1152,768]{1,0:T(8,128)(2,1)} %collective-permute-done.far_ref, bf16[1152,768]{1,0:T(8,128)(2,1)} %collective-permute-done.1.near_ref, bf16[1152,768]{1,0:T(8,128)(2,1)} %collective-permute-done.2.near_far_ref, ...), custom_call_target="tpu_custom_call" | custom-call | tf_op jit(solution)/shard_map/pallas_call | solution.py:76
  95.7 0.8 reduce
  96.5 0.1 reshape.90
  96.6 0.6 gather_fusion.2
  97.2 0.1 bitcast_select_fusion
  97.3 0.7 reshape.122
  98.0 3.5 %all-to-all-start.1 = ((f32[16,1,288]{2,1,0:T(1,128)}), f32[16,1,288]{2,1,0:T(1,128)S(1)}, u32[]{:S(2)}, u32[]{:S(2)}) async-start(f32[16,1,288]{2,1,0:T(1,128)} %reshape.122), calls=%async_computation.1 | async-start | bytes 49152 | tf_op jit(solution)/shard_map/all_to_all | solution.py:164
  101.6 6.5 %all-to-all-done.1 = f32[16,1,288]{2,1,0:T(1,128)S(1)} async-done(((f32[16,1,288]{2,1,0:T(1,128)}), f32[16,1,288]{2,1,0:T(1,128)S(1)}, u32[]{:S(2)}, u32[]{:S(2)}) %all-to-all-start.1) | async-done | bytes 18464 | tf_op jit(solution)/shard_map/all_to_all | solution.py:164
  108.1 0.5 broadcast.97
  108.6 0.7 reduce.1
  109.3 0.1 reshape.123
  109.4 0.1 copy.60
  109.5 0.8 select_reduce_fusion
  110.4 0.7 select_reduce_fusion.1
  (26 shorter events, 0.2 us)
Async XLA Ops:
  7.2 1.6 %copy-start.2 = (s32[128,8]{0,1:T(8,128)S(1)}, s32[128,8]{0,1:T(8,128)}, u32[]{:S(2)}) copy-start(s32[128,8]{0,1:T(8,128)} %param.9) | copy-start | bytes 12292
  7.2 1.6 %copy-start.3 = (bf16[128,8]{0,1:T(8,128)(2,1)S(1)}, bf16[128,8]{0,1:T(8,128)(2,1)}, u32[]{:S(2)}) copy-start(bf16[128,8]{0,1:T(8,128)(2,1)} %param.8) | copy-start | bytes 6148
  9.9 13.4 %all-to-all-start = ((bf16[132,4,512]{2,0,1:T(8,128)(2,1)}), bf16[132,4,512]{2,0,1:T(8,128)(2,1)S(1)}, u32[]{:S(2)}, u32[]{:S(2)}) async-start(bf16[132,4,512]{2,0,1:T(8,128)(2,1)} %pad_maximum_fusion), calls=%async_computation | async-start | bytes 1114112 | tf_op jit(solution)/shard_map/all_to_all | solution.py:122
  14.1 60.2 %all-gather.3.cloned.1.call-start = ((), (), s32[]{:S(2)}) async-start(), calls=%async_computation.2 | async-start | bytes 2785280 | tf_op jit(solution)/shard_map/all_gather | solution.py:133
  15.8 1.4 %copy-start = (s32[4]{0:T(128)S(1)}, s32[4]{0:T(128)}, u32[]{:S(2)}) copy-start(s32[4]{0:T(128)} %constant.49.clone) | copy-start | bytes 52
  17.2 7.6 %copy-start.1 = (bf16[1152,768]{1,0:T(8,128)(2,1)S(1)}, bf16[1152,768]{1,0:T(8,128)(2,1)}, u32[]{:S(2)}) copy-start(bf16[1152,768]{1,0:T(8,128)(2,1)} %reshape.86.own_ref) | copy-start | bytes 5308420
  24.8 40.1 %collective-permute-start = (bf16[1152,768]{1,0:T(8,128)(2,1)S(1)}, bf16[1152,768]{1,0:T(8,128)(2,1)}, u32[]{:S(2)}, u32[]{:S(2)}) collective-permute-start(bf16[1152,768]{1,0:T(8,128)(2,1)S(1)} %copy-done.1), channel_id=1, source_target_pairs={{0,2},{1,3},{2,0},{3,1},{4,6},{5,7},{6,4},{7,5},{8,10},{9,11},{10,... | collective-permute-start | bytes 5308424 | tf_op jit(solution)/shard_map/ppermute | solution.py:131
  25.9 52.0 %collective-permute-start.1 = (bf16[1152,768]{1,0:T(8,128)(2,1)S(1)}, bf16[1152,768]{1,0:T(8,128)(2,1)}, u32[]{:S(2)}, u32[]{:S(2)}) collective-permute-start(bf16[1152,768]{1,0:T(8,128)(2,1)S(1)} %copy-done.1), channel_id=1, source_target_pairs={{0,1},{1,0},{2,3},{3,2},{4,5},{5,4},{6,7},{7,6},{8,9},{9,8},{10,11... | collective-permute-start | bytes 5308424 | tf_op jit(solution)/shard_map/ppermute | solution.py:130
  65.0 13.0 %collective-permute-start.2 = (bf16[1152,768]{1,0:T(8,128)(2,1)}, bf16[1152,768]{1,0:T(8,128)(2,1)}, u32[]{:S(2)}, u32[]{:S(2)}) collective-permute-start(bf16[1152,768]{1,0:T(8,128)(2,1)} %collective-permute-done.far_ref), channel_id=1, source_target_pairs={{0,1},{1,0},{2,3},{3,2},{4,5},{5,4},{6,7},{7,6},{8,9},{9,8},{10,11... | collective-permute-start | bytes 5308424 | tf_op jit(solution)/shard_map/ppermute | solution.py:132
  98.0 10.1 %all-to-all-start.1 = ((f32[16,1,288]{2,1,0:T(1,128)}), f32[16,1,288]{2,1,0:T(1,128)S(1)}, u32[]{:S(2)}, u32[]{:S(2)}) async-start(f32[16,1,288]{2,1,0:T(1,128)} %reshape.122), calls=%async_computation.1 | async-start | bytes 49152 | tf_op jit(solution)/shard_map/all_to_all | solution.py:164
Sparse Core Ops, SparseCore 0:
  24.9 49.3 all-gather.2

commit v11 on v10

--- a/solution.py
+++ b/solution.py
@@ -21,10 +21,12 @@
     def _():
         h_scr[...] = jnp.zeros(h_scr.shape, h_scr.dtype)
 
+    my_dp = lax.axis_index("dp")
     for src in range(sources):
         for j, ref in enumerate(pieces):
-            row = (src * len(pieces) + j) * padded
-            h_scr[row:row + capacity, :] = ref[src * capacity:(src + 1) * capacity, :].astype(jnp.float32)
+            replica = my_dp ^ (0, 2, 1, 3)[j]
+            row = pl.multiple_of((src * len(pieces) + replica) * padded, 8)
+            h_scr[pl.ds(row, capacity), :] = ref[src * capacity:(src + 1) * capacity, :].astype(jnp.float32)
 
     slot_iota = lax.broadcasted_iota(jnp.int32, (padded, tok_ref.shape[1]), 0)
     for blk in range(blocks):
@@ -121,8 +123,6 @@
     cols = jnp.concatenate([cols, jnp.broadcast_to(meta, (meta_rows, shards, col_width))], axis=0)
     cols = lax.all_to_all(cols, "dp", split_axis=1, concat_axis=0, tiled=True)
     cols = cols.reshape(shards, tok_rows + meta_rows, col_width)
-    piece_xor = jnp.array([0, 2, 1, 3], jnp.int32)
-    cols = jnp.take(cols, piece_xor ^ my_dp, axis=0)
 
     hidden_shape = hidden.shape
     hidden = hidden.reshape(-1, hidden_width)
@@ -158,8 +158,6 @@
     )
     slot_part = slot_part.reshape(local_count, block_count, padded)[:, :, :capacity]
     slot_part = slot_part.transpose(1, 0, 2).reshape(peer_count, shards, local_count, capacity)
-    piece_of = jnp.array([0, 2, 1, 3], jnp.int32)[jnp.arange(shards, dtype=jnp.int32) ^ my_dp]
-    slot_part = jnp.take(slot_part, piece_of, axis=1)
     send_back = slot_part.reshape(block_count, local_count, capacity)
     returned = lax.all_to_all(
         send_back, ("expert", "dp"), split_axis=0, concat_axis=0, tiled=True

time: 118 us -> 120 us (1.017)
    gather x4 -> x0, local copies, waits for them, and re-layouts: 1.78 us -> none  [the longest x1 0.64 us: per_device(): jnp.array([0, 2, 1, 3], jnp.int32)]
    unnamed x14 -> x13, local copies, waits for them, and re-layouts: 4.24 us -> 5.04 us
  transfers between devices with their start and end apart: 6 -> 6, of which waited for: 4 -> 4; matrix products, arithmetic and copies ran while one was open for 7% -> 6% of each run, Pallas kernels for 0% -> 0%
where the time goes in v11:
time: 120 us; the launch traced here: 119 us
  waiting for transfers between devices  61.5 us (51%)
  Pallas kernels  18.6 us (16%)
  between operations  14.2 us (12%)
  local copies, waits for them, and re-layouts  10.3 us (9%)
  starting transfers between devices  8.17 us (7%)
  other arithmetic  5.55 us (5%)
    ppermute x1, waiting for transfers between devices, per_device(): far = lax.ppermute(hidden_sent, 'dp', [(j, j ^ 2) for j in range(shards)])  39.8 us
    pallas_call x1, Pallas kernels, expert_kernel(): pl.pallas_call(expert_body, grid=(local_count, steps), in_specs=[piece_sp...  18.6 us
    all_gather x1, waiting for transfers between devices, per_device(): got = lax.all_gather(cols, 'expert', axis=0, tiled=False)  9.06 us
    all_to_all x1, waiting for transfers between devices, per_device(): lax.all_to_all(send_back, ('expert', 'dp'), split_axis=0, concat_axis=0,...  6.53 us
    all_to_all x1, waiting for transfers between devices, per_device(): cols = lax.all_to_all(cols, 'dp', split_axis=1, concat_axis=0, tiled=True)  6.05 us
    unnamed x13, local copies, waits for them, and re-layouts  5.04 us
    all_to_all x1, starting transfers between devices, per_device(): cols = lax.all_to_all(cols, 'dp', split_axis=1, concat_axis=0, tiled=True)  4.21 us
    all_to_all x1, starting transfers between devices, per_device(): lax.all_to_all(send_back, ('expert', 'dp'), split_axis=0, concat_axis=0,...  3.53 us
  transfers between devices with their start and end apart: 6, of which 4 were waited for; matrix products, arithmetic and copies ran while one was open for 6% of the time, Pallas kernels for 0%

profile of v11, /device:TPU:0, one launch (start us, length us, event | category | flops | bytes accessed | tf_op | source)
XLA Modules:
  0.0 119.2 jit_solution(12840723200041477247)
XLA Ops:
  7.2 0.7 convert_element_type.19
  7.9 0.7 pad_maximum_fusion.1
  8.5 0.1 copy.59
  8.7 0.1 broadcast_in_dim.78
  8.8 0.2 copy.60
  9.0 1.3 %copy.58 = bf16[128,2048]{0,1:T(8,128)(2,1)S(1)} copy(bf16[128,2048]{1,0:T(8,128)(2,1)} %param.5) | data formatting | bytes 1048576 | tf_op args[0]
  10.3 0.1 broadcast_in_dim.79
  10.4 0.2 pad_maximum_fusion
  10.6 1.2 copy.61
  11.7 4.2 %all-to-all-start = ((bf16[132,4,512]{2,0,1:T(8,128)(2,1)}), bf16[132,4,512]{2,0,1:T(8,128)(2,1)S(1)}, u32[]{:S(2)}, u32[]{:S(2)}) async-start(bf16[132,4,512]{2,0,1:T(8,128)(2,1)} %copy.61), calls=%async_computation | async-start | bytes 1114112 | tf_op jit(solution)/shard_map/all_to_all | solution.py:124
  16.0 0.0 all-gather.3.cloned.1.call-start
  16.0 1.7 %copy.57 = bf16[8,1,4,36,768]{4,3,2,0,1:T(8,128)(2,1)S(1)} copy(bf16[8,1,4,36,768]{4,2,3,1,0:T(4,128)(2,1)} %param.8) | data formatting | bytes 3538944 | tf_op args[3]
  17.7 0.0 copy-start.2
  17.7 1.4 %reshape.41.own_ref = bf16[1152,768]{1,0:T(8,128)(2,1)} reshape(bf16[8,1,4,36,768]{4,3,2,0,1:T(8,128)(2,1)S(1)} %copy.57) | data formatting | bytes 3538944 | tf_op jit(solution)/shard_map/reshape | solution.py:128
  19.1 6.0 %all-to-all-done = bf16[132,4,512]{2,0,1:T(8,128)(2,1)S(1)} async-done(((bf16[132,4,512]{2,0,1:T(8,128)(2,1)}), bf16[132,4,512]{2,0,1:T(8,128)(2,1)S(1)}, u32[]{:S(2)}, u32[]{:S(2)}) %all-to-all-start) | async-done | bytes 540704 | tf_op jit(solution)/shard_map/all_to_all | solution.py:124
  25.1 0.0 copy-start
  25.2 0.8 copy-done
  26.0 0.0 all-gather.3.cloned.1.call-update
  26.0 0.4 collective-permute-start
  26.4 0.0 collective-permute-start.1
  26.4 39.8 %collective-permute-done.far_ref = bf16[1152,768]{1,0:T(8,128)(2,1)S(1)} collective-permute-done((bf16[1152,768]{1,0:T(8,128)(2,1)}, bf16[1152,768]{1,0:T(8,128)(2,1)S(1)}, u32[]{:S(2)}, u32[]{:S(2)}) %collective-permute-start) | collective-permute-done | bytes 1769504 | tf_op jit(solution)/shard_map/ppermute | solution.py:131
  66.2 0.0 collective-permute-start.2
  66.2 0.0 copy-done.2
  66.3 0.1 convolution_convert_fusion.1
  66.4 9.1 %all-gather.3.cloned.1.call-done.tok_ref = bf16[16,132,512]{2,1,0:T(8,128)(2,1)} async-done(((bf16[4,132,512]{2,1,0:T(8,128)(2,1)}), bf16[16,132,512]{2,1,0:T(8,128)(2,1)}) %all-gather.3.cloned.1.call-update) | async-done | bytes 2162704 | tf_op jit(solution)/shard_map/all_gather | solution.py:133
  75.5 0.9 slice.20
  76.4 0.4 reshape_reshape.3
  76.8 0.2 fusion.5
  77.0 0.2 copy.71
  77.2 0.2 copy.72
  77.4 0.0 copy-done.1
  77.4 0.1 compare_reduce_fusion
  77.6 0.7 fusion.1
  78.3 0.8 fusion
  79.1 0.0 collective-permute-done.1.near_ref
  79.1 0.0 collective-permute-done.2.near_far_ref
  79.1 18.6 %shard_map.68 = (f32[8,768,512]{2,1,0:T(8,128)}, f32[8,1,640]{2,1,0:T(1,128)}) custom-call(bf16[1152,768]{1,0:T(8,128)(2,1)} %reshape.41.own_ref, bf16[1152,768]{1,0:T(8,128)(2,1)} %copy-done.1, bf16[1152,768]{1,0:T(8,128)(2,1)} %collective-permute-done.1.near_ref, bf16[1152,768]{1,0:T(8,128)(2,1)} %collective-permute-done.2.near_far_ref, ...), custom_call_target="tpu_custom_call" | custom-call | tf_op jit(solution)/shard_map/pallas_call | solution.py:78
  97.7 0.8 reduce
  98.5 0.1 reshape.45
  98.6 0.7 reshape.51
  99.3 3.5 %all-to-all-start.1 = ((f32[16,1,288]{2,1,0:T(1,128)}), f32[16,1,288]{2,1,0:T(1,128)S(1)}, u32[]{:S(2)}, u32[]{:S(2)}) async-start(f32[16,1,288]{2,1,0:T(1,128)} %reshape.51), calls=%async_computation.1 | async-start | bytes 49152 | tf_op jit(solution)/shard_map/all_to_all | solution.py:162
  102.9 6.5 %all-to-all-done.1 = f32[16,1,288]{2,1,0:T(1,128)S(1)} async-done(((f32[16,1,288]{2,1,0:T(1,128)}), f32[16,1,288]{2,1,0:T(1,128)S(1)}, u32[]{:S(2)}, u32[]{:S(2)}) %all-to-all-start.1) | async-done | bytes 18464 | tf_op jit(solution)/shard_map/all_to_all | solution.py:162
  109.4 0.5 broadcast.16
  109.9 0.7 reduce.1
  110.7 0.1 reshape.52
  110.8 0.1 copy.67
  110.8 0.8 select_reduce_fusion
  111.7 0.7 select_reduce_fusion.1
  (9 shorter events, 0.1 us)
Async XLA Ops:
  11.7 13.4 %all-to-all-start = ((bf16[132,4,512]{2,0,1:T(8,128)(2,1)}), bf16[132,4,512]{2,0,1:T(8,128)(2,1)S(1)}, u32[]{:S(2)}, u32[]{:S(2)}) async-start(bf16[132,4,512]{2,0,1:T(8,128)(2,1)} %copy.61), calls=%async_computation | async-start | bytes 1114112 | tf_op jit(solution)/shard_map/all_to_all | solution.py:124
  16.0 59.5 %all-gather.3.cloned.1.call-start = ((), (), s32[]{:S(2)}) async-start(), calls=%async_computation.2 | async-start | bytes 2785280 | tf_op jit(solution)/shard_map/all_gather | solution.py:133
  17.7 48.5 %copy-start.2 = (s32[128,8]{0,1:T(8,128)S(1)}, s32[128,8]{0,1:T(8,128)}, u32[]{:S(2)}) copy-start(s32[128,8]{0,1:T(8,128)} %param.7) | copy-start | bytes 12292
  25.1 0.8 copy-start
  26.0 40.2 %collective-permute-start = (bf16[1152,768]{1,0:T(8,128)(2,1)}, bf16[1152,768]{1,0:T(8,128)(2,1)S(1)}, u32[]{:S(2)}, u32[]{:S(2)}) collective-permute-start(bf16[1152,768]{1,0:T(8,128)(2,1)} %reshape.41.own_ref), channel_id=1, source_target_pairs={{0,2},{1,3},{2,0},{3,1},{4,6},{5,7},{6,4},{7,5},{8,10},{9,11},{10,... | collective-permute-start | bytes 5308424 | tf_op jit(solution)/shard_map/ppermute | solution.py:131
  26.4 52.7 %collective-permute-start.1 = (bf16[1152,768]{1,0:T(8,128)(2,1)}, bf16[1152,768]{1,0:T(8,128)(2,1)}, u32[]{:S(2)}, u32[]{:S(2)}) collective-permute-start(bf16[1152,768]{1,0:T(8,128)(2,1)} %reshape.41.own_ref), channel_id=1, source_target_pairs={{0,1},{1,0},{2,3},{3,2},{4,5},{5,4},{6,7},{7,6},{8,9},{9,8},{10,11... | collective-permute-start | bytes 5308424 | tf_op jit(solution)/shard_map/ppermute | solution.py:130
  66.2 11.2 %copy-start.1 = (bf16[1152,768]{1,0:T(8,128)(2,1)}, bf16[1152,768]{1,0:T(8,128)(2,1)S(1)}, u32[]{:S(2)}) copy-start(bf16[1152,768]{1,0:T(8,128)(2,1)S(1)} %collective-permute-done.far_ref) | copy-start | bytes 5308420
  66.2 12.9 %collective-permute-start.2 = (bf16[1152,768]{1,0:T(8,128)(2,1)S(1)}, bf16[1152,768]{1,0:T(8,128)(2,1)}, u32[]{:S(2)}, u32[]{:S(2)}) collective-permute-start(bf16[1152,768]{1,0:T(8,128)(2,1)S(1)} %collective-permute-done.far_ref), channel_id=1, source_target_pairs={{0,1},{1,0},{2,3},{3,2},{4,5},{5,4},{6,7},{7,6},{8,9},{9,8},{10,11... | collective-permute-start | bytes 5308424 | tf_op jit(solution)/shard_map/ppermute | solution.py:132
  99.3 10.1 %all-to-all-start.1 = ((f32[16,1,288]{2,1,0:T(1,128)}), f32[16,1,288]{2,1,0:T(1,128)S(1)}, u32[]{:S(2)}, u32[]{:S(2)}) async-start(f32[16,1,288]{2,1,0:T(1,128)} %reshape.51), calls=%async_computation.1 | async-start | bytes 49152 | tf_op jit(solution)/shard_map/all_to_all | solution.py:162
Sparse Core Ops, SparseCore 0:
  26.1 49.3 all-gather.2

commit v12 on v10

--- a/solution.py
+++ b/solution.py
@@ -24,7 +24,7 @@
     for src in range(sources):
         for j, ref in enumerate(pieces):
             row = (src * len(pieces) + j) * padded
-            h_scr[row:row + capacity, :] = ref[src * capacity:(src + 1) * capacity, :].astype(jnp.float32)
+            h_scr[row:row + capacity, :] = ref[src * capacity:(src + 1) * capacity, :]
 
     slot_iota = lax.broadcasted_iota(jnp.int32, (padded, tok_ref.shape[1]), 0)
     for blk in range(blocks):
@@ -37,7 +37,7 @@
             (gate * rows).astype(jnp.bfloat16).astype(jnp.float32)
         )
 
-    h = h_scr[...].astype(jnp.bfloat16)
+    h = h_scr[...]
     part = lax.dot_general(
         h, s_scr[...].astype(jnp.bfloat16), (((0,), (0,)), ((), ())),
         preferred_element_type=jnp.float32,
@@ -91,7 +91,7 @@
             jax.ShapeDtypeStruct((local_count, 1, block_count * padded), jnp.float32),
         ],
         scratch_shapes=[
-            pltpu.VMEM((rows, hidden_width), jnp.float32),
+            pltpu.VMEM((rows, hidden_width), jnp.bfloat16),
             pltpu.VMEM((rows, col_width), jnp.float32),
             pltpu.VMEM((rows, col_width), jnp.float32),
         ],

time: 118 us -> 118 us (level)
  no operation moved by 1% of the time
where the time goes in v12:
time: 118 us
  waiting for transfers between devices  60.7 us (51%)
  Pallas kernels  17.6 us (15%)
  between operations  14.3 us (12%)
  local copies, waits for them, and re-layouts  10.2 us (9%)
  starting transfers between devices  8.17 us (7%)
  other arithmetic  5.89 us (5%)
    ppermute x1, waiting for transfers between devices, per_device(): far = lax.ppermute(hidden_sent, 'dp', [(j, j ^ 2) for j in range(shards)])  39 us
    pallas_call x1, Pallas kernels, expert_kernel(): pl.pallas_call(expert_body, grid=(local_count, steps), in_specs=[piece_sp...  17.6 us
    all_gather x1, waiting for transfers between devices, per_device(): got = lax.all_gather(cols, 'expert', axis=0, tiled=False)  9.04 us
    all_to_all x1, waiting for transfers between devices, per_device(): lax.all_to_all(send_back, ('expert', 'dp'), split_axis=0, concat_axis=0,...  6.53 us
    all_to_all x1, waiting for transfers between devices, per_device(): cols = lax.all_to_all(cols, 'dp', split_axis=1, concat_axis=0, tiled=True)  6.02 us
    unnamed x14, local copies, waits for them, and re-layouts  4.24 us
    all_to_all x1, starting transfers between devices, per_device(): cols = lax.all_to_all(cols, 'dp', split_axis=1, concat_axis=0, tiled=True)  4.21 us
    all_to_all x1, starting transfers between devices, per_device(): lax.all_to_all(send_back, ('expert', 'dp'), split_axis=0, concat_axis=0,...  3.53 us
  transfers between devices with their start and end apart: 6, of which 4 were waited for; matrix products, arithmetic and copies ran while one was open for 7% of the time, Pallas kernels for 0%

profile of v12, /device:TPU:0, one launch (start us, length us, event | category | flops | bytes accessed | tf_op | source)
XLA Modules:
  0.0 117.8 jit_solution(11348471262434253920)
XLA Ops:
  7.2 0.0 copy-start.2
  7.2 0.0 copy-start.3
  7.2 1.3 %copy.53 = bf16[128,2048]{0,1:T(8,128)(2,1)S(1)} copy(bf16[128,2048]{1,0:T(8,128)(2,1)} %param.7) | data formatting | bytes 1048576 | tf_op args[0]
  8.5 0.2 copy.55
  8.7 0.0 copy-done.2
  8.8 0.1 copy.54
  8.9 0.1 broadcast_in_dim.106
  9.0 0.9 pad_maximum_fusion
  9.9 4.2 %all-to-all-start = ((bf16[132,4,512]{2,0,1:T(8,128)(2,1)}), bf16[132,4,512]{2,0,1:T(8,128)(2,1)S(1)}, u32[]{:S(2)}, u32[]{:S(2)}) async-start(bf16[132,4,512]{2,0,1:T(8,128)(2,1)} %pad_maximum_fusion), calls=%async_computation | async-start | bytes 1114112 | tf_op jit(solution)/shard_map/all_to_all | solution.py:122
  14.1 1.7 %copy.52 = bf16[8,1,4,36,768]{4,3,2,0,1:T(8,128)(2,1)S(1)} copy(bf16[8,1,4,36,768]{4,2,3,1,0:T(4,128)(2,1)} %param.10) | data formatting | bytes 3538944 | tf_op args[3]
  15.8 0.0 copy-start
  15.9 1.4 %reshape.86.own_ref = bf16[1152,768]{1,0:T(8,128)(2,1)} reshape(bf16[8,1,4,36,768]{4,3,2,0,1:T(8,128)(2,1)S(1)} %copy.52) | data formatting | bytes 3538944 | tf_op jit(solution)/shard_map/reshape | solution.py:128
  17.3 6.0 %all-to-all-done = bf16[132,4,512]{2,0,1:T(8,128)(2,1)S(1)} async-done(((bf16[132,4,512]{2,0,1:T(8,128)(2,1)}), bf16[132,4,512]{2,0,1:T(8,128)(2,1)S(1)}, u32[]{:S(2)}, u32[]{:S(2)}) %all-to-all-start) | async-done | bytes 540704 | tf_op jit(solution)/shard_map/all_to_all | solution.py:122
  23.3 0.6 gather_fusion
  23.9 0.9 broadcast_select_fusion
  24.8 0.0 all-gather.3.cloned.1.call-update
  24.8 0.4 collective-permute-start
  25.3 0.6 gather_fusion.1
  25.9 0.0 collective-permute-start.1
  25.9 39.0 %collective-permute-done.far_ref = bf16[1152,768]{1,0:T(8,128)(2,1)} collective-permute-done((bf16[1152,768]{1,0:T(8,128)(2,1)S(1)}, bf16[1152,768]{1,0:T(8,128)(2,1)}, u32[]{:S(2)}, u32[]{:S(2)}) %collective-permute-start) | collective-permute-done | bytes 1769504 | tf_op jit(solution)/shard_map/ppermute | solution.py:131
  65.0 0.0 collective-permute-start.2
  65.0 0.1 broadcast_in_dim.119
  65.1 0.1 convolution_convert_fusion.1
  65.3 9.0 %all-gather.3.cloned.1.call-done.tok_ref = bf16[16,132,512]{2,1,0:T(8,128)(2,1)} async-done(((bf16[4,132,512]{2,1,0:T(8,128)(2,1)}), bf16[16,132,512]{2,1,0:T(8,128)(2,1)}) %all-gather.3.cloned.1.call-update) | async-done | bytes 2162704 | tf_op jit(solution)/shard_map/all_gather | solution.py:133
  74.3 0.9 slice.26
  75.2 0.4 reshape_reshape.3
  75.6 0.2 fusion.7
  75.9 0.2 copy.63
  76.1 0.2 copy.64
  76.3 0.1 compare_reduce_fusion
  76.4 0.7 fusion.1
  77.2 0.8 fusion
  77.9 0.0 collective-permute-done.1.near_ref
  77.9 0.0 collective-permute-done.2.near_far_ref
  77.9 17.6 %shard_map.86 = (f32[8,768,512]{2,1,0:T(8,128)}, f32[8,1,640]{2,1,0:T(1,128)}) custom-call(bf16[1152,768]{1,0:T(8,128)(2,1)} %reshape.86.own_ref, bf16[1152,768]{1,0:T(8,128)(2,1)} %collective-permute-done.far_ref, bf16[1152,768]{1,0:T(8,128)(2,1)} %collective-permute-done.1.near_ref, bf16[1152,768]{1,0:T(8,128)(2,1)} %collective-permute-done.2.near_far_ref, ...), custom_call_target="tpu_custom_call" | custom-call | tf_op jit(solution)/shard_map/pallas_call | solution.py:76
  95.6 0.8 reduce
  96.3 0.1 reshape.90
  96.5 0.6 gather_fusion.2
  97.0 0.1 bitcast_select_fusion
  97.1 0.7 reshape.122
  97.8 3.5 %all-to-all-start.1 = ((f32[16,1,288]{2,1,0:T(1,128)}), f32[16,1,288]{2,1,0:T(1,128)S(1)}, u32[]{:S(2)}, u32[]{:S(2)}) async-start(f32[16,1,288]{2,1,0:T(1,128)} %reshape.122), calls=%async_computation.1 | async-start | bytes 49152 | tf_op jit(solution)/shard_map/all_to_all | solution.py:164
  101.4 6.5 %all-to-all-done.1 = f32[16,1,288]{2,1,0:T(1,128)S(1)} async-done(((f32[16,1,288]{2,1,0:T(1,128)}), f32[16,1,288]{2,1,0:T(1,128)S(1)}, u32[]{:S(2)}, u32[]{:S(2)}) %all-to-all-start.1) | async-done | bytes 18464 | tf_op jit(solution)/shard_map/all_to_all | solution.py:164
  108.0 0.5 broadcast.97
  108.5 0.7 reduce.1
  109.2 0.1 reshape.123
  109.3 0.1 copy.60
  109.4 0.8 select_reduce_fusion
  110.2 0.7 select_reduce_fusion.1
  (26 shorter events, 0.2 us)
Async XLA Ops:
  7.2 1.6 %copy-start.2 = (s32[128,8]{0,1:T(8,128)S(1)}, s32[128,8]{0,1:T(8,128)}, u32[]{:S(2)}) copy-start(s32[128,8]{0,1:T(8,128)} %param.9) | copy-start | bytes 12292
  7.2 1.6 %copy-start.3 = (bf16[128,8]{0,1:T(8,128)(2,1)S(1)}, bf16[128,8]{0,1:T(8,128)(2,1)}, u32[]{:S(2)}) copy-start(bf16[128,8]{0,1:T(8,128)(2,1)} %param.8) | copy-start | bytes 6148
  9.9 13.4 %all-to-all-start = ((bf16[132,4,512]{2,0,1:T(8,128)(2,1)}), bf16[132,4,512]{2,0,1:T(8,128)(2,1)S(1)}, u32[]{:S(2)}, u32[]{:S(2)}) async-start(bf16[132,4,512]{2,0,1:T(8,128)(2,1)} %pad_maximum_fusion), calls=%async_computation | async-start | bytes 1114112 | tf_op jit(solution)/shard_map/all_to_all | solution.py:122
  14.1 60.2 %all-gather.3.cloned.1.call-start = ((), (), s32[]{:S(2)}) async-start(), calls=%async_computation.2 | async-start | bytes 2785280 | tf_op jit(solution)/shard_map/all_gather | solution.py:133
  15.8 1.4 %copy-start = (s32[4]{0:T(128)S(1)}, s32[4]{0:T(128)}, u32[]{:S(2)}) copy-start(s32[4]{0:T(128)} %constant.49.clone) | copy-start | bytes 52
  17.2 7.6 %copy-start.1 = (bf16[1152,768]{1,0:T(8,128)(2,1)S(1)}, bf16[1152,768]{1,0:T(8,128)(2,1)}, u32[]{:S(2)}) copy-start(bf16[1152,768]{1,0:T(8,128)(2,1)} %reshape.86.own_ref) | copy-start | bytes 5308420
  24.8 40.1 %collective-permute-start = (bf16[1152,768]{1,0:T(8,128)(2,1)S(1)}, bf16[1152,768]{1,0:T(8,128)(2,1)}, u32[]{:S(2)}, u32[]{:S(2)}) collective-permute-start(bf16[1152,768]{1,0:T(8,128)(2,1)S(1)} %copy-done.1), channel_id=1, source_target_pairs={{0,2},{1,3},{2,0},{3,1},{4,6},{5,7},{6,4},{7,5},{8,10},{9,11},{10,... | collective-permute-start | bytes 5308424 | tf_op jit(solution)/shard_map/ppermute | solution.py:131
  25.9 52.0 %collective-permute-start.1 = (bf16[1152,768]{1,0:T(8,128)(2,1)S(1)}, bf16[1152,768]{1,0:T(8,128)(2,1)}, u32[]{:S(2)}, u32[]{:S(2)}) collective-permute-start(bf16[1152,768]{1,0:T(8,128)(2,1)S(1)} %copy-done.1), channel_id=1, source_target_pairs={{0,1},{1,0},{2,3},{3,2},{4,5},{5,4},{6,7},{7,6},{8,9},{9,8},{10,11... | collective-permute-start | bytes 5308424 | tf_op jit(solution)/shard_map/ppermute | solution.py:130
  65.0 13.0 %collective-permute-start.2 = (bf16[1152,768]{1,0:T(8,128)(2,1)}, bf16[1152,768]{1,0:T(8,128)(2,1)}, u32[]{:S(2)}, u32[]{:S(2)}) collective-permute-start(bf16[1152,768]{1,0:T(8,128)(2,1)} %collective-permute-done.far_ref), channel_id=1, source_target_pairs={{0,1},{1,0},{2,3},{3,2},{4,5},{5,4},{6,7},{7,6},{8,9},{9,8},{10,11... | collective-permute-start | bytes 5308424 | tf_op jit(solution)/shard_map/ppermute | solution.py:132
  97.8 10.1 %all-to-all-start.1 = ((f32[16,1,288]{2,1,0:T(1,128)}), f32[16,1,288]{2,1,0:T(1,128)S(1)}, u32[]{:S(2)}, u32[]{:S(2)}) async-start(f32[16,1,288]{2,1,0:T(1,128)} %reshape.122), calls=%async_computation.1 | async-start | bytes 49152 | tf_op jit(solution)/shard_map/all_to_all | solution.py:164
Sparse Core Ops, SparseCore 0:
  24.9 49.3 all-gather.2

commit v13 on v12

--- a/solution.py
+++ b/solution.py
@@ -33,13 +33,11 @@
         rows = jnp.dot(sel, tok_ref[blk], preferred_element_type=jnp.float32)
         gate = jnp.sum(jnp.where(hit, gate_ref[blk, 0], 0.0), axis=1, keepdims=True)
         g_scr[blk * padded:(blk + 1) * padded, :] = rows
-        s_scr[blk * padded:(blk + 1) * padded, :] = (
-            (gate * rows).astype(jnp.bfloat16).astype(jnp.float32)
-        )
+        s_scr[blk * padded:(blk + 1) * padded, :] = (gate * rows).astype(jnp.bfloat16)
 
     h = h_scr[...]
     part = lax.dot_general(
-        h, s_scr[...].astype(jnp.bfloat16), (((0,), (0,)), ((), ())),
+        h, s_scr[...], (((0,), (0,)), ((), ())),
         preferred_element_type=jnp.float32,
     )
 
@@ -92,7 +90,7 @@
         ],
         scratch_shapes=[
             pltpu.VMEM((rows, hidden_width), jnp.bfloat16),
-            pltpu.VMEM((rows, col_width), jnp.float32),
+            pltpu.VMEM((rows, col_width), jnp.bfloat16),
             pltpu.VMEM((rows, col_width), jnp.float32),
         ],
     )(*pieces, tokens, slot_row, gate_row, weight)

time: 118 us -> 118 us (level)
  no operation moved by 1% of the time
where the time goes in v13:
time: 118 us
  waiting for transfers between devices  60.7 us (51%)
  Pallas kernels  17.6 us (15%)
  between operations  14.3 us (12%)
  local copies, waits for them, and re-layouts  10.2 us (9%)
  starting transfers between devices  8.17 us (7%)
  other arithmetic  5.89 us (5%)
    ppermute x1, waiting for transfers between devices, per_device(): far = lax.ppermute(hidden_sent, 'dp', [(j, j ^ 2) for j in range(shards)])  39 us
    pallas_call x1, Pallas kernels, expert_kernel(): pl.pallas_call(expert_body, grid=(local_count, steps), in_specs=[piece_sp...  17.6 us
    all_gather x1, waiting for transfers between devices, per_device(): got = lax.all_gather(cols, 'expert', axis=0, tiled=False)  9.04 us
    all_to_all x1, waiting for transfers between devices, per_device(): lax.all_to_all(send_back, ('expert', 'dp'), split_axis=0, concat_axis=0,...  6.53 us
    all_to_all x1, waiting for transfers between devices, per_device(): cols = lax.all_to_all(cols, 'dp', split_axis=1, concat_axis=0, tiled=True)  6.02 us
    unnamed x14, local copies, waits for them, and re-layouts  4.24 us
    all_to_all x1, starting transfers between devices, per_device(): cols = lax.all_to_all(cols, 'dp', split_axis=1, concat_axis=0, tiled=True)  4.21 us
    all_to_all x1, starting transfers between devices, per_device(): lax.all_to_all(send_back, ('expert', 'dp'), split_axis=0, concat_axis=0,...  3.53 us
  transfers between devices with their start and end apart: 6, of which 4 were waited for; matrix products, arithmetic and copies ran while one was open for 7% of the time, Pallas kernels for 0%

profile of v13, /device:TPU:0, one launch (start us, length us, event | category | flops | bytes accessed | tf_op | source)
XLA Modules:
  0.0 117.8 jit_solution(11348471262434253920)
XLA Ops:
  7.2 0.0 copy-start.2
  7.2 0.0 copy-start.3
  7.2 1.3 %copy.53 = bf16[128,2048]{0,1:T(8,128)(2,1)S(1)} copy(bf16[128,2048]{1,0:T(8,128)(2,1)} %param.7) | data formatting | bytes 1048576 | tf_op args[0]
  8.5 0.2 copy.55
  8.7 0.0 copy-done.2
  8.8 0.1 copy.54
  8.9 0.1 broadcast_in_dim.106
  9.0 0.9 pad_maximum_fusion
  9.9 4.2 %all-to-all-start = ((bf16[132,4,512]{2,0,1:T(8,128)(2,1)}), bf16[132,4,512]{2,0,1:T(8,128)(2,1)S(1)}, u32[]{:S(2)}, u32[]{:S(2)}) async-start(bf16[132,4,512]{2,0,1:T(8,128)(2,1)} %pad_maximum_fusion), calls=%async_computation | async-start | bytes 1114112 | tf_op jit(solution)/shard_map/all_to_all | solution.py:120
  14.1 1.7 %copy.52 = bf16[8,1,4,36,768]{4,3,2,0,1:T(8,128)(2,1)S(1)} copy(bf16[8,1,4,36,768]{4,2,3,1,0:T(4,128)(2,1)} %param.10) | data formatting | bytes 3538944 | tf_op args[3]
  15.8 0.0 copy-start
  15.9 1.4 %reshape.86.own_ref = bf16[1152,768]{1,0:T(8,128)(2,1)} reshape(bf16[8,1,4,36,768]{4,3,2,0,1:T(8,128)(2,1)S(1)} %copy.52) | data formatting | bytes 3538944 | tf_op jit(solution)/shard_map/reshape | solution.py:126
  17.3 6.0 %all-to-all-done = bf16[132,4,512]{2,0,1:T(8,128)(2,1)S(1)} async-done(((bf16[132,4,512]{2,0,1:T(8,128)(2,1)}), bf16[132,4,512]{2,0,1:T(8,128)(2,1)S(1)}, u32[]{:S(2)}, u32[]{:S(2)}) %all-to-all-start) | async-done | bytes 540704 | tf_op jit(solution)/shard_map/all_to_all | solution.py:120
  23.3 0.6 gather_fusion
  23.9 0.9 broadcast_select_fusion
  24.8 0.0 all-gather.3.cloned.1.call-update
  24.8 0.4 collective-permute-start
  25.3 0.6 gather_fusion.1
  25.9 0.0 collective-permute-start.1
  25.9 39.0 %collective-permute-done.far_ref = bf16[1152,768]{1,0:T(8,128)(2,1)} collective-permute-done((bf16[1152,768]{1,0:T(8,128)(2,1)S(1)}, bf16[1152,768]{1,0:T(8,128)(2,1)}, u32[]{:S(2)}, u32[]{:S(2)}) %collective-permute-start) | collective-permute-done | bytes 1769504 | tf_op jit(solution)/shard_map/ppermute | solution.py:129
  65.0 0.0 collective-permute-start.2
  65.0 0.1 broadcast_in_dim.119
  65.1 0.1 convolution_convert_fusion.1
  65.3 9.0 %all-gather.3.cloned.1.call-done.tok_ref = bf16[16,132,512]{2,1,0:T(8,128)(2,1)} async-done(((bf16[4,132,512]{2,1,0:T(8,128)(2,1)}), bf16[16,132,512]{2,1,0:T(8,128)(2,1)}) %all-gather.3.cloned.1.call-update) | async-done | bytes 2162704 | tf_op jit(solution)/shard_map/all_gather | solution.py:131
  74.3 0.9 slice.26
  75.2 0.4 reshape_reshape.3
  75.6 0.2 fusion.7
  75.9 0.2 copy.63
  76.1 0.2 copy.64
  76.3 0.1 compare_reduce_fusion
  76.4 0.7 fusion.1
  77.2 0.8 fusion
  77.9 0.0 collective-permute-done.1.near_ref
  77.9 0.0 collective-permute-done.2.near_far_ref
  77.9 17.6 %shard_map.86 = (f32[8,768,512]{2,1,0:T(8,128)}, f32[8,1,640]{2,1,0:T(1,128)}) custom-call(bf16[1152,768]{1,0:T(8,128)(2,1)} %reshape.86.own_ref, bf16[1152,768]{1,0:T(8,128)(2,1)} %collective-permute-done.far_ref, bf16[1152,768]{1,0:T(8,128)(2,1)} %collective-permute-done.1.near_ref, bf16[1152,768]{1,0:T(8,128)(2,1)} %collective-permute-done.2.near_far_ref, ...), custom_call_target="tpu_custom_call" | custom-call | tf_op jit(solution)/shard_map/pallas_call | solution.py:74
  95.6 0.8 reduce
  96.3 0.1 reshape.90
  96.5 0.6 gather_fusion.2
  97.0 0.1 bitcast_select_fusion
  97.1 0.7 reshape.122
  97.8 3.5 %all-to-all-start.1 = ((f32[16,1,288]{2,1,0:T(1,128)}), f32[16,1,288]{2,1,0:T(1,128)S(1)}, u32[]{:S(2)}, u32[]{:S(2)}) async-start(f32[16,1,288]{2,1,0:T(1,128)} %reshape.122), calls=%async_computation.1 | async-start | bytes 49152 | tf_op jit(solution)/shard_map/all_to_all | solution.py:162
  101.4 6.5 %all-to-all-done.1 = f32[16,1,288]{2,1,0:T(1,128)S(1)} async-done(((f32[16,1,288]{2,1,0:T(1,128)}), f32[16,1,288]{2,1,0:T(1,128)S(1)}, u32[]{:S(2)}, u32[]{:S(2)}) %all-to-all-start.1) | async-done | bytes 18464 | tf_op jit(solution)/shard_map/all_to_all | solution.py:162
  108.0 0.5 broadcast.97
  108.5 0.7 reduce.1
  109.2 0.1 reshape.123
  109.3 0.1 copy.60
  109.4 0.8 select_reduce_fusion
  110.2 0.7 select_reduce_fusion.1
  (26 shorter events, 0.2 us)
Async XLA Ops:
  7.2 1.6 %copy-start.2 = (s32[128,8]{0,1:T(8,128)S(1)}, s32[128,8]{0,1:T(8,128)}, u32[]{:S(2)}) copy-start(s32[128,8]{0,1:T(8,128)} %param.9) | copy-start | bytes 12292
  7.2 1.6 %copy-start.3 = (bf16[128,8]{0,1:T(8,128)(2,1)S(1)}, bf16[128,8]{0,1:T(8,128)(2,1)}, u32[]{:S(2)}) copy-start(bf16[128,8]{0,1:T(8,128)(2,1)} %param.8) | copy-start | bytes 6148
  9.9 13.4 %all-to-all-start = ((bf16[132,4,512]{2,0,1:T(8,128)(2,1)}), bf16[132,4,512]{2,0,1:T(8,128)(2,1)S(1)}, u32[]{:S(2)}, u32[]{:S(2)}) async-start(bf16[132,4,512]{2,0,1:T(8,128)(2,1)} %pad_maximum_fusion), calls=%async_computation | async-start | bytes 1114112 | tf_op jit(solution)/shard_map/all_to_all | solution.py:120
  14.1 60.2 %all-gather.3.cloned.1.call-start = ((), (), s32[]{:S(2)}) async-start(), calls=%async_computation.2 | async-start | bytes 2785280 | tf_op jit(solution)/shard_map/all_gather | solution.py:131
  15.8 1.4 %copy-start = (s32[4]{0:T(128)S(1)}, s32[4]{0:T(128)}, u32[]{:S(2)}) copy-start(s32[4]{0:T(128)} %constant.49.clone) | copy-start | bytes 52
  17.2 7.6 %copy-start.1 = (bf16[1152,768]{1,0:T(8,128)(2,1)S(1)}, bf16[1152,768]{1,0:T(8,128)(2,1)}, u32[]{:S(2)}) copy-start(bf16[1152,768]{1,0:T(8,128)(2,1)} %reshape.86.own_ref) | copy-start | bytes 5308420
  24.8 40.1 %collective-permute-start = (bf16[1152,768]{1,0:T(8,128)(2,1)S(1)}, bf16[1152,768]{1,0:T(8,128)(2,1)}, u32[]{:S(2)}, u32[]{:S(2)}) collective-permute-start(bf16[1152,768]{1,0:T(8,128)(2,1)S(1)} %copy-done.1), channel_id=1, source_target_pairs={{0,2},{1,3},{2,0},{3,1},{4,6},{5,7},{6,4},{7,5},{8,10},{9,11},{10,... | collective-permute-start | bytes 5308424 | tf_op jit(solution)/shard_map/ppermute | solution.py:129
  25.9 52.0 %collective-permute-start.1 = (bf16[1152,768]{1,0:T(8,128)(2,1)S(1)}, bf16[1152,768]{1,0:T(8,128)(2,1)}, u32[]{:S(2)}, u32[]{:S(2)}) collective-permute-start(bf16[1152,768]{1,0:T(8,128)(2,1)S(1)} %copy-done.1), channel_id=1, source_target_pairs={{0,1},{1,0},{2,3},{3,2},{4,5},{5,4},{6,7},{7,6},{8,9},{9,8},{10,11... | collective-permute-start | bytes 5308424 | tf_op jit(solution)/shard_map/ppermute | solution.py:128
  65.0 13.0 %collective-permute-start.2 = (bf16[1152,768]{1,0:T(8,128)(2,1)}, bf16[1152,768]{1,0:T(8,128)(2,1)}, u32[]{:S(2)}, u32[]{:S(2)}) collective-permute-start(bf16[1152,768]{1,0:T(8,128)(2,1)} %collective-permute-done.far_ref), channel_id=1, source_target_pairs={{0,1},{1,0},{2,3},{3,2},{4,5},{5,4},{6,7},{7,6},{8,9},{9,8},{10,11... | collective-permute-start | bytes 5308424 | tf_op jit(solution)/shard_map/ppermute | solution.py:130
  97.8 10.1 %all-to-all-start.1 = ((f32[16,1,288]{2,1,0:T(1,128)}), f32[16,1,288]{2,1,0:T(1,128)S(1)}, u32[]{:S(2)}, u32[]{:S(2)}) async-start(f32[16,1,288]{2,1,0:T(1,128)} %reshape.122), calls=%async_computation.1 | async-start | bytes 49152 | tf_op jit(solution)/shard_map/all_to_all | solution.py:162
Sparse Core Ops, SparseCore 0:
  24.9 49.3 all-gather.2

commit v14 on v13

--- a/solution.py
+++ b/solution.py
@@ -27,11 +27,14 @@
             h_scr[row:row + capacity, :] = ref[src * capacity:(src + 1) * capacity, :]
 
     slot_iota = lax.broadcasted_iota(jnp.int32, (padded, tok_ref.shape[1]), 0)
+    my_dp = lax.axis_index("dp")
     for blk in range(blocks):
-        hit = sel_ref[blk, 0] == slot_iota
+        src, j = divmod(blk, len(pieces))
+        nat = src * len(pieces) + (my_dp ^ (0, 2, 1, 3)[j])
+        hit = sel_ref[nat, 0] == slot_iota
         sel = hit.astype(jnp.bfloat16)
-        rows = jnp.dot(sel, tok_ref[blk], preferred_element_type=jnp.float32)
-        gate = jnp.sum(jnp.where(hit, gate_ref[blk, 0], 0.0), axis=1, keepdims=True)
+        rows = jnp.dot(sel, tok_ref[nat], preferred_element_type=jnp.float32)
+        gate = jnp.sum(jnp.where(hit, gate_ref[nat, 0], 0.0), axis=1, keepdims=True)
         g_scr[blk * padded:(blk + 1) * padded, :] = rows
         s_scr[blk * padded:(blk + 1) * padded, :] = (gate * rows).astype(jnp.bfloat16)
 
@@ -119,8 +122,6 @@
     cols = jnp.concatenate([cols, jnp.broadcast_to(meta, (meta_rows, shards, col_width))], axis=0)
     cols = lax.all_to_all(cols, "dp", split_axis=1, concat_axis=0, tiled=True)
     cols = cols.reshape(shards, tok_rows + meta_rows, col_width)
-    piece_xor = jnp.array([0, 2, 1, 3], jnp.int32)
-    cols = jnp.take(cols, piece_xor ^ my_dp, axis=0)
 
     hidden_shape = hidden.shape
     hidden = hidden.reshape(-1, hidden_width)

time: 118 us -> 120 us (1.017)
  local copies, waits for them, and re-layouts: 10.2 us -> 11.6 us
  transfers between devices with their start and end apart: 6 -> 6, of which waited for: 4 -> 4; matrix products, arithmetic and copies ran while one was open for 7% -> 6% of each run, Pallas kernels for 0% -> 0%
where the time goes in v14:
time: 120 us; the launch traced here: 119 us
  waiting for transfers between devices  60.7 us (51%)
  Pallas kernels  17.9 us (15%)
  between operations  14.3 us (12%)
  local copies, waits for them, and re-layouts  11.6 us (10%)
  starting transfers between devices  8.18 us (7%)
  other arithmetic  5.67 us (5%)
    ppermute x1, waiting for transfers between devices, per_device(): far = lax.ppermute(hidden_sent, 'dp', [(j, j ^ 2) for j in range(shards)])  39.1 us
    pallas_call x1, Pallas kernels, expert_kernel(): pl.pallas_call(expert_body, grid=(local_count, steps), in_specs=[piece_sp...  17.9 us
    all_gather x1, waiting for transfers between devices, per_device(): got = lax.all_gather(cols, 'expert', axis=0, tiled=False)  8.94 us
    all_to_all x1, waiting for transfers between devices, per_device(): lax.all_to_all(send_back, ('expert', 'dp'), split_axis=0, concat_axis=0,...  6.53 us
    all_to_all x1, waiting for transfers between devices, per_device(): cols = lax.all_to_all(cols, 'dp', split_axis=1, concat_axis=0, tiled=True)  6.03 us
    unnamed x14, local copies, waits for them, and re-layouts  5.03 us
    all_to_all x1, starting transfers between devices, per_device(): cols = lax.all_to_all(cols, 'dp', split_axis=1, concat_axis=0, tiled=True)  4.21 us
    all_to_all x1, starting transfers between devices, per_device(): lax.all_to_all(send_back, ('expert', 'dp'), split_axis=0, concat_axis=0,...  3.54 us
  transfers between devices with their start and end apart: 6, of which 4 were waited for; matrix products, arithmetic and copies ran while one was open for 6% of the time, Pallas kernels for 0%

profile of v14, /device:TPU:0, one launch (start us, length us, event | category | flops | bytes accessed | tf_op | source)
XLA Modules:
  0.0 119.2 jit_solution(15095269341698268846)
XLA Ops:
  7.2 0.7 convert_element_type.19
  7.9 0.7 pad_maximum_fusion.1
  8.5 0.1 copy.67
  8.7 0.1 broadcast_in_dim.93
  8.8 0.2 copy.68
  9.0 1.3 %copy.66 = bf16[128,2048]{0,1:T(8,128)(2,1)S(1)} copy(bf16[128,2048]{1,0:T(8,128)(2,1)} %param.6) | data formatting | bytes 1048576 | tf_op args[0]
  10.3 0.1 broadcast_in_dim.94
  10.4 0.2 pad_maximum_fusion
  10.6 1.2 copy.69
  11.7 4.2 %all-to-all-start = ((bf16[132,4,512]{2,0,1:T(8,128)(2,1)}), bf16[132,4,512]{2,0,1:T(8,128)(2,1)S(1)}, u32[]{:S(2)}, u32[]{:S(2)}) async-start(bf16[132,4,512]{2,0,1:T(8,128)(2,1)} %copy.69), calls=%async_computation | async-start | bytes 1114112 | tf_op jit(solution)/shard_map/all_to_all | solution.py:123
  16.0 1.7 %copy.65 = bf16[8,1,4,36,768]{4,3,2,0,1:T(8,128)(2,1)S(1)} copy(bf16[8,1,4,36,768]{4,2,3,1,0:T(4,128)(2,1)} %param.9) | data formatting | bytes 3538944 | tf_op args[3]
  17.7 0.0 copy-start
  17.7 0.0 copy-start.3
  17.7 1.4 %reshape.81.own_ref = bf16[1152,768]{1,0:T(8,128)(2,1)} reshape(bf16[8,1,4,36,768]{4,3,2,0,1:T(8,128)(2,1)S(1)} %copy.65) | data formatting | bytes 3538944 | tf_op jit(solution)/shard_map/reshape | solution.py:127
  19.1 6.0 %all-to-all-done = bf16[132,4,512]{2,0,1:T(8,128)(2,1)S(1)} async-done(((bf16[132,4,512]{2,0,1:T(8,128)(2,1)}), bf16[132,4,512]{2,0,1:T(8,128)(2,1)S(1)}, u32[]{:S(2)}, u32[]{:S(2)}) %all-to-all-start) | async-done | bytes 540704 | tf_op jit(solution)/shard_map/all_to_all | solution.py:123
  25.2 0.8 copy-done.1
  26.0 0.0 all-gather.3.cloned.1.call-update
  26.0 0.4 collective-permute-start
  26.4 0.6 gather_fusion
  27.1 0.0 collective-permute-start.1
  27.1 39.1 %collective-permute-done.far_ref = bf16[1152,768]{1,0:T(8,128)(2,1)S(1)} collective-permute-done((bf16[1152,768]{1,0:T(8,128)(2,1)}, bf16[1152,768]{1,0:T(8,128)(2,1)S(1)}, u32[]{:S(2)}, u32[]{:S(2)}) %collective-permute-start) | collective-permute-done | bytes 1769504 | tf_op jit(solution)/shard_map/ppermute | solution.py:130
  66.2 0.0 collective-permute-start.2
  66.2 0.1 broadcast_in_dim.104
  66.4 0.1 convolution_convert_fusion.1
  66.5 8.9 %all-gather.3.cloned.1.call-done.tok_ref = bf16[16,132,512]{2,1,0:T(8,128)(2,1)} async-done(((bf16[4,132,512]{2,1,0:T(8,128)(2,1)}), bf16[16,132,512]{2,1,0:T(8,128)(2,1)}) %all-gather.3.cloned.1.call-update) | async-done | bytes 2162704 | tf_op jit(solution)/shard_map/all_gather | solution.py:132
  75.5 0.9 slice.24
  76.4 0.4 reshape_reshape.3
  76.8 0.2 fusion.7
  77.0 0.2 copy.77
  77.2 0.2 copy.78
  77.4 0.1 compare_reduce_fusion
  77.6 0.7 fusion.1
  78.3 0.8 fusion
  79.1 0.0 collective-permute-done.1.near_ref
  79.1 17.9 %shard_map.77 = (f32[8,768,512]{2,1,0:T(8,128)}, f32[8,1,640]{2,1,0:T(1,128)}) custom-call(bf16[1152,768]{1,0:T(8,128)(2,1)} %reshape.81.own_ref, bf16[1152,768]{1,0:T(8,128)(2,1)} %copy-done.2, bf16[1152,768]{1,0:T(8,128)(2,1)} %collective-permute-done.1.near_ref, bf16[1152,768]{1,0:T(8,128)(2,1)} %collective-permute-done.2.near_far_ref, ...), custom_call_target="tpu_custom_call" | custom-call | tf_op jit(solution)/shard_map/pallas_call | solution.py:77
  97.0 0.8 reduce
  97.8 0.1 reshape.85
  97.9 0.6 gather_fusion.1
  98.5 0.1 bitcast_select_fusion
  98.6 0.7 reshape.108
  99.3 3.5 %all-to-all-start.1 = ((f32[16,1,288]{2,1,0:T(1,128)}), f32[16,1,288]{2,1,0:T(1,128)S(1)}, u32[]{:S(2)}, u32[]{:S(2)}) async-start(f32[16,1,288]{2,1,0:T(1,128)} %reshape.108), calls=%async_computation.1 | async-start | bytes 49152 | tf_op jit(solution)/shard_map/all_to_all | solution.py:163
  102.9 6.5 %all-to-all-done.1 = f32[16,1,288]{2,1,0:T(1,128)S(1)} async-done(((f32[16,1,288]{2,1,0:T(1,128)}), f32[16,1,288]{2,1,0:T(1,128)S(1)}, u32[]{:S(2)}, u32[]{:S(2)}) %all-to-all-start.1) | async-done | bytes 18464 | tf_op jit(solution)/shard_map/all_to_all | solution.py:163
  109.4 0.5 broadcast.100
  109.9 0.7 reduce.1
  110.6 0.1 reshape.109
  110.7 0.1 copy.74
  110.8 0.8 select_reduce_fusion
  111.7 0.7 select_reduce_fusion.1
  (23 shorter events, 0.2 us)
Async XLA Ops:
  11.7 13.4 %all-to-all-start = ((bf16[132,4,512]{2,0,1:T(8,128)(2,1)}), bf16[132,4,512]{2,0,1:T(8,128)(2,1)S(1)}, u32[]{:S(2)}, u32[]{:S(2)}) async-start(bf16[132,4,512]{2,0,1:T(8,128)(2,1)} %copy.69), calls=%async_computation | async-start | bytes 1114112 | tf_op jit(solution)/shard_map/all_to_all | solution.py:123
  16.0 59.5 %all-gather.3.cloned.1.call-start = ((), (), s32[]{:S(2)}) async-start(), calls=%async_computation.2 | async-start | bytes 2785280 | tf_op jit(solution)/shard_map/all_gather | solution.py:132
  17.7 8.7 %copy-start = (s32[4]{0:T(128)S(1)}, s32[4]{0:T(128)}, u32[]{:S(2)}) copy-start(s32[4]{0:T(128)} %constant.36.clone) | copy-start | bytes 52
  17.7 48.6 %copy-start.3 = (s32[128,8]{0,1:T(8,128)S(1)}, s32[128,8]{0,1:T(8,128)}, u32[]{:S(2)}) copy-start(s32[128,8]{0,1:T(8,128)} %param.8) | copy-start | bytes 12292
  25.1 0.8 copy-start.1
  26.0 40.2 %collective-permute-start = (bf16[1152,768]{1,0:T(8,128)(2,1)}, bf16[1152,768]{1,0:T(8,128)(2,1)S(1)}, u32[]{:S(2)}, u32[]{:S(2)}) collective-permute-start(bf16[1152,768]{1,0:T(8,128)(2,1)} %reshape.81.own_ref), channel_id=1, source_target_pairs={{0,2},{1,3},{2,0},{3,1},{4,6},{5,7},{6,4},{7,5},{8,10},{9,11},{10,... | collective-permute-start | bytes 5308424 | tf_op jit(solution)/shard_map/ppermute | solution.py:130
  27.1 52.0 %collective-permute-start.1 = (bf16[1152,768]{1,0:T(8,128)(2,1)}, bf16[1152,768]{1,0:T(8,128)(2,1)}, u32[]{:S(2)}, u32[]{:S(2)}) collective-permute-start(bf16[1152,768]{1,0:T(8,128)(2,1)} %reshape.81.own_ref), channel_id=1, source_target_pairs={{0,1},{1,0},{2,3},{3,2},{4,5},{5,4},{6,7},{7,6},{8,9},{9,8},{10,11... | collective-permute-start | bytes 5308424 | tf_op jit(solution)/shard_map/ppermute | solution.py:129
  66.2 11.2 %copy-start.2 = (bf16[1152,768]{1,0:T(8,128)(2,1)}, bf16[1152,768]{1,0:T(8,128)(2,1)S(1)}, u32[]{:S(2)}) copy-start(bf16[1152,768]{1,0:T(8,128)(2,1)S(1)} %collective-permute-done.far_ref) | copy-start | bytes 5308420
  66.2 12.9 %collective-permute-start.2 = (bf16[1152,768]{1,0:T(8,128)(2,1)S(1)}, bf16[1152,768]{1,0:T(8,128)(2,1)}, u32[]{:S(2)}, u32[]{:S(2)}) collective-permute-start(bf16[1152,768]{1,0:T(8,128)(2,1)S(1)} %collective-permute-done.far_ref), channel_id=1, source_target_pairs={{0,1},{1,0},{2,3},{3,2},{4,5},{5,4},{6,7},{7,6},{8,9},{9,8},{10,11... | collective-permute-start | bytes 5308424 | tf_op jit(solution)/shard_map/ppermute | solution.py:131
  99.3 10.1 %all-to-all-start.1 = ((f32[16,1,288]{2,1,0:T(1,128)}), f32[16,1,288]{2,1,0:T(1,128)S(1)}, u32[]{:S(2)}, u32[]{:S(2)}) async-start(f32[16,1,288]{2,1,0:T(1,128)} %reshape.108), calls=%async_computation.1 | async-start | bytes 49152 | tf_op jit(solution)/shard_map/all_to_all | solution.py:163
Sparse Core Ops, SparseCore 0:
  26.1 49.3 all-gather.2

commit v15 on v13

--- a/solution.py
+++ b/solution.py
@@ -154,16 +154,15 @@
     weight_grad, slot_part = expert_kernel(
         (hidden, far, near, near_far), got, slot_row, gate_row, down_weight, padded, hidden_shape
     )
-    slot_part = slot_part.reshape(local_count, block_count, padded)[:, :, :capacity]
-    slot_part = slot_part.transpose(1, 0, 2).reshape(peer_count, shards, local_count, capacity)
+    slot_part = slot_part.reshape(local_count, peer_count, shards, padded)
     piece_of = jnp.array([0, 2, 1, 3], jnp.int32)[jnp.arange(shards, dtype=jnp.int32) ^ my_dp]
-    slot_part = jnp.take(slot_part, piece_of, axis=1)
-    send_back = slot_part.reshape(block_count, local_count, capacity)
+    slot_part = jnp.take(slot_part, piece_of, axis=2)[:, :, :, :capacity]
+    send_back = slot_part.reshape(local_count, block_count, capacity)
     returned = lax.all_to_all(
-        send_back, ("expert", "dp"), split_axis=0, concat_axis=0, tiled=True
+        send_back, ("expert", "dp"), split_axis=1, concat_axis=1, tiled=True
     )
-    returned = returned.reshape(peer_count, shards, local_count, capacity)
-    slot_grad = jnp.sum(returned, axis=1).reshape(expert_count, capacity)
+    returned = returned.reshape(local_count, peer_count, shards, capacity)
+    slot_grad = jnp.sum(returned, axis=2).transpose(1, 0, 2).reshape(expert_count, capacity)
 
     own_hit = expert_ids[:, :, None] == jnp.arange(expert_count, dtype=jnp.int32)[None, None, :]
     own_chose = jnp.any(own_hit, axis=1)

time: 118 us -> 118 us (level)
  transfers between devices with their start and end apart: 6 -> 6, of which waited for: 4 -> 4; matrix products, arithmetic and copies ran while one was open for 7% -> 6% of each run, Pallas kernels for 0% -> 0%
where the time goes in v15:
time: 118 us
  waiting for transfers between devices  60.7 us (51%)
  Pallas kernels  17.6 us (15%)
  between operations  14.3 us (12%)
  local copies, waits for them, and re-layouts  10.1 us (9%)
  starting transfers between devices  8.23 us (7%)
  other arithmetic  5.89 us (5%)
    ppermute x1, waiting for transfers between devices, per_device(): far = lax.ppermute(hidden_sent, 'dp', [(j, j ^ 2) for j in range(shards)])  39.6 us
    pallas_call x1, Pallas kernels, expert_kernel(): pl.pallas_call(expert_body, grid=(local_count, steps), in_specs=[piece_sp...  17.6 us
    all_gather x1, waiting for transfers between devices, per_device(): got = lax.all_gather(cols, 'expert', axis=0, tiled=False)  8.5 us
    all_to_all x1, waiting for transfers between devices, per_device(): lax.all_to_all(send_back, ('expert', 'dp'), split_axis=1, concat_axis=1,...  6.53 us
    all_to_all x1, waiting for transfers between devices, per_device(): cols = lax.all_to_all(cols, 'dp', split_axis=1, concat_axis=0, tiled=True)  6.02 us
    unnamed x14, local copies, waits for them, and re-layouts  4.25 us
    all_to_all x1, starting transfers between devices, per_device(): cols = lax.all_to_all(cols, 'dp', split_axis=1, concat_axis=0, tiled=True)  4.21 us
    all_to_all x1, starting transfers between devices, per_device(): lax.all_to_all(send_back, ('expert', 'dp'), split_axis=1, concat_axis=1,...  3.52 us
  transfers between devices with their start and end apart: 6, of which 4 were waited for; matrix products, arithmetic and copies ran while one was open for 6% of the time, Pallas kernels for 0%

profile of v15, /device:TPU:0, one launch (start us, length us, event | category | flops | bytes accessed | tf_op | source)
XLA Modules:
  0.0 117.8 jit_solution(12401088565696020411)
XLA Ops:
  7.2 0.0 copy-start.2
  7.2 0.0 copy-start.3
  7.2 1.3 %copy.53 = bf16[128,2048]{0,1:T(8,128)(2,1)S(1)} copy(bf16[128,2048]{1,0:T(8,128)(2,1)} %param.7) | data formatting | bytes 1048576 | tf_op args[0]
  8.5 0.2 copy.55
  8.7 0.0 copy-done.2
  8.8 0.0 copy-done.3
  8.8 0.1 copy.54
  8.9 0.1 broadcast_in_dim.102
  9.0 0.9 pad_maximum_fusion
  9.9 4.2 %all-to-all-start = ((bf16[132,4,512]{2,0,1:T(8,128)(2,1)}), bf16[132,4,512]{2,0,1:T(8,128)(2,1)S(1)}, u32[]{:S(2)}, u32[]{:S(2)}) async-start(bf16[132,4,512]{2,0,1:T(8,128)(2,1)} %pad_maximum_fusion), calls=%async_computation | async-start | bytes 1114112 | tf_op jit(solution)/shard_map/all_to_all | solution.py:120
  14.1 1.7 %copy.52 = bf16[8,1,4,36,768]{4,3,2,0,1:T(8,128)(2,1)S(1)} copy(bf16[8,1,4,36,768]{4,2,3,1,0:T(4,128)(2,1)} %param.10) | data formatting | bytes 3538944 | tf_op args[3]
  15.8 0.0 copy-start
  15.9 1.4 %reshape.83.own_ref = bf16[1152,768]{1,0:T(8,128)(2,1)} reshape(bf16[8,1,4,36,768]{4,3,2,0,1:T(8,128)(2,1)S(1)} %copy.52) | data formatting | bytes 3538944 | tf_op jit(solution)/shard_map/reshape | solution.py:126
  17.3 6.0 %all-to-all-done = bf16[132,4,512]{2,0,1:T(8,128)(2,1)S(1)} async-done(((bf16[132,4,512]{2,0,1:T(8,128)(2,1)}), bf16[132,4,512]{2,0,1:T(8,128)(2,1)S(1)}, u32[]{:S(2)}, u32[]{:S(2)}) %all-to-all-start) | async-done | bytes 540704 | tf_op jit(solution)/shard_map/all_to_all | solution.py:120
  23.3 0.6 gather_fusion
  23.9 0.9 broadcast_select_fusion
  24.8 0.0 all-gather.3.cloned.1.call-update
  24.8 0.4 collective-permute-start
  25.3 0.1 collective-permute-start.1
  25.4 39.6 %collective-permute-done.far_ref = bf16[1152,768]{1,0:T(8,128)(2,1)} collective-permute-done((bf16[1152,768]{1,0:T(8,128)(2,1)S(1)}, bf16[1152,768]{1,0:T(8,128)(2,1)}, u32[]{:S(2)}, u32[]{:S(2)}) %collective-permute-start) | collective-permute-done | bytes 1769504 | tf_op jit(solution)/shard_map/ppermute | solution.py:129
  65.0 0.0 collective-permute-start.2
  65.0 0.6 gather_fusion.1
  65.7 0.1 convolution_convert_fusion.1
  65.8 8.5 %all-gather.3.cloned.1.call-done.tok_ref = bf16[16,132,512]{2,1,0:T(8,128)(2,1)} async-done(((bf16[4,132,512]{2,1,0:T(8,128)(2,1)}), bf16[16,132,512]{2,1,0:T(8,128)(2,1)}) %all-gather.3.cloned.1.call-update) | async-done | bytes 2162704 | tf_op jit(solution)/shard_map/all_gather | solution.py:131
  74.3 0.9 slice.26
  75.2 0.4 reshape_reshape.3
  75.6 0.2 fusion.7
  75.9 0.2 copy.63
  76.1 0.2 copy.64
  76.3 0.1 compare_reduce_fusion
  76.4 0.7 fusion.1
  77.2 0.8 fusion
  77.9 0.0 collective-permute-done.1.near_ref
  77.9 0.0 collective-permute-done.2.near_far_ref
  77.9 17.6 %shard_map.86 = (f32[8,768,512]{2,1,0:T(8,128)}, f32[8,1,640]{2,1,0:T(1,128)}) custom-call(bf16[1152,768]{1,0:T(8,128)(2,1)} %reshape.83.own_ref, bf16[1152,768]{1,0:T(8,128)(2,1)} %collective-permute-done.far_ref, bf16[1152,768]{1,0:T(8,128)(2,1)} %collective-permute-done.1.near_ref, bf16[1152,768]{1,0:T(8,128)(2,1)} %collective-permute-done.2.near_far_ref, ...), custom_call_target="tpu_custom_call" | custom-call | tf_op jit(solution)/shard_map/pallas_call | solution.py:74
  95.6 0.8 reduce
  96.3 0.1 reshape.87
  96.5 0.6 gather_fusion.2
  97.1 0.1 select_bitcast_fusion
  97.2 0.7 reshape.119
  97.9 3.5 %all-to-all-start.1 = ((f32[16,1,288]{2,1,0:T(1,128)}), f32[16,1,288]{2,1,0:T(1,128)S(1)}, u32[]{:S(2)}, u32[]{:S(2)}) async-start(f32[16,1,288]{2,1,0:T(1,128)} %reshape.119), calls=%async_computation.1 | async-start | bytes 49152 | tf_op jit(solution)/shard_map/all_to_all | solution.py:161
  101.4 6.5 %all-to-all-done.1 = f32[16,1,288]{2,1,0:T(1,128)S(1)} async-done(((f32[16,1,288]{2,1,0:T(1,128)}), f32[16,1,288]{2,1,0:T(1,128)S(1)}, u32[]{:S(2)}, u32[]{:S(2)}) %all-to-all-start.1) | async-done | bytes 18464 | tf_op jit(solution)/shard_map/all_to_all | solution.py:161
  108.0 0.5 broadcast.99
  108.5 0.7 reduce.1
  109.2 0.1 reshape.120
  109.3 0.1 copy.60
  109.4 0.8 select_reduce_fusion
  110.2 0.7 select_reduce_fusion.1
  (23 shorter events, 0.2 us)
Async XLA Ops:
  7.2 1.6 %copy-start.2 = (s32[128,8]{0,1:T(8,128)S(1)}, s32[128,8]{0,1:T(8,128)}, u32[]{:S(2)}) copy-start(s32[128,8]{0,1:T(8,128)} %param.9) | copy-start | bytes 12292
  7.2 1.6 %copy-start.3 = (bf16[128,8]{0,1:T(8,128)(2,1)S(1)}, bf16[128,8]{0,1:T(8,128)(2,1)}, u32[]{:S(2)}) copy-start(bf16[128,8]{0,1:T(8,128)(2,1)} %param.8) | copy-start | bytes 6148
  9.9 13.4 %all-to-all-start = ((bf16[132,4,512]{2,0,1:T(8,128)(2,1)}), bf16[132,4,512]{2,0,1:T(8,128)(2,1)S(1)}, u32[]{:S(2)}, u32[]{:S(2)}) async-start(bf16[132,4,512]{2,0,1:T(8,128)(2,1)} %pad_maximum_fusion), calls=%async_computation | async-start | bytes 1114112 | tf_op jit(solution)/shard_map/all_to_all | solution.py:120
  14.1 60.2 %all-gather.3.cloned.1.call-start = ((), (), s32[]{:S(2)}) async-start(), calls=%async_computation.2 | async-start | bytes 2785280 | tf_op jit(solution)/shard_map/all_gather | solution.py:131
  15.8 1.4 %copy-start = (s32[4]{0:T(128)S(1)}, s32[4]{0:T(128)}, u32[]{:S(2)}) copy-start(s32[4]{0:T(128)} %constant.49.clone) | copy-start | bytes 52
  17.2 7.6 %copy-start.1 = (bf16[1152,768]{1,0:T(8,128)(2,1)S(1)}, bf16[1152,768]{1,0:T(8,128)(2,1)}, u32[]{:S(2)}) copy-start(bf16[1152,768]{1,0:T(8,128)(2,1)} %reshape.83.own_ref) | copy-start | bytes 5308420
  24.8 40.1 %collective-permute-start = (bf16[1152,768]{1,0:T(8,128)(2,1)S(1)}, bf16[1152,768]{1,0:T(8,128)(2,1)}, u32[]{:S(2)}, u32[]{:S(2)}) collective-permute-start(bf16[1152,768]{1,0:T(8,128)(2,1)S(1)} %copy-done.1), channel_id=1, source_target_pairs={{0,2},{1,3},{2,0},{3,1},{4,6},{5,7},{6,4},{7,5},{8,10},{9,11},{10,... | collective-permute-start | bytes 5308424 | tf_op jit(solution)/shard_map/ppermute | solution.py:129
  25.3 52.7 %collective-permute-start.1 = (bf16[1152,768]{1,0:T(8,128)(2,1)S(1)}, bf16[1152,768]{1,0:T(8,128)(2,1)}, u32[]{:S(2)}, u32[]{:S(2)}) collective-permute-start(bf16[1152,768]{1,0:T(8,128)(2,1)S(1)} %copy-done.1), channel_id=1, source_target_pairs={{0,1},{1,0},{2,3},{3,2},{4,5},{5,4},{6,7},{7,6},{8,9},{9,8},{10,11... | collective-permute-start | bytes 5308424 | tf_op jit(solution)/shard_map/ppermute | solution.py:128
  65.0 13.0 %collective-permute-start.2 = (bf16[1152,768]{1,0:T(8,128)(2,1)}, bf16[1152,768]{1,0:T(8,128)(2,1)}, u32[]{:S(2)}, u32[]{:S(2)}) collective-permute-start(bf16[1152,768]{1,0:T(8,128)(2,1)} %collective-permute-done.far_ref), channel_id=1, source_target_pairs={{0,1},{1,0},{2,3},{3,2},{4,5},{5,4},{6,7},{7,6},{8,9},{9,8},{10,11... | collective-permute-start | bytes 5308424 | tf_op jit(solution)/shard_map/ppermute | solution.py:130
  97.9 10.1 %all-to-all-start.1 = ((f32[16,1,288]{2,1,0:T(1,128)}), f32[16,1,288]{2,1,0:T(1,128)S(1)}, u32[]{:S(2)}, u32[]{:S(2)}) async-start(f32[16,1,288]{2,1,0:T(1,128)} %reshape.119), calls=%async_computation.1 | async-start | bytes 49152 | tf_op jit(solution)/shard_map/all_to_all | solution.py:161
Sparse Core Ops, SparseCore 0:
  24.9 49.3 all-gather.2
